TPU v7x, 256 devices: a whole 4x4x8 slice. The times are simulated.
256 devices in a mesh: expert: 64 (over x, z, core), tensor: 4 (over y).
Axes of the slice: x: 4, y: 4, z: 8, core: 2. Of those that a mesh axis runs over, the one named last changes fastest.
Arguments:
- tokens: bfloat16 [8192, 3584], P('expert'), may hold values from -6 to 6
- cotangent: bfloat16 [8192, 3584], P('expert'), may hold values from -6 to 6
- chosen_experts: int32 [8192, 8], P('expert'), may hold values from 0 to 255, as said below
- chosen_slots: int32 [8192, 8], P('expert'), may hold values from 0 to 127, as said below
- routing_gate_weight: float32 [8192, 8], P('expert'), may hold values from 0.1 to 1
- padded_slot_count: int32 [64, 64], P('expert'), may hold values from 0 to 8, as said below
- w_gate: bfloat16 [64, 3584, 1024], P('expert', None, 'tensor'), may hold values from -0.09375 to 0.09375
- w_up: bfloat16 [64, 3584, 1024], P('expert', None, 'tensor'), may hold values from -0.09375 to 0.09375
- w_down: bfloat16 [64, 1024, 3584], P('expert', 'tensor'), may hold values from -0.1875 to 0.1875
Outputs:
- mixed: bfloat16 [8192, 3584], P('expert', 'tensor')
- token_gradient: bfloat16 [8192, 3584], P('expert', 'tensor')
- gate_gradient: float32 [8192, 8], P('expert')
- grad_w_gate: bfloat16 [64, 3584, 1024], P('expert', None, 'tensor')
- grad_w_up: bfloat16 [64, 3584, 1024], P('expert', None, 'tensor')
- grad_w_down: bfloat16 [64, 1024, 3584], P('expert', 'tensor')
Inputs may be any that keep to these rules, and one draw needn't show every extreme that they name: `chosen_experts`: each token names 8 different experts; only experts under 64 are in flight. `chosen_slots`: within one block of 128 tokens, the routes that name one expert are numbered 0, 1, 2 and so on in order of token and then of route. In every block some expert in flight is named by every token. padded_slot_count[s, e] is the smaller of 8 and the number of routes of block s that name expert e; in every block some expert reaches 8, and some expert in flight is named by no route.
All inputs are finite; a program needn't handle non-finite values.
Results may differ from a plain program's by a relative error of at most 0.015.
Values may be sent and summed in bfloat16 or wider, within the bound.
No kernel may reach another device: no remote copies, remote signals or barrier semaphores. Data moves between devices by JAX's collectives and lax.ppermute only.
A program may use at most 128 MiB of HBM per device.

v0:
```python
import jax
import jax.numpy as jnp
from jax import lax
from jax.sharding import PartitionSpec as P

OWNED = 4


def routing_layout(chosen_expert, chosen_slot, slot_count_row, expert_capacity):
    expert_number = slot_count_row.shape[0]
    one_hot = (
        chosen_expert[:, :, None] == jnp.arange(expert_number, dtype=jnp.int32)[None, None, :]
    ).astype(jnp.int32)
    slot_ceiling = jnp.sum(one_hot * slot_count_row[None, None, :], axis=2)
    slot_alive_mask = (chosen_expert < expert_number) & (chosen_slot < slot_ceiling)
    destination_slot = jnp.where(slot_alive_mask, chosen_expert * expert_capacity + chosen_slot, -1)
    return (slot_alive_mask, destination_slot)


def pack_slots(tok_block, cot_block, block_gates, destination_slot, send_rows):
    select = destination_slot[None, :, :] == jnp.arange(send_rows, dtype=jnp.int32)[:, None, None]
    picked = jnp.sum(select.astype(jnp.int32), axis=2).astype(jnp.bfloat16)
    slot_gate = jnp.sum(jnp.where(select, block_gates[None, :, :], 0.0), axis=(1, 2))
    token_sum = jnp.dot(picked, tok_block, preferred_element_type=jnp.float32).astype(jnp.bfloat16)
    cot_sum = jnp.dot(picked, cot_block, preferred_element_type=jnp.float32)
    return (token_sum, (slot_gate[:, None] * cot_sum).astype(jnp.bfloat16))


def expert_group(expert_rows, expert_cots, gate_weight, up_weight, down_weight):
    pre_gate = jnp.dot(expert_rows, gate_weight, preferred_element_type=jnp.float32)
    pre_up = jnp.dot(expert_rows, up_weight, preferred_element_type=jnp.float32)
    logistic = jax.nn.sigmoid(pre_gate)
    active = pre_gate * logistic
    hidden = (active * pre_up).astype(jnp.bfloat16)
    part_out = jnp.dot(hidden, down_weight, preferred_element_type=jnp.float32)
    grad_hidden = jnp.dot(expert_cots, down_weight.T, preferred_element_type=jnp.float32)
    grad_pre_gate = (grad_hidden * pre_up * logistic * (1.0 + pre_gate * (1.0 - logistic))).astype(
        jnp.bfloat16
    )
    grad_pre_up = (grad_hidden * active).astype(jnp.bfloat16)
    part_back = jnp.dot(grad_pre_gate, gate_weight.T, preferred_element_type=jnp.float32) + jnp.dot(
        grad_pre_up, up_weight.T, preferred_element_type=jnp.float32
    )
    grad_gate_w = jnp.dot(expert_rows.T, grad_pre_gate, preferred_element_type=jnp.float32).astype(
        jnp.bfloat16
    )
    grad_up_w = jnp.dot(expert_rows.T, grad_pre_up, preferred_element_type=jnp.float32).astype(
        jnp.bfloat16
    )
    grad_down_w = jnp.dot(hidden.T, expert_cots, preferred_element_type=jnp.float32).astype(
        jnp.bfloat16
    )
    return (part_out, part_back, (grad_gate_w, grad_up_w, grad_down_w))


def local(
    tokens,
    cotangent,
    chosen_experts,
    chosen_slots,
    routing_gate_weight,
    padded_slot_count,
    w_gate,
    w_up,
    w_down,
):
    tok_rows, feature_width = tokens.shape
    per_token = chosen_experts.shape[1]
    expert_number = padded_slot_count.shape[1]
    expert_capacity = 2 * tok_rows * per_token // (OWNED * lax.axis_size("expert"))
    send_rows = expert_number * expert_capacity
    feature_share = feature_width // lax.axis_size("tensor")
    first_col = lax.axis_index("tensor") * feature_share
    slot_alive_mask, destination_slot = routing_layout(
        chosen_experts, chosen_slots, padded_slot_count[0], expert_capacity
    )
    token_sum, cot_rows = pack_slots(
        tokens, cotangent, routing_gate_weight, destination_slot, send_rows
    )
    expert_rows, expert_cots = (
        lax.all_to_all(
            token_sum.reshape(expert_number, expert_capacity, feature_width),
            "expert",
            split_axis=0,
            concat_axis=0,
            tiled=True,
        ),
        lax.all_to_all(
            cot_rows.reshape(expert_number, expert_capacity, feature_width),
            "expert",
            split_axis=0,
            concat_axis=0,
            tiled=True,
        ),
    )
    expert_rows = expert_rows.reshape(-1, feature_width)
    expert_cots = expert_cots.reshape(-1, feature_width)
    part_out, part_back, grads = expert_group(
        expert_rows, expert_cots, w_gate[0], w_up[0], w_down[0]
    )
    rounded_out = lax.optimization_barrier(part_out.astype(jnp.bfloat16)).astype(jnp.float32)
    rounded_back = lax.optimization_barrier(part_back.astype(jnp.bfloat16)).astype(jnp.float32)
    total_out, total_back = (
        lax.psum_scatter(
            rounded_out.astype(jnp.bfloat16), "tensor", scatter_dimension=1, tiled=True
        ).astype(jnp.float32),
        lax.psum_scatter(
            rounded_back.astype(jnp.bfloat16), "tensor", scatter_dimension=1, tiled=True
        ).astype(jnp.float32),
    )
    sources = total_out.shape[0] // expert_capacity
    slot_out = total_out.astype(jnp.bfloat16).reshape(sources, expert_capacity, feature_share)
    slot_back = total_back.astype(jnp.bfloat16).reshape(sources, expert_capacity, feature_share)
    came_out, came_back = (
        lax.all_to_all(slot_out, "expert", split_axis=0, concat_axis=0, tiled=True),
        lax.all_to_all(slot_back, "expert", split_axis=0, concat_axis=0, tiled=True),
    )
    came_out = came_out.reshape(send_rows, feature_share)
    came_back = came_back.reshape(send_rows, feature_share)
    positions = jnp.maximum(destination_slot, 0).reshape(-1)
    out_rows = (
        jnp.take(came_out, positions, axis=0)
        .reshape(tok_rows, per_token, feature_share)
        .astype(jnp.float32)
    )
    returned_rows = (
        jnp.take(came_back, positions, axis=0)
        .reshape(tok_rows, per_token, feature_share)
        .astype(jnp.float32)
    )
    gate_scaling = jnp.where(slot_alive_mask, routing_gate_weight, 0.0)
    mixed = jnp.sum(gate_scaling[:, :, None] * out_rows, axis=1).astype(jnp.bfloat16)
    token_gradient = jnp.sum(
        jnp.where(slot_alive_mask[:, :, None], returned_rows, 0.0), axis=1
    ).astype(jnp.bfloat16)
    local_cotangent = lax.dynamic_slice_in_dim(cotangent, first_col, feature_share, 1).astype(
        jnp.float32
    )
    hidden_totals = jnp.sum(local_cotangent[:, None, :] * out_rows, axis=2)
    gate_gradient = lax.psum(jnp.where(slot_alive_mask, hidden_totals, 0.0), "tensor")
    grad_gate_w, grad_up_w, grad_down_w = grads
    return (
        mixed,
        token_gradient,
        gate_gradient,
        grad_gate_w[None],
        grad_up_w[None],
        grad_down_w[None],
    )


def solution(mesh):
    in_specs = (
        P("expert", None),
        P("expert", None),
        P("expert", None),
        P("expert", None),
        P("expert", None),
        P("expert", None),
        P("expert", None, "tensor"),
        P("expert", None, "tensor"),
        P("expert", "tensor", None),
    )
    out_specs = (
        P("expert", "tensor"),
        P("expert", "tensor"),
        P("expert", None),
        P("expert", None, "tensor"),
        P("expert", None, "tensor"),
        P("expert", "tensor", None),
    )
    return jax.shard_map(local, mesh=mesh, in_specs=in_specs, out_specs=out_specs, check_vma=False)
```

profile of v0, /device:TPU:6, one launch (start us, length us, event | category | flops | bytes accessed | tf_op | source)
XLA Modules:
  0.0 373.7 jit_solution(1520988641652286640)
XLA Ops:
  7.2 0.0 copy-start
  7.2 0.9 select_reduce_fusion.1
  8.1 0.7 broadcast_select_fusion.2
  8.9 0.0 copy-start.7
  8.9 0.7 broadcast_maximum_fusion
  9.6 1.7 select_reduce_fusion
  11.3 0.7 convert_reduce_fusion
  12.0 4.1 %fusion.1 = bf16[64,8,3584]{2,1,0:T(8,128)(2,1)} fusion(bf16[128,3584]{1,0:T(8,128)(2,1)} %param.12, f32[512]{0:T(512)S(1)} %select_reduce_fusion, s32[512,128]{1,0:T(8,128)S(1)} %convert_reduce_fusion), kind=kOutput, calls=%fused_computation.7 | convolution fusion | flops 473497600 | bytes 4851712 | tf_op jit(solution)/shard_map/dot_general | solution.py:25
  16.1 12.5 %all-to-all-start.2 = ((bf16[64,8,3584]{2,1,0:T(8,128)(2,1)}), bf16[64,8,3584]{2,1,0:T(8,128)(2,1)}, u32[]{:S(2)}, u32[]{:S(2)}) async-start(bf16[64,8,3584]{2,1,0:T(8,128)(2,1)} %fusion.1), calls=%async_computation.2 | async-start | bytes 7340032 | tf_op jit(solution)/shard_map/all_to_all | solution.py:88
  28.6 0.0 copy-done.2
  28.6 3.0 fusion
  31.6 79.6 %all-to-all-done.2 = bf16[64,8,3584]{2,1,0:T(8,128)(2,1)} async-done(((bf16[64,8,3584]{2,1,0:T(8,128)(2,1)}), bf16[64,8,3584]{2,1,0:T(8,128)(2,1)}, u32[]{:S(2)}, u32[]{:S(2)}) %all-to-all-start.2) | async-done | bytes 3670048 | tf_op jit(solution)/shard_map/all_to_all | solution.py:88
  111.2 8.0 %all-to-all-start = ((bf16[64,8,3584]{2,1,0:T(8,128)(2,1)}), bf16[64,8,3584]{2,1,0:T(8,128)(2,1)}, u32[]{:S(2)}, u32[]{:S(2)}) async-start(bf16[64,8,3584]{2,1,0:T(8,128)(2,1)} %fusion), calls=%async_computation | async-start | bytes 7340032 | tf_op jit(solution)/shard_map/all_to_all | solution.py:81
  119.2 0.0 reduce-scatter.7.cloned.1.call-start
  119.2 3.8 %fusion.10 = f32[512,256]{1,0:T(8,128)S(1)} fusion(bf16[64,8,3584]{2,1,0:T(8,128)(2,1)} %all-to-all-done.2, bf16[1,256,3584]{2,1,0:T(8,128)(2,1)} %param.19), kind=kOutput, calls=%fused_computation.22 | convolution fusion | flops 939524096 | bytes 6029312 | tf_op jit(solution)/shard_map/dot_general | solution.py:36
  123.0 78.8 %all-to-all-done = bf16[64,8,3584]{2,1,0:T(8,128)(2,1)} async-done(((bf16[64,8,3584]{2,1,0:T(8,128)(2,1)}), bf16[64,8,3584]{2,1,0:T(8,128)(2,1)}, u32[]{:S(2)}, u32[]{:S(2)}) %all-to-all-start) | async-done | bytes 3670048 | tf_op jit(solution)/shard_map/all_to_all | solution.py:81
  201.8 3.7 fusion.16
  205.5 0.0 copy-done
  205.5 0.0 copy-start.1
  205.5 3.4 multiply_convert_fusion.3
  208.9 0.0 copy-start.5
  208.9 0.0 copy-start.3
  208.9 0.0 copy-done.1
  208.9 3.0 convolution_convert_fusion
  212.0 5.9 %copy.46 = bf16[512,3584]{0,1:T(8,128)(2,1)} copy(bf16[512,3584]{1,0:T(8,128)(2,1)} %convolution_convert_fusion) | data formatting | bytes 7340032
  217.9 0.0 reduce-scatter.7.cloned.1.call-update
  217.9 0.2 reduce-scatter.9.cloned.1.call-start
  218.2 0.0 copy-done.5
  218.2 2.6 fusion.22
  220.8 0.0 copy-done.3
  220.8 3.1 add_convert_fusion
  223.9 6.0 %copy.48 = bf16[512,3584]{0,1:T(8,128)(2,1)} copy(bf16[512,3584]{1,0:T(8,128)(2,1)} %add_convert_fusion) | data formatting | bytes 7340032
  229.9 0.0 reduce-scatter.9.cloned.1.call-update
  229.9 31.9 %reduce-scatter.7.cloned.1.call-done = bf16[896,512]{1,0:T(8,128)(2,1)} async-done(((bf16[3584,512]{1,0:T(8,128)(2,1)}), bf16[896,512]{1,0:T(8,128)(2,1)}) %reduce-scatter.7.cloned.1.call-update) | async-done | bytes 917520
  261.8 2.2 copy.47
  264.0 10.7 %all-to-all-start.1 = ((bf16[64,8,896]{2,1,0:T(8,128)(2,1)}), bf16[64,8,896]{2,1,0:T(8,128)(2,1)S(1)}, u32[]{:S(2)}, u32[]{:S(2)}) async-start(bf16[64,8,896]{2,1,0:T(8,128)(2,1)} %bitcast.75), calls=%async_computation.1 | async-start | bytes 1835008 | tf_op jit(solution)/shard_map/all_to_all | solution.py:115
  274.7 0.1 copy.43
  274.8 0.1 reshape.64
  274.9 0.6 fusion.28
  275.5 33.7 %reduce-scatter.9.cloned.1.call-done = bf16[896,512]{1,0:T(8,128)(2,1)} async-done(((bf16[3584,512]{1,0:T(8,128)(2,1)}), bf16[896,512]{1,0:T(8,128)(2,1)}) %reduce-scatter.9.cloned.1.call-update) | async-done | bytes 917520
  309.3 2.3 copy.49
  311.5 0.0 all-to-all-done.1
  311.5 10.9 %all-to-all-start.3 = ((bf16[64,8,896]{2,1,0:T(8,128)(2,1)}), bf16[64,8,896]{2,1,0:T(8,128)(2,1)}, u32[]{:S(2)}, u32[]{:S(2)}) async-start(bf16[64,8,896]{2,1,0:T(8,128)(2,1)} %bitcast.74), calls=%async_computation.3 | async-start | bytes 1835008 | tf_op jit(solution)/shard_map/all_to_all | solution.py:116
  322.5 0.6 compare_and_fusion
  323.0 0.0 copy-done.7
  323.0 0.1 copy.44
  323.2 0.1 copy.42
  323.3 1.0 dynamic-slice_convert_fusion
  324.2 4.4 %fusion.4 = bf16[1,256,3584]{2,1,0:T(8,128)(2,1)} fusion(bf16[512,256]{1,0:T(8,128)(2,1)S(1)} %get-tuple-element.25, bf16[64,8,3584]{2,1,0:T(8,128)(2,1)} %all-to-all-done.2), kind=kOutput, calls=%fused_computation.13 | convolution fusion | flops 940441600 | bytes 5767168 | tf_op jit(solution)/shard_map/dot_general | solution.py:50
  328.6 0.0 copy-start.4
  328.6 4.5 %fusion.2 = bf16[1,3584,256]{2,1,0:T(8,128)(2,1)} fusion(bf16[512,256]{1,0:T(8,128)(2,1)} %copy-done.5, bf16[64,8,3584]{2,1,0:T(8,128)(2,1)} %all-to-all-done), kind=kOutput, calls=%fused_computation.11 | convolution fusion | flops 940441600 | bytes 5767168 | tf_op jit(solution)/shard_map/dot_general | solution.py:44
  333.1 0.0 copy-done.4
  333.1 4.4 %fusion.3 = bf16[1,3584,256]{2,1,0:T(8,128)(2,1)} fusion(bf16[512,256]{1,0:T(8,128)(2,1)S(1)} %copy-done.4, bf16[64,8,3584]{2,1,0:T(8,128)(2,1)} %all-to-all-done), kind=kOutput, calls=%fused_computation.12 | convolution fusion | flops 940441600 | bytes 5767168 | tf_op jit(solution)/shard_map/dot_general | solution.py:47
  337.6 0.0 copy-start.9
  337.6 5.6 %gather_fusion = bf16[1024,896]{1,0:T(8,128)(2,1)} fusion(bf16[512,896]{1,0:T(8,128)(2,1)S(1)} %bitcast.71, s32[1024]{0:T(1024)} %fusion.28), kind=kCustom, calls=%fused_computation.clone | custom fusion | bytes 3674112 | tf_op jit(solution)/shard_map/jit(_take)/gather | solution.py:122
  343.2 0.0 copy-done.9
  343.2 2.2 fusion.7
  345.5 0.1 reduce_sum.62
  345.6 0.0 copy-done.8
  345.6 9.2 %psum.7 = f32[128,8]{0,1:T(8,128)} all-reduce(f32[128,8]{0,1:T(8,128)S(1)} %broadcast_select_fusion.1), channel_id=1, replica_groups=mesh['expert'=64,'tensor'=4] {'tensor'}, use_global_device_ids=true, to_apply=%region_8.10 | all-reduce | flops 1024 | bytes 8192 | tf_op jit(solution)/shard_map/psum | solution.py:140
  354.8 0.0 all-to-all-done.3
  354.8 0.0 copy-done.6
  354.8 7.0 %gather_fusion.1 = bf16[1024,896]{1,0:T(8,128)(2,1)} fusion(bf16[512,896]{1,0:T(8,128)(2,1)} %bitcast.12, s32[1024]{0:T(1024)S(1)} %copy-done.6), kind=kCustom, calls=%fused_computation.1.clone | custom fusion | bytes 3674112 | tf_op jit(solution)/shard_map/jit(_take)/gather | solution.py:127
  361.8 5.0 %fusion.8 = (bf16[128,896]{1,0:T(8,128)(2,1)}, bf16[128,896]{1,0:T(8,128)(2,1)}) fusion(bf16[1024,896]{1,0:T(8,128)(2,1)} %gather_fusion.1, pred[1024]{0:T(1024)(128)(4,1)S(1)} %copy-done.9, pred[128,8]{1,0:T(8,128)(4,1)S(1)} %copy.44, bf16[1024,896]{1,0:T(8,128)(2,1)} %gather_fusion, f32[128,8]{1,0:T(8,128)S(1)} %copy.42), kind=kLoop, calls=%fused_computation.20 | loop fusion | flops 7110656 | bytes 4134912 | tf_op jit(solution)/shard_map/reduce_sum | solution.py:133
  (5 shorter events, 0.1 us)
Async XLA Ops:
  7.2 198.3 %copy-start = (bf16[1,3584,256]{2,1,0:T(8,128)(2,1)S(1)}, bf16[1,3584,256]{2,1,0:T(8,128)(2,1)}, u32[]{:S(2)}) copy-start(bf16[1,3584,256]{2,1,0:T(8,128)(2,1)} %param.18) | copy-start | bytes 5505028
  8.9 314.2 %copy-start.7 = (pred[128,8]{0,1:T(8,128)(4,1)}, pred[128,8]{0,1:T(8,128)(4,1)S(1)}, u32[]{:S(2)}) copy-start(pred[128,8]{0,1:T(8,128)(4,1)S(1)} %get-tuple-element.22) | copy-start | bytes 3076
  16.1 12.5 %copy-start.2 = (bf16[128,3584]{1,0:T(8,128)(2,1)S(1)}, bf16[128,3584]{1,0:T(8,128)(2,1)}, u32[]{:S(2)}) copy-start(bf16[128,3584]{1,0:T(8,128)(2,1)} %param.11) | copy-start | bytes 2752516
  16.1 95.1 %all-to-all-start.2 = ((bf16[64,8,3584]{2,1,0:T(8,128)(2,1)}), bf16[64,8,3584]{2,1,0:T(8,128)(2,1)}, u32[]{:S(2)}, u32[]{:S(2)}) async-start(bf16[64,8,3584]{2,1,0:T(8,128)(2,1)} %fusion.1), calls=%async_computation.2 | async-start | bytes 7340032 | tf_op jit(solution)/shard_map/all_to_all | solution.py:88
  111.2 90.6 %all-to-all-start = ((bf16[64,8,3584]{2,1,0:T(8,128)(2,1)}), bf16[64,8,3584]{2,1,0:T(8,128)(2,1)}, u32[]{:S(2)}, u32[]{:S(2)}) async-start(bf16[64,8,3584]{2,1,0:T(8,128)(2,1)} %fusion), calls=%async_computation | async-start | bytes 7340032 | tf_op jit(solution)/shard_map/all_to_all | solution.py:81
  119.2 142.6 %reduce-scatter.7.cloned.1.call-start = ((), (), s32[]{:S(2)}) async-start(), calls=%async_computation.6 | async-start | bytes 4587520
  205.5 3.4 copy-start.1
  208.9 9.3 %copy-start.5 = (bf16[512,256]{1,0:T(8,128)(2,1)}, bf16[512,256]{1,0:T(8,128)(2,1)S(1)}, u32[]{:S(2)}) copy-start(bf16[512,256]{1,0:T(8,128)(2,1)S(1)} %get-tuple-element.26) | copy-start | bytes 786436
  208.9 11.9 %copy-start.3 = (bf16[512,256]{1,0:T(8,128)(2,1)}, bf16[512,256]{1,0:T(8,128)(2,1)S(1)}, u32[]{:S(2)}) copy-start(bf16[512,256]{1,0:T(8,128)(2,1)S(1)} %get-tuple-element.27) | copy-start | bytes 786436
  217.9 91.3 %reduce-scatter.9.cloned.1.call-start = ((), (), s32[]{:S(2)}) async-start(), calls=%async_computation.7 | async-start | bytes 4587520
  264.0 47.5 %all-to-all-start.1 = ((bf16[64,8,896]{2,1,0:T(8,128)(2,1)}), bf16[64,8,896]{2,1,0:T(8,128)(2,1)S(1)}, u32[]{:S(2)}, u32[]{:S(2)}) async-start(bf16[64,8,896]{2,1,0:T(8,128)(2,1)} %bitcast.75), calls=%async_computation.1 | async-start | bytes 1835008 | tf_op jit(solution)/shard_map/all_to_all | solution.py:115
  311.5 43.3 %all-to-all-start.3 = ((bf16[64,8,896]{2,1,0:T(8,128)(2,1)}), bf16[64,8,896]{2,1,0:T(8,128)(2,1)}, u32[]{:S(2)}, u32[]{:S(2)}) async-start(bf16[64,8,896]{2,1,0:T(8,128)(2,1)} %bitcast.74), calls=%async_computation.3 | async-start | bytes 1835008 | tf_op jit(solution)/shard_map/all_to_all | solution.py:116
  328.6 4.5 %copy-start.4 = (bf16[512,256]{1,0:T(8,128)(2,1)S(1)}, bf16[512,256]{1,0:T(8,128)(2,1)}, u32[]{:S(2)}) copy-start(bf16[512,256]{1,0:T(8,128)(2,1)} %copy-done.3) | copy-start | bytes 786436
  337.6 5.6 %copy-start.9 = (pred[1024]{0:T(1024)(128)(4,1)S(1)}, pred[1024]{0:T(1024)(128)(4,1)}, u32[]{:S(2)}) copy-start(pred[1024]{0:T(1024)(128)(4,1)} %compare_and_fusion) | copy-start | bytes 3076
  337.6 8.0 %copy-start.8 = (pred[128,8]{0,1:T(8,128)(4,1)S(1)}, pred[128,8]{0,1:T(8,128)(4,1)}, u32[]{:S(2)}) copy-start(pred[128,8]{0,1:T(8,128)(4,1)} %copy-done.7) | copy-start | bytes 3076
  337.6 17.2 %copy-start.6 = (s32[1024]{0:T(1024)S(1)}, s32[1024]{0:T(1024)}, u32[]{:S(2)}) copy-start(s32[1024]{0:T(1024)} %fusion.28) | copy-start | bytes 12292
Sparse Core Ops, SparseCore 0:
  218.0 43.6 reduce-scatter.6
  264.3 44.8 reduce-scatter.8
where the time goes:
time: 375 us; the launch traced here: 374 us
  waiting for transfers between devices  224 us (60%)
  starting transfers between devices  42.4 us (11%)
  matrix products  40.1 us (11%)
  local copies, waits for them, and re-layouts  29.7 us (8%)
  other arithmetic  14.2 us (4%)
  between operations  14.2 us (4%)
  blocking collectives  9.19 us (2%)
    all_to_all x1, waiting for transfers between devices, local(): lax.all_to_all(cot_rows.reshape(expert_number, expert_capacity, feature_w...  79.6 us
    all_to_all x1, waiting for transfers between devices, local(): lax.all_to_all(token_sum.reshape(expert_number, expert_capacity, feature_...  78.8 us
    unnamed x4, waiting for transfers between devices  65.6 us
    unnamed x24, local copies, waits for them, and re-layouts  16.4 us
    all_to_all x1, starting transfers between devices, local(): lax.all_to_all(cot_rows.reshape(expert_number, expert_capacity, feature_w...  12.5 us
    all_to_all x1, starting transfers between devices, local(): lax.all_to_all(slot_back, 'expert', split_axis=0, concat_axis=0, tiled=True)  10.9 us
    all_to_all x1, starting transfers between devices, local(): lax.all_to_all(slot_out, 'expert', split_axis=0, concat_axis=0, tiled=True)  10.7 us
    psum x1, blocking collectives, local(): lax.psum(jnp.where(slot_alive_mask, hidden_totals, 0.0), 'tensor')  9.19 us
  transfers between devices with their start and end apart: 6, of which 4 were waited for; matrix products, arithmetic and copies ran while one was open for 13% of the time, Pallas kernels for 0%

commit v1 on v0

--- a/solution.py
+++ b/solution.py
@@ -53,6 +53,37 @@
     return (part_out, part_back, (grad_gate_w, grad_up_w, grad_down_w))
 
 
+def expert_group_t(expert_rows, expert_cots, gate_weight, up_weight, down_weight):
+    pre_gate = jnp.dot(expert_rows, gate_weight, preferred_element_type=jnp.float32)
+    pre_up = jnp.dot(expert_rows, up_weight, preferred_element_type=jnp.float32)
+    logistic = jax.nn.sigmoid(pre_gate)
+    active = pre_gate * logistic
+    hidden = (active * pre_up).astype(jnp.bfloat16)
+    contract_h = (((1,), (1,)), ((), ()))
+    out_t = lax.dot_general(
+        down_weight.T, hidden, contract_h, preferred_element_type=jnp.float32
+    ).astype(jnp.bfloat16)
+    grad_hidden = jnp.dot(expert_cots, down_weight.T, preferred_element_type=jnp.float32)
+    grad_pre_gate = (grad_hidden * pre_up * logistic * (1.0 + pre_gate * (1.0 - logistic))).astype(
+        jnp.bfloat16
+    )
+    grad_pre_up = (grad_hidden * active).astype(jnp.bfloat16)
+    back_t = (
+        lax.dot_general(gate_weight, grad_pre_gate, contract_h, preferred_element_type=jnp.float32)
+        + lax.dot_general(up_weight, grad_pre_up, contract_h, preferred_element_type=jnp.float32)
+    ).astype(jnp.bfloat16)
+    grad_gate_w = jnp.dot(expert_rows.T, grad_pre_gate, preferred_element_type=jnp.float32).astype(
+        jnp.bfloat16
+    )
+    grad_up_w = jnp.dot(expert_rows.T, grad_pre_up, preferred_element_type=jnp.float32).astype(
+        jnp.bfloat16
+    )
+    grad_down_w = jnp.dot(hidden.T, expert_cots, preferred_element_type=jnp.float32).astype(
+        jnp.bfloat16
+    )
+    return (out_t, back_t, (grad_gate_w, grad_up_w, grad_down_w))
+
+
 def local(
     tokens,
     cotangent,
@@ -74,49 +105,32 @@
     slot_alive_mask, destination_slot = routing_layout(
         chosen_experts, chosen_slots, padded_slot_count[0], expert_capacity
     )
+    local_tokens = lax.dynamic_slice_in_dim(tokens, first_col, feature_share, 1)
+    local_cotangent_bf = lax.dynamic_slice_in_dim(cotangent, first_col, feature_share, 1)
     token_sum, cot_rows = pack_slots(
-        tokens, cotangent, routing_gate_weight, destination_slot, send_rows
+        local_tokens, local_cotangent_bf, routing_gate_weight, destination_slot, send_rows
     )
-    expert_rows, expert_cots = (
-        lax.all_to_all(
-            token_sum.reshape(expert_number, expert_capacity, feature_width),
-            "expert",
-            split_axis=0,
-            concat_axis=0,
-            tiled=True,
-        ),
-        lax.all_to_all(
-            cot_rows.reshape(expert_number, expert_capacity, feature_width),
-            "expert",
-            split_axis=0,
-            concat_axis=0,
-            tiled=True,
-        ),
+    packed = jnp.stack([token_sum, cot_rows]).reshape(
+        2, expert_number, expert_capacity, feature_share
     )
-    expert_rows = expert_rows.reshape(-1, feature_width)
-    expert_cots = expert_cots.reshape(-1, feature_width)
-    part_out, part_back, grads = expert_group(
+    arrived = lax.all_to_all(packed, "expert", split_axis=1, concat_axis=1, tiled=True)
+    arrived = arrived.reshape(2, send_rows, feature_share)
+    gathered = lax.all_gather(arrived, "tensor", axis=2, tiled=True)
+    expert_rows = gathered[0]
+    expert_cots = gathered[1]
+    out_t, back_t, grads = expert_group_t(
         expert_rows, expert_cots, w_gate[0], w_up[0], w_down[0]
     )
-    rounded_out = lax.optimization_barrier(part_out.astype(jnp.bfloat16)).astype(jnp.float32)
-    rounded_back = lax.optimization_barrier(part_back.astype(jnp.bfloat16)).astype(jnp.float32)
-    total_out, total_back = (
-        lax.psum_scatter(
-            rounded_out.astype(jnp.bfloat16), "tensor", scatter_dimension=1, tiled=True
-        ).astype(jnp.float32),
-        lax.psum_scatter(
-            rounded_back.astype(jnp.bfloat16), "tensor", scatter_dimension=1, tiled=True
-        ).astype(jnp.float32),
+    total_out = lax.psum_scatter(out_t, "tensor", scatter_dimension=0, tiled=True)
+    total_back = lax.psum_scatter(back_t, "tensor", scatter_dimension=0, tiled=True)
+    sources = total_out.shape[1] // expert_capacity
+    slot_both = jnp.stack([total_out.T, total_back.T]).reshape(
+        2, sources, expert_capacity, feature_share
     )
-    sources = total_out.shape[0] // expert_capacity
-    slot_out = total_out.astype(jnp.bfloat16).reshape(sources, expert_capacity, feature_share)
-    slot_back = total_back.astype(jnp.bfloat16).reshape(sources, expert_capacity, feature_share)
-    came_out, came_back = (
-        lax.all_to_all(slot_out, "expert", split_axis=0, concat_axis=0, tiled=True),
-        lax.all_to_all(slot_back, "expert", split_axis=0, concat_axis=0, tiled=True),
-    )
-    came_out = came_out.reshape(send_rows, feature_share)
-    came_back = came_back.reshape(send_rows, feature_share)
+    came = lax.all_to_all(slot_both, "expert", split_axis=1, concat_axis=1, tiled=True)
+    came = came.reshape(2, send_rows, feature_share)
+    came_out = came[0]
+    came_back = came[1]
     positions = jnp.maximum(destination_slot, 0).reshape(-1)
     out_rows = (
         jnp.take(came_out, positions, axis=0)
@@ -133,9 +147,7 @@
     token_gradient = jnp.sum(
         jnp.where(slot_alive_mask[:, :, None], returned_rows, 0.0), axis=1
     ).astype(jnp.bfloat16)
-    local_cotangent = lax.dynamic_slice_in_dim(cotangent, first_col, feature_share, 1).astype(
-        jnp.float32
-    )
+    local_cotangent = local_cotangent_bf.astype(jnp.float32)
     hidden_totals = jnp.sum(local_cotangent[:, None, :] * out_rows, axis=2)
     gate_gradient = lax.psum(jnp.where(slot_alive_mask, hidden_totals, 0.0), "tensor")
     grad_gate_w, grad_up_w, grad_down_w = grads

time: 375 us -> 359 us (0.957)
  blocking collectives: 9.19 us -> 64.2 us
  waiting for transfers between devices: 224 us -> 185 us
  starting transfers between devices: 42.4 us -> 11 us
  matrix products: 40.1 us -> 31.4 us
  local copies, waits for them, and re-layouts: 29.7 us -> 33.5 us
    all_to_all x4 -> x1, waiting for transfers between devices: 158 us -> 28.8 us  [local(): lax.all_to_all(slot_both, 'expert', split_axis=1, concat_axis=1, tiled=True)]
    all_gather x0 -> x1, waiting for transfers between devices: none -> 76.1 us  [local(): gathered = lax.all_gather(arrived, 'tensor', axis=2, tiled=True)]
    all_to_all x0 -> x1, blocking collectives: none -> 55 us  [local(): lax.all_to_all(packed, 'expert', split_axis=1, concat_axis=1, tiled=True)]
    all_to_all x4 -> x1, starting transfers between devices: 42.1 us -> 10.9 us  [local(): lax.all_to_all(slot_both, 'expert', split_axis=1, concat_axis=1, tiled=True)]
    unnamed x4 -> x5, waiting for transfers between devices: 65.6 us -> 80.3 us
    dot_general x9, matrix products: 33 us -> 28.7 us  [the longest x1 4.59 us: expert_group_t(): jnp.dot(expert_rows.T, grad_pre_gate, preferred_element_type=jnp.float32)]
    unnamed x24 -> x32, local copies, waits for them, and re-layouts: 16.4 us -> 16.8 us
  transfers between devices with their start and end apart: 6 -> 4, of which waited for: 4 -> 4; matrix products, arithmetic and copies ran while one was open for 13% -> 8% of each run, Pallas kernels for 0% -> 0%
where the time goes in v1:
time: 359 us; the launch traced here: 356 us
  waiting for transfers between devices  185 us (52%)
  blocking collectives  64.2 us (18%)
  local copies, waits for them, and re-layouts  33.5 us (9%)
  matrix products  31.4 us (9%)
  other arithmetic  17 us (5%)
  between operations  14 us (4%)
  starting transfers between devices  11 us (3%)
    unnamed x5, waiting for transfers between devices  80.3 us
    all_gather x1, waiting for transfers between devices, local(): gathered = lax.all_gather(arrived, 'tensor', axis=2, tiled=True)  76.1 us
    all_to_all x1, blocking collectives, local(): lax.all_to_all(packed, 'expert', split_axis=1, concat_axis=1, tiled=True)  55 us
    all_to_all x1, waiting for transfers between devices, local(): lax.all_to_all(slot_both, 'expert', split_axis=1, concat_axis=1, tiled=True)  28.8 us
    unnamed x32, local copies, waits for them, and re-layouts  16.8 us
    all_to_all x1, starting transfers between devices, local(): lax.all_to_all(slot_both, 'expert', split_axis=1, concat_axis=1, tiled=True)  10.9 us
    psum x1, blocking collectives, local(): lax.psum(jnp.where(slot_alive_mask, hidden_totals, 0.0), 'tensor')  9.18 us
  transfers between devices with their start and end apart: 4, of which 4 were waited for; matrix products, arithmetic and copies ran while one was open for 8% of the time, Pallas kernels for 0%

profile of v1, /device:TPU:6, one launch (start us, length us, event | category | flops | bytes accessed | tf_op | source)
XLA Modules:
  0.0 356.4 jit_solution(852221532995339387)
XLA Ops:
  7.2 0.0 copy-start
  7.2 0.0 all-gather.2.cloned.1.call-start
  7.2 0.9 select_reduce_fusion.1
  8.2 0.7 broadcast_select_fusion.2
  8.9 0.7 broadcast_maximum_fusion
  9.6 1.7 select_reduce_fusion
  11.3 0.7 convert_reduce_fusion
  12.1 1.3 fusion.19
  13.4 1.3 fusion.20
  14.7 0.2 pad_maximum_fusion
  14.9 55.0 %all_to_all.10 = bf16[2,64,8,896]{3,2,0,1:T(8,128)(2,1)S(1)} all-to-all(bf16[2,64,8,896]{3,2,0,1:T(8,128)(2,1)S(1)} %pad_maximum_fusion), channel_id=1, replica_groups=mesh['expert'=64,'tensor'=4] {'expert'}, dimensions={1} | all-to-all | bytes 3670016 | tf_op jit(solution)/shard_map/all_to_all | solution.py:116
  70.0 1.4 copy.76
  71.3 0.0 all-gather.2.cloned.1.call-update
  71.4 0.0 reduce-scatter.7.cloned.1.call-start
  71.4 76.1 %all-gather.2.cloned.1.call-done = bf16[2,512,3584]{2,1,0:T(8,128)(2,1)} async-done(((bf16[2,512,896]{2,1,0:T(8,128)(2,1)}), bf16[2,512,3584]{2,1,0:T(8,128)(2,1)}) %all-gather.2.cloned.1.call-update) | async-done | bytes 7340048 | tf_op jit(solution)/shard_map/all_gather | solution.py:118
  147.5 3.9 %fusion.9 = f32[512,256]{1,0:T(8,128)S(1)} fusion(bf16[2,512,3584]{2,1,0:T(8,128)(2,1)} %all-gather.2.cloned.1.call-done, bf16[1,256,3584]{2,1,0:T(8,128)(2,1)} %param.19), kind=kOutput, calls=%fused_computation.21 | convolution fusion | flops 939524096 | bytes 6029312 | tf_op jit(solution)/shard_map/dot_general | solution.py:66
  151.4 0.0 copy-done.1
  151.4 0.0 copy-start.2
  151.4 3.3 fusion.11
  154.7 0.0 copy-done
  154.7 0.9 copy-done.2
  155.6 1.2 multiply_convert_fusion.3
  156.8 0.0 copy-start.6
  156.8 0.0 copy-start.4
  156.8 0.3 copy-done.3
  157.1 3.0 fusion.1
  160.1 5.9 %copy.71 = bf16[3584,512]{1,0:T(8,128)(2,1)} copy(bf16[3584,512]{0,1:T(8,128)(2,1)} %fusion.1) | data formatting | bytes 7340032
  166.1 0.0 reduce-scatter.7.cloned.1.call-update
  166.1 0.0 reduce-scatter.9.cloned.1.call-start
  166.1 0.0 copy-done.6
  166.2 2.7 fusion.16
  168.8 0.0 copy-done.4
  168.8 3.1 fusion
  171.9 5.9 %copy.73 = bf16[3584,512]{1,0:T(8,128)(2,1)} copy(bf16[3584,512]{0,1:T(8,128)(2,1)} %fusion) | data formatting | bytes 7340032
  177.8 0.0 reduce-scatter.9.cloned.1.call-update
  177.9 34.3 %reduce-scatter.7.cloned.1.call-done = bf16[896,512]{1,0:T(8,128)(2,1)} async-done(((bf16[3584,512]{1,0:T(8,128)(2,1)}), bf16[896,512]{1,0:T(8,128)(2,1)}) %reduce-scatter.7.cloned.1.call-update) | async-done | bytes 917520
  212.2 1.5 copy.72
  213.7 45.9 %reduce-scatter.9.cloned.1.call-done = bf16[896,512]{1,0:T(8,128)(2,1)} async-done(((bf16[3584,512]{1,0:T(8,128)(2,1)}), bf16[896,512]{1,0:T(8,128)(2,1)}) %reduce-scatter.9.cloned.1.call-update) | async-done | bytes 917520
  259.7 2.2 copy.74
  261.9 2.6 pad_maximum_fusion.1
  264.5 10.9 %all-to-all-start.1 = ((bf16[2,64,8,896]{3,2,0,1:T(8,128)(2,1)}), bf16[2,64,8,896]{3,2,0,1:T(8,128)(2,1)}, u32[]{:S(2)}, u32[]{:S(2)}) async-start(bf16[2,64,8,896]{3,2,0,1:T(8,128)(2,1)} %pad_maximum_fusion.1), calls=%async_computation.1 | async-start | bytes 3670016 | tf_op jit(solution)/shard_map/all_to_all | solution.py:130
  275.4 0.0 copy-done.9
  275.4 0.1 copy.69
  275.6 0.1 copy.63
  275.7 0.1 reshape.55
  275.8 0.1 copy.62
  275.9 1.0 dynamic-slice_convert_fusion
  276.8 0.6 compare_and_fusion
  277.4 0.6 fusion.26
  278.0 4.6 %fusion.4 = bf16[1,256,3584]{2,1,0:T(8,128)(2,1)} fusion(bf16[512,256]{1,0:T(8,128)(2,1)S(1)} %get-tuple-element.33, bf16[2,512,3584]{2,1,0:T(8,128)(2,1)} %all-gather.2.cloned.1.call-done), kind=kOutput, calls=%fused_computation.11 | convolution fusion | flops 940441600 | bytes 5767168 | tf_op jit(solution)/shard_map/dot_general | solution.py:81
  282.6 0.0 copy-done.7
  282.6 4.6 %fusion.2 = bf16[1,3584,256]{2,1,0:T(8,128)(2,1)} fusion(bf16[512,256]{1,0:T(8,128)(2,1)S(1)} %copy-done.7, bf16[2,512,3584]{2,1,0:T(8,128)(2,1)} %all-gather.2.cloned.1.call-done), kind=kOutput, calls=%fused_computation.9 | convolution fusion | flops 940441600 | bytes 5767168 | tf_op jit(solution)/shard_map/dot_general | solution.py:75
  287.1 0.0 slice-done
  287.2 0.0 slice-done.1
  287.2 2.4 fusion.3
  289.6 28.8 %all-to-all-done.1 = bf16[2,64,8,896]{3,2,0,1:T(8,128)(2,1)} async-done(((bf16[2,64,8,896]{3,2,0,1:T(8,128)(2,1)}), bf16[2,64,8,896]{3,2,0,1:T(8,128)(2,1)}, u32[]{:S(2)}, u32[]{:S(2)}) %all-to-all-start.1) | async-done | bytes 1835040 | tf_op jit(solution)/shard_map/all_to_all | solution.py:130
  318.4 2.5 slice_bitcast_fusion.9
  320.9 0.0 copy-done.8
  320.9 7.0 %gather_fusion = bf16[1024,896]{1,0:T(8,128)(2,1)} fusion(bf16[512,896]{1,0:T(8,128)(2,1)} %get-tuple-element.31, s32[1024]{0:T(1024)S(1)} %copy-done.8), kind=kCustom, calls=%fused_computation.clone | custom fusion | bytes 3674112 | tf_op jit(solution)/shard_map/jit(_take)/gather | solution.py:136
  328.0 2.3 fusion.7
  330.2 0.1 reduce_sum.62
  330.4 9.2 %psum.7 = f32[128,8]{0,1:T(8,128)} all-reduce(f32[128,8]{0,1:T(8,128)S(1)} %broadcast_select_fusion.1), channel_id=1, replica_groups=mesh['expert'=64,'tensor'=4] {'tensor'}, use_global_device_ids=true, to_apply=%region_8.10 | all-reduce | flops 1024 | bytes 8192 | tf_op jit(solution)/shard_map/psum | solution.py:152
  339.6 5.3 %gather_fusion.1 = bf16[1024,896]{1,0:T(8,128)(2,1)} fusion(bf16[512,896]{1,0:T(8,128)(2,1)S(1)} %get-tuple-element.32, s32[1024]{0:T(1024)S(1)} %copy-done.8), kind=kCustom, calls=%fused_computation.1.clone | custom fusion | bytes 3674112 | tf_op jit(solution)/shard_map/jit(_take)/gather | solution.py:141
  344.8 5.0 %fusion.8 = (bf16[128,896]{1,0:T(8,128)(2,1)}, bf16[128,896]{1,0:T(8,128)(2,1)}) fusion(bf16[1024,896]{1,0:T(8,128)(2,1)} %gather_fusion.1, pred[1024]{0:T(1024)(128)(4,1)S(1)} %copy-done.11, pred[128,8]{1,0:T(8,128)(4,1)S(1)} %copy.69, bf16[1024,896]{1,0:T(8,128)(2,1)} %gather_fusion, f32[128,8]{1,0:T(8,128)S(1)} %copy.62), kind=kLoop, calls=%fused_computation.20 | loop fusion | flops 7110656 | bytes 4134912 | tf_op jit(solution)/shard_map/reduce_sum | solution.py:147
  (16 shorter events, 0.1 us)
Async XLA Ops:
  7.2 147.6 %copy-start = (bf16[1,3584,256]{2,1,0:T(8,128)(2,1)S(1)}, bf16[1,3584,256]{2,1,0:T(8,128)(2,1)}, u32[]{:S(2)}) copy-start(bf16[1,3584,256]{2,1,0:T(8,128)(2,1)} %param.18) | copy-start | bytes 5505028
  7.2 140.3 %all-gather.2.cloned.1.call-start = ((), (), s32[]{:S(2)}) async-start(), calls=%async_computation.4 | async-start | bytes 9175040 | tf_op jit(solution)/shard_map/all_gather | solution.py:118
  8.9 266.5 %copy-start.9 = (pred[128,8]{0,1:T(8,128)(4,1)}, pred[128,8]{0,1:T(8,128)(4,1)S(1)}, u32[]{:S(2)}) copy-start(pred[128,8]{0,1:T(8,128)(4,1)S(1)} %get-tuple-element.28) | copy-start | bytes 3076
  71.4 140.8 %reduce-scatter.7.cloned.1.call-start = ((), (), s32[]{:S(2)}) async-start(), calls=%async_computation.5 | async-start | bytes 4587520
  147.5 3.9 %copy-start.1 = (bf16[1,3584,256]{2,1,0:T(8,128)(2,1)S(1)}, bf16[1,3584,256]{2,1,0:T(8,128)(2,1)}, u32[]{:S(2)}) copy-start(bf16[1,3584,256]{2,1,0:T(8,128)(2,1)} %param.17) | copy-start | bytes 5505028
  151.4 4.2 %copy-start.2 = (bf16[2,512,3584]{2,1,0:T(8,128)(2,1)S(1)}, bf16[2,512,3584]{2,1,0:T(8,128)(2,1)}, u32[]{:S(2)}) copy-start(bf16[2,512,3584]{2,1,0:T(8,128)(2,1)} %all-gather.2.cloned.1.call-done) | copy-start | bytes 22020100
  155.6 1.5 copy-start.3
  156.8 9.3 %copy-start.6 = (bf16[512,256]{1,0:T(8,128)(2,1)}, bf16[512,256]{1,0:T(8,128)(2,1)S(1)}, u32[]{:S(2)}) copy-start(bf16[512,256]{1,0:T(8,128)(2,1)S(1)} %get-tuple-element.34) | copy-start | bytes 786436
  156.8 12.0 %copy-start.4 = (bf16[512,256]{1,0:T(8,128)(2,1)}, bf16[512,256]{1,0:T(8,128)(2,1)S(1)}, u32[]{:S(2)}) copy-start(bf16[512,256]{1,0:T(8,128)(2,1)S(1)} %get-tuple-element.35) | copy-start | bytes 786436
  166.1 93.6 %reduce-scatter.9.cloned.1.call-start = ((), (), s32[]{:S(2)}) async-start(), calls=%async_computation.6 | async-start | bytes 4587520
  264.5 53.9 %all-to-all-start.1 = ((bf16[2,64,8,896]{3,2,0,1:T(8,128)(2,1)}), bf16[2,64,8,896]{3,2,0,1:T(8,128)(2,1)}, u32[]{:S(2)}, u32[]{:S(2)}) async-start(bf16[2,64,8,896]{3,2,0,1:T(8,128)(2,1)} %pad_maximum_fusion.1), calls=%async_computation.1 | async-start | bytes 3670016 | tf_op jit(solution)/shard_map/all_to_all | solution.py:130
  278.0 4.6 %copy-start.7 = (bf16[512,256]{1,0:T(8,128)(2,1)S(1)}, bf16[512,256]{1,0:T(8,128)(2,1)}, u32[]{:S(2)}) copy-start(bf16[512,256]{1,0:T(8,128)(2,1)} %copy-done.6) | copy-start | bytes 786436
  278.0 9.2 %slice-start = ((s8[7340032]{0:T(1024)(128)(4,1)}), s8[4194304]{0:T(1024)(128)(4,1)S(1)}, s32[]{:S(2)}) async-start(s8[7340032]{0:T(1024)(128)(4,1)} %bitcast.87), calls=%async_computation.7 | async-start | bytes 8388608
  282.6 4.6 %slice-start.1 = ((s8[7340032]{0:T(1024)(128)(4,1)}), s8[3145728]{0:T(1024)(128)(4,1)S(1)}, s32[]{:S(2)}) async-start(s8[7340032]{0:T(1024)(128)(4,1)} %bitcast.87), calls=%async_computation.8 | async-start | bytes 6291456
  282.6 4.6 %copy-start.5 = (bf16[512,256]{1,0:T(8,128)(2,1)S(1)}, bf16[512,256]{1,0:T(8,128)(2,1)}, u32[]{:S(2)}) copy-start(bf16[512,256]{1,0:T(8,128)(2,1)} %copy-done.4) | copy-start | bytes 786436
  289.6 31.4 %copy-start.8 = (s32[1024]{0:T(1024)S(1)}, s32[1024]{0:T(1024)}, u32[]{:S(2)}) copy-start(s32[1024]{0:T(1024)} %fusion.26) | copy-start | bytes 12292
  320.9 7.0 %copy-start.11 = (pred[1024]{0:T(1024)(128)(4,1)S(1)}, pred[1024]{0:T(1024)(128)(4,1)}, u32[]{:S(2)}) copy-start(pred[1024]{0:T(1024)(128)(4,1)} %compare_and_fusion) | copy-start | bytes 3076
  328.0 2.4 copy-start.10
Sparse Core Ops, SparseCore 0:
  71.5 75.9 all-gather.1
  166.2 45.9 reduce-scatter.6
  214.8 44.8 reduce-scatter.8

commit v2 on v1

--- a/solution.py
+++ b/solution.py
@@ -110,27 +110,30 @@
     token_sum, cot_rows = pack_slots(
         local_tokens, local_cotangent_bf, routing_gate_weight, destination_slot, send_rows
     )
-    packed = jnp.stack([token_sum, cot_rows]).reshape(
-        2, expert_number, expert_capacity, feature_share
-    )
-    arrived = lax.all_to_all(packed, "expert", split_axis=1, concat_axis=1, tiled=True)
-    arrived = arrived.reshape(2, send_rows, feature_share)
-    gathered = lax.all_gather(arrived, "tensor", axis=2, tiled=True)
-    expert_rows = gathered[0]
-    expert_cots = gathered[1]
+    rows_q = lax.all_to_all(
+        token_sum.reshape(expert_number, expert_capacity, feature_share),
+        "expert", split_axis=0, concat_axis=0, tiled=True,
+    ).reshape(send_rows, feature_share)
+    rows_all = lax.all_gather(rows_q, "tensor", axis=1, tiled=True)
+    cots_q = lax.all_to_all(
+        cot_rows.reshape(expert_number, expert_capacity, feature_share),
+        "expert", split_axis=0, concat_axis=0, tiled=True,
+    ).reshape(send_rows, feature_share)
+    cots_all = lax.all_gather(cots_q, "tensor", axis=1, tiled=True)
     out_t, back_t, grads = expert_group_t(
-        expert_rows, expert_cots, w_gate[0], w_up[0], w_down[0]
+        rows_all, cots_all, w_gate[0], w_up[0], w_down[0]
     )
     total_out = lax.psum_scatter(out_t, "tensor", scatter_dimension=0, tiled=True)
+    sources = total_out.shape[1] // expert_capacity
+    came_out = lax.all_to_all(
+        total_out.T.reshape(sources, expert_capacity, feature_share),
+        "expert", split_axis=0, concat_axis=0, tiled=True,
+    ).reshape(send_rows, feature_share)
     total_back = lax.psum_scatter(back_t, "tensor", scatter_dimension=0, tiled=True)
-    sources = total_out.shape[1] // expert_capacity
-    slot_both = jnp.stack([total_out.T, total_back.T]).reshape(
-        2, sources, expert_capacity, feature_share
-    )
-    came = lax.all_to_all(slot_both, "expert", split_axis=1, concat_axis=1, tiled=True)
-    came = came.reshape(2, send_rows, feature_share)
-    came_out = came[0]
-    came_back = came[1]
+    came_back = lax.all_to_all(
+        total_back.T.reshape(sources, expert_capacity, feature_share),
+        "expert", split_axis=0, concat_axis=0, tiled=True,
+    ).reshape(send_rows, feature_share)
     positions = jnp.maximum(destination_slot, 0).reshape(-1)
     out_rows = (
         jnp.take(came_out, positions, axis=0)

time: 359 us -> 312 us (0.87)
  waiting for transfers between devices: 185 us -> 123 us
  blocking collectives: 64.2 us -> 77.2 us
  starting transfers between devices: 11 us -> 21.8 us
  local copies, waits for them, and re-layouts: 33.5 us -> 29.9 us
    all_to_all x1 -> x2, waiting for transfers between devices: 28.8 us -> 0.01 us  [the longest x1 0.01 us: local(): lax.all_to_all(total_out.T.reshape(sources, expert_capacity, feature_shar...]
    all_gather x1 -> x2, waiting for transfers between devices: 76.1 us -> 55.8 us  [the longest x1 44 us: local(): rows_all = lax.all_gather(rows_q, 'tensor', axis=1, tiled=True)]
    all_to_all x1 -> x2, blocking collectives: 55 us -> 68.1 us  [the longest x1 36.2 us: local(): lax.all_to_all(cot_rows.reshape(expert_number, expert_capacity, feature_s...]
    unnamed x5 -> x6, waiting for transfers between devices: 80.3 us -> 67.5 us
    all_to_all x1 -> x2, starting transfers between devices: 10.9 us -> 21.6 us  [the longest x1 10.9 us: local(): lax.all_to_all(total_back.T.reshape(sources, expert_capacity, feature_sha...]
    unnamed x32 -> x30, local copies, waits for them, and re-layouts: 16.8 us -> 16.7 us
  transfers between devices with their start and end apart: 4 -> 6, of which waited for: 4 -> 4; matrix products, arithmetic and copies ran while one was open for 8% -> 14% of each run, Pallas kernels for 0% -> 0%
where the time goes in v2:
time: 312 us; the launch traced here: 311 us
  waiting for transfers between devices  123 us (39%)
  blocking collectives  77.2 us (25%)
  matrix products  30.4 us (10%)
  local copies, waits for them, and re-layouts  29.9 us (10%)
  starting transfers between devices  21.8 us (7%)
  other arithmetic  14.2 us (5%)
  between operations  14 us (4%)
    unnamed x6, waiting for transfers between devices  67.5 us
    all_gather x1, waiting for transfers between devices, local(): rows_all = lax.all_gather(rows_q, 'tensor', axis=1, tiled=True)  44 us
    all_to_all x1, blocking collectives, local(): lax.all_to_all(cot_rows.reshape(expert_number, expert_capacity, feature_s...  36.2 us
    all_to_all x1, blocking collectives, local(): lax.all_to_all(token_sum.reshape(expert_number, expert_capacity, feature_...  31.8 us
    unnamed x30, local copies, waits for them, and re-layouts  16.7 us
    all_gather x1, waiting for transfers between devices, local(): cots_all = lax.all_gather(cots_q, 'tensor', axis=1, tiled=True)  11.8 us
    all_to_all x1, starting transfers between devices, local(): lax.all_to_all(total_back.T.reshape(sources, expert_capacity, feature_sha...  10.9 us
    all_to_all x1, starting transfers between devices, local(): lax.all_to_all(total_out.T.reshape(sources, expert_capacity, feature_shar...  10.7 us
  transfers between devices with their start and end apart: 6, of which 4 were waited for; matrix products, arithmetic and copies ran while one was open for 14% of the time, Pallas kernels for 0%

profile of v2, /device:TPU:6, one launch (start us, length us, event | category | flops | bytes accessed | tf_op | source)
XLA Modules:
  0.0 310.8 jit_solution(4196553413456630743)
XLA Ops:
  7.2 0.0 copy-start
  7.2 0.0 all-gather.5.cloned.1.call-start
  7.2 0.9 select_reduce_fusion.1
  8.2 0.7 broadcast_select_fusion.2
  8.9 0.7 broadcast_maximum_fusion
  9.6 1.7 select_reduce_fusion
  11.3 0.7 convert_reduce_fusion
  12.1 1.3 fusion.20
  13.4 36.2 %all_to_all.20 = bf16[64,8,896]{2,1,0:T(8,128)(2,1)} all-to-all(bf16[64,8,896]{2,1,0:T(8,128)(2,1)S(1)} %fusion.20), channel_id=1, replica_groups=mesh['expert'=64,'tensor'=4] {'expert'}, dimensions={0} | all-to-all | bytes 1835008 | tf_op jit(solution)/shard_map/all_to_all | solution.py:118
  49.6 0.0 all-gather.5.cloned.1.call-update
  49.7 0.0 all-gather.3.cloned.1.call-start
  49.7 1.3 fusion.19
  51.1 31.8 %all_to_all.21 = bf16[64,8,896]{2,1,0:T(8,128)(2,1)} all-to-all(bf16[64,8,896]{2,1,0:T(8,128)(2,1)S(1)} %fusion.19), channel_id=1, replica_groups=mesh['expert'=64,'tensor'=4] {'expert'}, dimensions={0} | all-to-all | bytes 1835008 | tf_op jit(solution)/shard_map/all_to_all | solution.py:113
  82.9 0.0 all-gather.3.cloned.1.call-update
  82.9 0.0 reduce-scatter.7.cloned.1.call-start
  83.0 11.8 %all-gather.5.cloned.1.call-done = bf16[512,3584]{1,0:T(8,128)(2,1)} async-done(((bf16[512,896]{1,0:T(8,128)(2,1)}), bf16[512,3584]{1,0:T(8,128)(2,1)}) %all-gather.5.cloned.1.call-update) | async-done | bytes 3670032 | tf_op jit(solution)/shard_map/all_gather | solution.py:122
  94.8 4.6 %fusion.9 = f32[512,256]{1,0:T(8,128)} fusion(bf16[512,3584]{1,0:T(8,128)(2,1)} %all-gather.5.cloned.1.call-done, bf16[1,256,3584]{2,1,0:T(8,128)(2,1)} %param.19), kind=kOutput, calls=%fused_computation.22 | convolution fusion | flops 939524096 | bytes 6029312 | tf_op jit(solution)/shard_map/dot_general | solution.py:66
  99.3 44.0 %all-gather.3.cloned.1.call-done = bf16[512,3584]{1,0:T(8,128)(2,1)} async-done(((bf16[512,896]{1,0:T(8,128)(2,1)}), bf16[512,3584]{1,0:T(8,128)(2,1)}) %all-gather.3.cloned.1.call-update) | async-done | bytes 3670032 | tf_op jit(solution)/shard_map/all_gather | solution.py:117
  143.3 3.9 %fusion.17 = f32[512,256]{1,0:T(8,128)S(1)} fusion(bf16[512,3584]{1,0:T(8,128)(2,1)} %all-gather.3.cloned.1.call-done, bf16[1,3584,256]{2,1,0:T(8,128)(2,1)} %param.17), kind=kOutput, calls=%fused_computation.30 | convolution fusion | flops 939524096 | bytes 6029312 | tf_op jit(solution)/shard_map/dot_general | solution.py:57
  147.2 0.0 copy-done
  147.2 0.0 copy-done.10
  147.2 0.0 copy-done.12
  147.2 0.0 copy-start.1
  147.2 1.2 multiply_convert_fusion.3
  148.4 0.0 copy-start.4
  148.5 0.0 copy-start.2
  148.5 0.2 copy-done.1
  148.7 3.0 fusion.1
  151.7 6.0 %copy.46 = bf16[3584,512]{1,0:T(8,128)(2,1)} copy(bf16[3584,512]{0,1:T(8,128)(2,1)} %fusion.1) | data formatting | bytes 7340032
  157.7 0.0 reduce-scatter.7.cloned.1.call-update
  157.7 0.0 reduce-scatter.9.cloned.1.call-start
  157.8 0.0 copy-done.4
  157.8 2.7 fusion.15
  160.4 3.1 fusion
  163.5 5.9 %copy.48 = bf16[3584,512]{1,0:T(8,128)(2,1)} copy(bf16[3584,512]{0,1:T(8,128)(2,1)} %fusion) | data formatting | bytes 7340032
  169.4 0.0 reduce-scatter.9.cloned.1.call-update
  169.5 33.8 %reduce-scatter.7.cloned.1.call-done = bf16[896,512]{1,0:T(8,128)(2,1)} async-done(((bf16[3584,512]{1,0:T(8,128)(2,1)}), bf16[896,512]{1,0:T(8,128)(2,1)}) %reduce-scatter.7.cloned.1.call-update) | async-done | bytes 917520
  203.3 2.2 copy.47
  205.5 10.7 %all-to-all-start.1 = ((bf16[64,8,896]{2,1,0:T(8,128)(2,1)}), bf16[64,8,896]{2,1,0:T(8,128)(2,1)S(1)}, u32[]{:S(2)}, u32[]{:S(2)}) async-start(bf16[64,8,896]{2,1,0:T(8,128)(2,1)} %bitcast.70), calls=%async_computation.1 | async-start | bytes 1835008 | tf_op jit(solution)/shard_map/all_to_all | solution.py:128
  216.3 0.1 copy.43
  216.4 0.1 reshape.64
  216.4 0.6 fusion.26
  217.0 33.6 %reduce-scatter.9.cloned.1.call-done = bf16[896,512]{1,0:T(8,128)(2,1)} async-done(((bf16[3584,512]{1,0:T(8,128)(2,1)}), bf16[896,512]{1,0:T(8,128)(2,1)}) %reduce-scatter.9.cloned.1.call-update) | async-done | bytes 917520
  250.6 2.3 copy.49
  252.9 0.0 all-to-all-done.1
  252.9 10.9 %all-to-all-start.3 = ((bf16[64,8,896]{2,1,0:T(8,128)(2,1)}), bf16[64,8,896]{2,1,0:T(8,128)(2,1)}, u32[]{:S(2)}, u32[]{:S(2)}) async-start(bf16[64,8,896]{2,1,0:T(8,128)(2,1)} %bitcast.68), calls=%async_computation.3 | async-start | bytes 1835008 | tf_op jit(solution)/shard_map/all_to_all | solution.py:133
  263.8 0.6 compare_and_fusion
  264.4 0.0 copy-done.7
  264.4 0.1 copy.44
  264.5 0.1 copy.42
  264.6 1.0 dynamic-slice_convert_fusion
  265.6 0.0 copy-start.5
  265.6 4.6 %fusion.4 = bf16[1,256,3584]{2,1,0:T(8,128)(2,1)} fusion(bf16[512,256]{1,0:T(8,128)(2,1)S(1)} %get-tuple-element.25, bf16[512,3584]{1,0:T(8,128)(2,1)} %all-gather.5.cloned.1.call-done), kind=kOutput, calls=%fused_computation.11 | convolution fusion | flops 940441600 | bytes 5767168 | tf_op jit(solution)/shard_map/dot_general | solution.py:81
  270.2 2.4 fusion.2
  272.6 0.0 copy-done.3
  272.6 2.4 fusion.3
  275.0 5.6 %gather_fusion = bf16[1024,896]{1,0:T(8,128)(2,1)} fusion(bf16[512,896]{1,0:T(8,128)(2,1)S(1)} %bitcast.67, s32[1024]{0:T(1024)} %fusion.26), kind=kCustom, calls=%fused_computation.clone | custom fusion | bytes 3674112 | tf_op jit(solution)/shard_map/jit(_take)/gather | solution.py:139
  280.6 0.0 copy-done.9
  280.6 2.3 fusion.7
  282.9 0.1 reduce_sum.62
  283.0 9.1 %psum.7 = f32[128,8]{0,1:T(8,128)} all-reduce(f32[128,8]{0,1:T(8,128)S(1)} %broadcast_select_fusion.1), channel_id=1, replica_groups=mesh['expert'=64,'tensor'=4] {'tensor'}, use_global_device_ids=true, to_apply=%region_8.10 | all-reduce | flops 1024 | bytes 8192 | tf_op jit(solution)/shard_map/psum | solution.py:155
  292.2 0.0 all-to-all-done.3
  292.2 7.1 %gather_fusion.1 = bf16[1024,896]{1,0:T(8,128)(2,1)} fusion(bf16[512,896]{1,0:T(8,128)(2,1)} %bitcast.16, s32[1024]{0:T(1024)S(1)} %copy-done.6), kind=kCustom, calls=%fused_computation.1.clone | custom fusion | bytes 3674112 | tf_op jit(solution)/shard_map/jit(_take)/gather | solution.py:144
  299.3 5.0 %fusion.8 = (bf16[128,896]{1,0:T(8,128)(2,1)}, bf16[128,896]{1,0:T(8,128)(2,1)}) fusion(bf16[1024,896]{1,0:T(8,128)(2,1)} %gather_fusion.1, pred[1024]{0:T(1024)(128)(4,1)S(1)} %copy-done.9, pred[128,8]{1,0:T(8,128)(4,1)S(1)} %copy.44, bf16[1024,896]{1,0:T(8,128)(2,1)} %gather_fusion, f32[128,8]{1,0:T(8,128)S(1)} %copy.42), kind=kLoop, calls=%fused_computation.18 | loop fusion | flops 7110656 | bytes 4134912 | tf_op jit(solution)/shard_map/reduce_sum | solution.py:150
  (15 shorter events, 0.1 us)
Async XLA Ops:
  7.2 140.0 %copy-start = (bf16[1,3584,256]{2,1,0:T(8,128)(2,1)S(1)}, bf16[1,3584,256]{2,1,0:T(8,128)(2,1)}, u32[]{:S(2)}) copy-start(bf16[1,3584,256]{2,1,0:T(8,128)(2,1)} %param.18) | copy-start | bytes 5505028
  7.2 87.6 %all-gather.5.cloned.1.call-start = ((), (), s32[]{:S(2)}) async-start(), calls=%async_computation.7 | async-start | bytes 4587520 | tf_op jit(solution)/shard_map/all_gather | solution.py:122
  8.9 255.5 %copy-start.7 = (pred[128,8]{0,1:T(8,128)(4,1)}, pred[128,8]{0,1:T(8,128)(4,1)S(1)}, u32[]{:S(2)}) copy-start(pred[128,8]{0,1:T(8,128)(4,1)S(1)} %get-tuple-element.22) | copy-start | bytes 3076
  49.7 93.6 %all-gather.3.cloned.1.call-start = ((), (), s32[]{:S(2)}) async-start(), calls=%async_computation.6 | async-start | bytes 4587520 | tf_op jit(solution)/shard_map/all_gather | solution.py:117
  82.9 120.4 %reduce-scatter.7.cloned.1.call-start = ((), (), s32[]{:S(2)}) async-start(), calls=%async_computation.8 | async-start | bytes 4587520
  143.3 3.9 %copy-start.10 = (bf16[512,3584]{1,0:T(8,128)(2,1)S(1)}, bf16[512,3584]{1,0:T(8,128)(2,1)}, u32[]{:S(2)}) copy-start(bf16[512,3584]{1,0:T(8,128)(2,1)} %all-gather.3.cloned.1.call-done) | copy-start | bytes 11010052
  143.3 3.9 %copy-start.12 = (f32[512,256]{1,0:T(8,128)S(1)}, f32[512,256]{1,0:T(8,128)}, u32[]{:S(2)}) copy-start(f32[512,256]{1,0:T(8,128)} %fusion.9) | copy-start | bytes 1572868
  147.2 1.5 copy-start.1
  148.4 9.3 %copy-start.4 = (bf16[512,256]{1,0:T(8,128)(2,1)}, bf16[512,256]{1,0:T(8,128)(2,1)S(1)}, u32[]{:S(2)}) copy-start(bf16[512,256]{1,0:T(8,128)(2,1)S(1)} %get-tuple-element.26) | copy-start | bytes 786436
  148.5 12.0 %copy-start.2 = (bf16[512,256]{1,0:T(8,128)(2,1)}, bf16[512,256]{1,0:T(8,128)(2,1)S(1)}, u32[]{:S(2)}) copy-start(bf16[512,256]{1,0:T(8,128)(2,1)S(1)} %get-tuple-element.27) | copy-start | bytes 786436
  157.7 92.9 %reduce-scatter.9.cloned.1.call-start = ((), (), s32[]{:S(2)}) async-start(), calls=%async_computation.9 | async-start | bytes 4587520
  205.5 47.4 %all-to-all-start.1 = ((bf16[64,8,896]{2,1,0:T(8,128)(2,1)}), bf16[64,8,896]{2,1,0:T(8,128)(2,1)S(1)}, u32[]{:S(2)}, u32[]{:S(2)}) async-start(bf16[64,8,896]{2,1,0:T(8,128)(2,1)} %bitcast.70), calls=%async_computation.1 | async-start | bytes 1835008 | tf_op jit(solution)/shard_map/all_to_all | solution.py:128
  252.9 39.3 %all-to-all-start.3 = ((bf16[64,8,896]{2,1,0:T(8,128)(2,1)}), bf16[64,8,896]{2,1,0:T(8,128)(2,1)}, u32[]{:S(2)}, u32[]{:S(2)}) async-start(bf16[64,8,896]{2,1,0:T(8,128)(2,1)} %bitcast.68), calls=%async_computation.3 | async-start | bytes 1835008 | tf_op jit(solution)/shard_map/all_to_all | solution.py:133
  265.6 4.6 %copy-start.5 = (bf16[512,256]{1,0:T(8,128)(2,1)S(1)}, bf16[512,256]{1,0:T(8,128)(2,1)}, u32[]{:S(2)}) copy-start(bf16[512,256]{1,0:T(8,128)(2,1)} %copy-done.4) | copy-start | bytes 786436
  265.6 4.6 %copy-start.11 = (bf16[512,3584]{1,0:T(8,128)(2,1)S(1)}, bf16[512,3584]{1,0:T(8,128)(2,1)}, u32[]{:S(2)}) copy-start(bf16[512,3584]{1,0:T(8,128)(2,1)} %all-gather.3.cloned.1.call-done) | copy-start | bytes 11010052
  270.2 2.4 copy-start.3
  275.0 5.6 %copy-start.9 = (pred[1024]{0:T(1024)(128)(4,1)S(1)}, pred[1024]{0:T(1024)(128)(4,1)}, u32[]{:S(2)}) copy-start(pred[1024]{0:T(1024)(128)(4,1)} %compare_and_fusion) | copy-start | bytes 3076
  280.6 2.4 copy-start.8
  280.6 11.6 %copy-start.6 = (s32[1024]{0:T(1024)S(1)}, s32[1024]{0:T(1024)}, u32[]{:S(2)}) copy-start(s32[1024]{0:T(1024)} %fusion.26) | copy-start | bytes 12292
Sparse Core Ops, SparseCore 0:
  49.8 44.9 all-gather.4
  96.6 46.6 all-gather.2
  157.8 45.4 reduce-scatter.6
  205.7 44.8 reduce-scatter.8

commit v3 on v2

--- a/solution.py
+++ b/solution.py
@@ -59,6 +59,9 @@
     logistic = jax.nn.sigmoid(pre_gate)
     active = pre_gate * logistic
     hidden = (active * pre_up).astype(jnp.bfloat16)
+    pre_gate, pre_up, logistic, active, hidden = lax.optimization_barrier(
+        (pre_gate, pre_up, logistic, active, hidden)
+    )
     contract_h = (((1,), (1,)), ((), ()))
     out_t = lax.dot_general(
         down_weight.T, hidden, contract_h, preferred_element_type=jnp.float32
@@ -114,6 +117,7 @@
         token_sum.reshape(expert_number, expert_capacity, feature_share),
         "expert", split_axis=0, concat_axis=0, tiled=True,
     ).reshape(send_rows, feature_share)
+    rows_q, cot_rows = lax.optimization_barrier((rows_q, cot_rows))
     rows_all = lax.all_gather(rows_q, "tensor", axis=1, tiled=True)
     cots_q = lax.all_to_all(
         cot_rows.reshape(expert_number, expert_capacity, feature_share),

time: 312 us -> 300 us (0.962)
  blocking collectives: 77.2 us -> 41.2 us
  starting transfers between devices: 21.8 us -> 34 us
  waiting for transfers between devices: 123 us -> 135 us
    all_to_all x1 -> x0, blocking collectives: 31.8 us -> none  [local(): lax.all_to_all(token_sum.reshape(expert_number, expert_capacity, feature_...]
    all_gather x1, waiting for transfers between devices: 44 us -> 12.9 us  [local(): rows_all = lax.all_gather(rows_q, 'tensor', axis=1, tiled=True)]
    all_gather x1, waiting for transfers between devices: 11.8 us -> 33.6 us  [local(): cots_all = lax.all_gather(cots_q, 'tensor', axis=1, tiled=True)]
    all_to_all x0 -> x1, waiting for transfers between devices: none -> 20.8 us  [local(): lax.all_to_all(token_sum.reshape(expert_number, expert_capacity, feature_...]
    all_to_all x0 -> x1, starting transfers between devices: none -> 12.2 us  [local(): lax.all_to_all(token_sum.reshape(expert_number, expert_capacity, feature_...]
    all_to_all x1, blocking collectives: 36.2 us -> 32.1 us  [local(): lax.all_to_all(cot_rows.reshape(expert_number, expert_capacity, feature_s...]
    unnamed x30 -> x34, local copies, waits for them, and re-layouts: 16.7 us -> 17.4 us
  transfers between devices with their start and end apart: 6 -> 7, of which waited for: 4 -> 5; matrix products, arithmetic and copies ran while one was open for 14% -> 19% of each run, Pallas kernels for 0% -> 0%
where the time goes in v3:
time: 300 us; the launch traced here: 299 us
  waiting for transfers between devices  135 us (45%)
  blocking collectives  41.2 us (14%)
  starting transfers between devices  34 us (11%)
  matrix products  31 us (10%)
  local copies, waits for them, and re-layouts  30.3 us (10%)
  between operations  14 us (5%)
  other arithmetic  13.5 us (4%)
    unnamed x6, waiting for transfers between devices  67.4 us
    all_gather x1, waiting for transfers between devices, local(): cots_all = lax.all_gather(cots_q, 'tensor', axis=1, tiled=True)  33.6 us
    all_to_all x1, blocking collectives, local(): lax.all_to_all(cot_rows.reshape(expert_number, expert_capacity, feature_s...  32.1 us
    all_to_all x1, waiting for transfers between devices, local(): lax.all_to_all(token_sum.reshape(expert_number, expert_capacity, feature_...  20.8 us
    unnamed x34, local copies, waits for them, and re-layouts  17.4 us
    all_gather x1, waiting for transfers between devices, local(): rows_all = lax.all_gather(rows_q, 'tensor', axis=1, tiled=True)  12.9 us
    all_to_all x1, starting transfers between devices, local(): lax.all_to_all(token_sum.reshape(expert_number, expert_capacity, feature_...  12.2 us
    all_to_all x1, starting transfers between devices, local(): lax.all_to_all(total_back.T.reshape(sources, expert_capacity, feature_sha...  10.9 us
  transfers between devices with their start and end apart: 7, of which 5 were waited for; matrix products, arithmetic and copies ran while one was open for 19% of the time, Pallas kernels for 0%

profile of v3, /device:TPU:6, one launch (start us, length us, event | category | flops | bytes accessed | tf_op | source)
XLA Modules:
  0.0 298.6 jit_solution(7754781590543957501)
XLA Ops:
  7.2 0.0 copy-start
  7.2 0.0 copy-start.9
  7.2 0.9 select_reduce_fusion.1
  8.1 0.7 broadcast_select_fusion.2
  8.9 0.7 broadcast_maximum_fusion
  9.6 0.7 convert_reduce_fusion
  10.3 2.3 fusion.19
  12.6 12.2 %all-to-all-start = ((bf16[64,8,896]{2,1,0:T(8,128)(2,1)}), bf16[64,8,896]{2,1,0:T(8,128)(2,1)S(1)}, u32[]{:S(2)}, u32[]{:S(2)}) async-start(bf16[64,8,896]{2,1,0:T(8,128)(2,1)} %fusion.19), calls=%async_computation | async-start | bytes 1835008 | tf_op jit(solution)/shard_map/all_to_all | solution.py:116
  24.7 0.0 all-gather.3.cloned.1.call-start
  24.8 0.0 copy-done.9
  24.8 1.0 select_reduce_fusion
  25.8 2.3 multiply_convert_fusion
  28.1 20.8 %all-to-all-done = bf16[64,8,896]{2,1,0:T(8,128)(2,1)S(1)} async-done(((bf16[64,8,896]{2,1,0:T(8,128)(2,1)}), bf16[64,8,896]{2,1,0:T(8,128)(2,1)S(1)}, u32[]{:S(2)}, u32[]{:S(2)}) %all-to-all-start) | async-done | bytes 917536 | tf_op jit(solution)/shard_map/all_to_all | solution.py:116
  48.9 0.9 copy-done.2
  49.8 0.0 all-gather.3.cloned.1.call-update
  49.9 0.0 all-gather.5.cloned.1.call-start
  49.9 32.1 %all_to_all.20 = bf16[64,8,896]{2,1,0:T(8,128)(2,1)} all-to-all(bf16[64,8,896]{2,1,0:T(8,128)(2,1)} %bitcast.72), channel_id=1, replica_groups=mesh['expert'=64,'tensor'=4] {'expert'}, dimensions={0} | all-to-all | bytes 1835008 | tf_op jit(solution)/shard_map/all_to_all | solution.py:122
  82.0 0.0 all-gather.5.cloned.1.call-update
  82.0 0.0 reduce-scatter.7.cloned.1.call-start
  82.0 12.9 %all-gather.3.cloned.1.call-done = bf16[512,3584]{1,0:T(8,128)(2,1)} async-done(((bf16[512,896]{1,0:T(8,128)(2,1)}), bf16[512,3584]{1,0:T(8,128)(2,1)}) %all-gather.3.cloned.1.call-update) | async-done | bytes 3670032 | tf_op jit(solution)/shard_map/all_gather | solution.py:121
  94.9 3.9 %fusion.17 = f32[512,256]{1,0:T(8,128)S(1)} fusion(bf16[512,3584]{1,0:T(8,128)(2,1)} %all-gather.3.cloned.1.call-done, bf16[1,3584,256]{2,1,0:T(8,128)(2,1)} %param.17), kind=kOutput, calls=%fused_computation.30 | convolution fusion | flops 939524096 | bytes 6029312 | tf_op jit(solution)/shard_map/dot_general | solution.py:57
  98.8 0.0 copy-done
  98.8 0.0 copy-start.1
  98.8 2.0 multiply_convert_fusion.3
  100.9 3.0 %fusion.1 = bf16[3584,512]{0,1:T(8,128)(2,1)} fusion(bf16[512,256]{1,0:T(8,128)(2,1)S(1)} %get-tuple-element.15, bf16[1,256,3584]{2,1,0:T(8,128)(2,1)S(1)} %copy-done.1), kind=kOutput, calls=%fused_computation.5 | convolution fusion | flops 941359104 | bytes 5767168 | tf_op jit(solution)/shard_map/dot_general | solution.py:66
  103.9 6.0 %copy.46 = bf16[3584,512]{1,0:T(8,128)(2,1)} copy(bf16[3584,512]{0,1:T(8,128)(2,1)} %fusion.1) | data formatting | bytes 7340032
  109.9 0.0 reduce-scatter.7.cloned.1.call-update
  109.9 0.0 reduce-scatter.9.cloned.1.call-start
  109.9 33.6 %all-gather.5.cloned.1.call-done = bf16[512,3584]{1,0:T(8,128)(2,1)} async-done(((bf16[512,896]{1,0:T(8,128)(2,1)}), bf16[512,3584]{1,0:T(8,128)(2,1)}) %all-gather.5.cloned.1.call-update) | async-done | bytes 3670032 | tf_op jit(solution)/shard_map/all_gather | solution.py:126
  143.5 4.1 %multiply_convert_fusion.1 = (bf16[512,256]{1,0:T(8,128)(2,1)S(1)}, bf16[512,256]{1,0:T(8,128)(2,1)S(1)}) fusion(f32[512,256]{1,0:T(8,128)S(1)} %get-tuple-element.20, f32[512,256]{1,0:T(8,128)S(1)} %fusion.17, f32[512,256]{1,0:T(8,128)} %get-tuple-element.18, f32[512,256]{1,0:T(8,128)} %get-tuple-element.17, ...), kind=kOutput, calls=%fused_computation.36 | convolution fusion | flops 940703744 | bytes 8126464 | tf_op jit(solution)/shard_map/dot_general | solution.py:69
  147.6 0.0 copy-start.4
  147.6 0.0 copy-start.6
  147.6 1.1 fusion.15
  148.8 0.0 copy-done.4
  148.8 0.0 copy-done.6
  148.8 3.0 fusion
  151.8 5.9 %copy.48 = bf16[3584,512]{1,0:T(8,128)(2,1)} copy(bf16[3584,512]{0,1:T(8,128)(2,1)} %fusion) | data formatting | bytes 7340032
  157.7 0.0 reduce-scatter.9.cloned.1.call-update
  157.7 33.8 %reduce-scatter.7.cloned.1.call-done = bf16[896,512]{1,0:T(8,128)(2,1)} async-done(((bf16[3584,512]{1,0:T(8,128)(2,1)}), bf16[896,512]{1,0:T(8,128)(2,1)}) %reduce-scatter.7.cloned.1.call-update) | async-done | bytes 917520
  191.5 2.2 copy.47
  193.7 10.7 %all-to-all-start.1 = ((bf16[64,8,896]{2,1,0:T(8,128)(2,1)}), bf16[64,8,896]{2,1,0:T(8,128)(2,1)S(1)}, u32[]{:S(2)}, u32[]{:S(2)}) async-start(bf16[64,8,896]{2,1,0:T(8,128)(2,1)} %bitcast.73), calls=%async_computation.1 | async-start | bytes 1835008 | tf_op jit(solution)/shard_map/all_to_all | solution.py:132
  204.5 0.1 copy.43
  204.6 0.1 reshape.64
  204.7 0.6 fusion.24
  205.3 33.6 %reduce-scatter.9.cloned.1.call-done = bf16[896,512]{1,0:T(8,128)(2,1)} async-done(((bf16[3584,512]{1,0:T(8,128)(2,1)}), bf16[896,512]{1,0:T(8,128)(2,1)}) %reduce-scatter.9.cloned.1.call-update) | async-done | bytes 917520
  238.8 2.3 copy.49
  241.1 0.0 all-to-all-done.1
  241.1 10.9 %all-to-all-start.3 = ((bf16[64,8,896]{2,1,0:T(8,128)(2,1)}), bf16[64,8,896]{2,1,0:T(8,128)(2,1)}, u32[]{:S(2)}, u32[]{:S(2)}) async-start(bf16[64,8,896]{2,1,0:T(8,128)(2,1)} %bitcast.69), calls=%async_computation.3 | async-start | bytes 1835008 | tf_op jit(solution)/shard_map/all_to_all | solution.py:137
  252.0 0.6 compare_and_fusion
  252.6 0.1 copy.44
  252.7 0.1 copy.42
  252.8 1.0 dynamic-slice_convert_fusion
  253.8 0.0 copy-start.7
  253.8 4.6 %fusion.4 = bf16[1,256,3584]{2,1,0:T(8,128)(2,1)} fusion(bf16[512,256]{1,0:T(8,128)(2,1)S(1)} %get-tuple-element.15, bf16[512,3584]{1,0:T(8,128)(2,1)} %all-gather.5.cloned.1.call-done), kind=kOutput, calls=%fused_computation.11 | convolution fusion | flops 940441600 | bytes 5767168 | tf_op jit(solution)/shard_map/dot_general | solution.py:84
  258.4 2.4 fusion.3
  260.8 2.4 fusion.2
  263.2 5.3 %gather_fusion = bf16[1024,896]{1,0:T(8,128)(2,1)} fusion(bf16[512,896]{1,0:T(8,128)(2,1)S(1)} %bitcast.68, s32[1024]{0:T(1024)S(1)} %copy-done.8), kind=kCustom, calls=%fused_computation.clone | custom fusion | bytes 3674112 | tf_op jit(solution)/shard_map/jit(_take)/gather | solution.py:143
  268.5 0.0 copy-done.12
  268.5 2.3 fusion.7
  270.7 0.1 reduce_sum.62
  270.9 9.1 %psum.7 = f32[128,8]{0,1:T(8,128)} all-reduce(f32[128,8]{0,1:T(8,128)S(1)} %broadcast_select_fusion.1), channel_id=1, replica_groups=mesh['expert'=64,'tensor'=4] {'tensor'}, use_global_device_ids=true, to_apply=%region_8.10 | all-reduce | flops 1024 | bytes 8192 | tf_op jit(solution)/shard_map/psum | solution.py:159
  280.0 0.0 all-to-all-done.3
  280.0 7.1 %gather_fusion.1 = bf16[1024,896]{1,0:T(8,128)(2,1)} fusion(bf16[512,896]{1,0:T(8,128)(2,1)} %bitcast.16, s32[1024]{0:T(1024)S(1)} %copy-done.8), kind=kCustom, calls=%fused_computation.1.clone | custom fusion | bytes 3674112 | tf_op jit(solution)/shard_map/jit(_take)/gather | solution.py:148
  287.1 5.0 %fusion.8 = (bf16[128,896]{1,0:T(8,128)(2,1)}, bf16[128,896]{1,0:T(8,128)(2,1)}) fusion(bf16[1024,896]{1,0:T(8,128)(2,1)} %gather_fusion.1, pred[1024]{0:T(1024)(128)(4,1)S(1)} %copy-done.12, pred[128,8]{1,0:T(8,128)(4,1)S(1)} %copy.44, bf16[1024,896]{1,0:T(8,128)(2,1)} %gather_fusion, f32[128,8]{1,0:T(8,128)S(1)} %copy.42), kind=kLoop, calls=%fused_computation.18 | loop fusion | flops 7110656 | bytes 4134912 | tf_op jit(solution)/shard_map/reduce_sum | solution.py:154
  (20 shorter events, 0.1 us)
Async XLA Ops:
  7.2 91.6 %copy-start = (bf16[1,3584,256]{2,1,0:T(8,128)(2,1)S(1)}, bf16[1,3584,256]{2,1,0:T(8,128)(2,1)}, u32[]{:S(2)}) copy-start(bf16[1,3584,256]{2,1,0:T(8,128)(2,1)} %param.18) | copy-start | bytes 5505028
  7.2 17.6 %copy-start.9 = (f32[128,8]{0,1:T(8,128)S(1)}, f32[128,8]{0,1:T(8,128)}, u32[]{:S(2)}) copy-start(f32[128,8]{0,1:T(8,128)} %param.15) | copy-start | bytes 12292
  8.9 243.7 %copy-start.10 = (pred[128,8]{0,1:T(8,128)(4,1)}, pred[128,8]{0,1:T(8,128)(4,1)S(1)}, u32[]{:S(2)}) copy-start(pred[128,8]{0,1:T(8,128)(4,1)S(1)} %get-tuple-element.36) | copy-start | bytes 3076
  12.6 36.3 %all-to-all-start = ((bf16[64,8,896]{2,1,0:T(8,128)(2,1)}), bf16[64,8,896]{2,1,0:T(8,128)(2,1)S(1)}, u32[]{:S(2)}, u32[]{:S(2)}) async-start(bf16[64,8,896]{2,1,0:T(8,128)(2,1)} %fusion.19), calls=%async_computation | async-start | bytes 1835008 | tf_op jit(solution)/shard_map/all_to_all | solution.py:116
  24.7 70.2 %all-gather.3.cloned.1.call-start = ((), (), s32[]{:S(2)}) async-start(), calls=%async_computation.6 | async-start | bytes 4587520 | tf_op jit(solution)/shard_map/all_gather | solution.py:121
  48.9 0.9 copy-start.2
  49.9 93.6 %all-gather.5.cloned.1.call-start = ((), (), s32[]{:S(2)}) async-start(), calls=%async_computation.7 | async-start | bytes 4587520 | tf_op jit(solution)/shard_map/all_gather | solution.py:126
  82.0 109.5 %reduce-scatter.7.cloned.1.call-start = ((), (), s32[]{:S(2)}) async-start(), calls=%async_computation.8 | async-start | bytes 4587520
  94.9 3.9 %copy-start.13 = (bf16[512,3584]{1,0:T(8,128)(2,1)S(1)}, bf16[512,3584]{1,0:T(8,128)(2,1)}, u32[]{:S(2)}) copy-start(bf16[512,3584]{1,0:T(8,128)(2,1)} %all-gather.3.cloned.1.call-done) | copy-start | bytes 11010052
  98.8 2.0 copy-start.1
  109.9 128.9 %reduce-scatter.9.cloned.1.call-start = ((), (), s32[]{:S(2)}) async-start(), calls=%async_computation.9 | async-start | bytes 4587520
  143.5 4.1 %copy-start.3 = (bf16[1,3584,256]{2,1,0:T(8,128)(2,1)S(1)}, bf16[1,3584,256]{2,1,0:T(8,128)(2,1)}, u32[]{:S(2)}) copy-start(bf16[1,3584,256]{2,1,0:T(8,128)(2,1)} %param.17) | copy-start | bytes 5505028
  147.6 1.2 copy-start.4
  147.6 1.2 copy-start.6
  193.7 47.4 %all-to-all-start.1 = ((bf16[64,8,896]{2,1,0:T(8,128)(2,1)}), bf16[64,8,896]{2,1,0:T(8,128)(2,1)S(1)}, u32[]{:S(2)}, u32[]{:S(2)}) async-start(bf16[64,8,896]{2,1,0:T(8,128)(2,1)} %bitcast.73), calls=%async_computation.1 | async-start | bytes 1835008 | tf_op jit(solution)/shard_map/all_to_all | solution.py:132
  241.1 38.9 %all-to-all-start.3 = ((bf16[64,8,896]{2,1,0:T(8,128)(2,1)}), bf16[64,8,896]{2,1,0:T(8,128)(2,1)}, u32[]{:S(2)}, u32[]{:S(2)}) async-start(bf16[64,8,896]{2,1,0:T(8,128)(2,1)} %bitcast.69), calls=%async_computation.3 | async-start | bytes 1835008 | tf_op jit(solution)/shard_map/all_to_all | solution.py:137
  253.8 4.6 %copy-start.7 = (bf16[512,256]{1,0:T(8,128)(2,1)S(1)}, bf16[512,256]{1,0:T(8,128)(2,1)}, u32[]{:S(2)}) copy-start(bf16[512,256]{1,0:T(8,128)(2,1)} %copy-done.6) | copy-start | bytes 786436
  253.8 4.6 %copy-start.14 = (bf16[512,3584]{1,0:T(8,128)(2,1)S(1)}, bf16[512,3584]{1,0:T(8,128)(2,1)}, u32[]{:S(2)}) copy-start(bf16[512,3584]{1,0:T(8,128)(2,1)} %all-gather.3.cloned.1.call-done) | copy-start | bytes 11010052
  258.4 2.4 copy-start.5
  260.8 2.4 copy-start.8
  263.2 5.3 %copy-start.12 = (pred[1024]{0:T(1024)(128)(4,1)S(1)}, pred[1024]{0:T(1024)(128)(4,1)}, u32[]{:S(2)}) copy-start(pred[1024]{0:T(1024)(128)(4,1)} %compare_and_fusion) | copy-start | bytes 3076
  268.5 2.4 copy-start.11
Sparse Core Ops, SparseCore 0:
  50.0 44.9 all-gather.2
  96.8 46.6 all-gather.4
  146.1 45.4 reduce-scatter.6
  193.9 44.8 reduce-scatter.8

commit v4 on v3

--- a/solution.py
+++ b/solution.py
@@ -110,8 +110,11 @@
     )
     local_tokens = lax.dynamic_slice_in_dim(tokens, first_col, feature_share, 1)
     local_cotangent_bf = lax.dynamic_slice_in_dim(cotangent, first_col, feature_share, 1)
-    token_sum, cot_rows = pack_slots(
-        local_tokens, local_cotangent_bf, routing_gate_weight, destination_slot, send_rows
+    token_sum, _ = pack_slots(
+        local_tokens, local_cotangent_bf[:, :0], routing_gate_weight, destination_slot, send_rows
+    )
+    _, cot_rows = pack_slots(
+        tokens[:, :0], cotangent, routing_gate_weight, destination_slot, send_rows
     )
     rows_q = lax.all_to_all(
         token_sum.reshape(expert_number, expert_capacity, feature_share),
@@ -119,11 +122,10 @@
     ).reshape(send_rows, feature_share)
     rows_q, cot_rows = lax.optimization_barrier((rows_q, cot_rows))
     rows_all = lax.all_gather(rows_q, "tensor", axis=1, tiled=True)
-    cots_q = lax.all_to_all(
-        cot_rows.reshape(expert_number, expert_capacity, feature_share),
+    cots_all = lax.all_to_all(
+        cot_rows.reshape(expert_number, expert_capacity, feature_width),
         "expert", split_axis=0, concat_axis=0, tiled=True,
-    ).reshape(send_rows, feature_share)
-    cots_all = lax.all_gather(cots_q, "tensor", axis=1, tiled=True)
+    ).reshape(send_rows, feature_width)
     out_t, back_t, grads = expert_group_t(
         rows_all, cots_all, w_gate[0], w_up[0], w_down[0]
     )

time: 300 us -> 264 us (0.88)
  blocking collectives: 41.2 us -> 9.18 us
  waiting for transfers between devices: 135 us -> 121 us
  starting transfers between devices: 34 us -> 41.9 us
    all_gather x1 -> x0, waiting for transfers between devices: 33.6 us -> none  [local(): cots_all = lax.all_gather(cots_q, 'tensor', axis=1, tiled=True)]
    unnamed x6 -> x5, waiting for transfers between devices: 67.4 us -> 34.4 us
    all_to_all x1 -> x0, blocking collectives: 32.1 us -> none  [local(): lax.all_to_all(cot_rows.reshape(expert_number, expert_capacity, feature_s...]
    all_to_all x0 -> x1, waiting for transfers between devices: none -> 30.6 us  [local(): lax.all_to_all(cot_rows.reshape(expert_number, expert_capacity, feature_w...]
    all_gather x1, waiting for transfers between devices: 12.9 us -> 37.1 us  [local(): rows_all = lax.all_gather(rows_q, 'tensor', axis=1, tiled=True)]
    all_to_all x0 -> x1, starting transfers between devices: none -> 7.95 us  [local(): lax.all_to_all(cot_rows.reshape(expert_number, expert_capacity, feature_w...]
  transfers between devices with their start and end apart: 7 -> 7, of which waited for: 5 -> 5; matrix products, arithmetic and copies ran while one was open for 19% -> 22% of each run, Pallas kernels for 0% -> 0%
where the time goes in v4:
time: 264 us; the launch traced here: 263 us
  waiting for transfers between devices  121 us (46%)
  starting transfers between devices  41.9 us (16%)
  matrix products  32.9 us (12%)
  local copies, waits for them, and re-layouts  30.3 us (11%)
  between operations  14 us (5%)
  other arithmetic  13.5 us (5%)
  blocking collectives  9.18 us (3%)
    all_gather x1, waiting for transfers between devices, local(): rows_all = lax.all_gather(rows_q, 'tensor', axis=1, tiled=True)  37.1 us
    unnamed x5, waiting for transfers between devices  34.4 us
    all_to_all x1, waiting for transfers between devices, local(): lax.all_to_all(cot_rows.reshape(expert_number, expert_capacity, feature_w...  30.6 us
    all_to_all x1, waiting for transfers between devices, local(): lax.all_to_all(token_sum.reshape(expert_number, expert_capacity, feature_...  18.9 us
    unnamed x34, local copies, waits for them, and re-layouts  17.4 us
    all_to_all x1, starting transfers between devices, local(): lax.all_to_all(token_sum.reshape(expert_number, expert_capacity, feature_...  12.2 us
    all_to_all x1, starting transfers between devices, local(): lax.all_to_all(total_back.T.reshape(sources, expert_capacity, feature_sha...  10.9 us
    all_to_all x1, starting transfers between devices, local(): lax.all_to_all(total_out.T.reshape(sources, expert_capacity, feature_shar...  10.7 us
  transfers between devices with their start and end apart: 7, of which 5 were waited for; matrix products, arithmetic and copies ran while one was open for 22% of the time, Pallas kernels for 0%

profile of v4, /device:TPU:6, one launch (start us, length us, event | category | flops | bytes accessed | tf_op | source)
XLA Modules:
  0.0 262.6 jit_solution(7142021216410195462)
XLA Ops:
  7.2 0.0 copy-start
  7.2 0.0 copy-start.9
  7.2 0.9 select_reduce_fusion.1
  8.1 0.7 broadcast_select_fusion.2
  8.9 0.7 broadcast_maximum_fusion
  9.6 0.7 convert_reduce_fusion
  10.3 2.3 fusion.21
  12.6 12.2 %all-to-all-start = ((bf16[64,8,896]{2,1,0:T(8,128)(2,1)}), bf16[64,8,896]{2,1,0:T(8,128)(2,1)S(1)}, u32[]{:S(2)}, u32[]{:S(2)}) async-start(bf16[64,8,896]{2,1,0:T(8,128)(2,1)} %fusion.21), calls=%async_computation | async-start | bytes 1835008 | tf_op jit(solution)/shard_map/all_to_all | solution.py:119
  24.7 0.0 all-gather.2.cloned.1.call-start
  24.8 0.0 copy-done.9
  24.8 1.0 select_reduce_fusion
  25.8 4.2 %multiply_convert_fusion = bf16[512,3584]{1,0:T(8,128)(2,1)} fusion(bf16[128,3584]{1,0:T(8,128)(2,1)} %param.12, f32[512]{0:T(512)S(1)} %select_reduce_fusion, s32[512,128]{1,0:T(8,128)S(1)} %convert_reduce_fusion), kind=kOutput, calls=%fused_computation.3 | convolution fusion | flops 473497600 | bytes 4851712 | tf_op jit(solution)/shard_map/dot_general | solution.py:25
  30.0 18.9 %all-to-all-done = bf16[64,8,896]{2,1,0:T(8,128)(2,1)S(1)} async-done(((bf16[64,8,896]{2,1,0:T(8,128)(2,1)}), bf16[64,8,896]{2,1,0:T(8,128)(2,1)S(1)}, u32[]{:S(2)}, u32[]{:S(2)}) %all-to-all-start) | async-done | bytes 917536 | tf_op jit(solution)/shard_map/all_to_all | solution.py:119
  48.9 0.9 copy-done.2
  49.8 0.0 all-gather.2.cloned.1.call-update
  49.9 7.9 %all-to-all-start.2 = ((bf16[64,8,3584]{2,1,0:T(8,128)(2,1)}), bf16[64,8,3584]{2,1,0:T(8,128)(2,1)}, u32[]{:S(2)}, u32[]{:S(2)}) async-start(bf16[64,8,3584]{2,1,0:T(8,128)(2,1)} %bitcast.74), calls=%async_computation.2 | async-start | bytes 7340032 | tf_op jit(solution)/shard_map/all_to_all | solution.py:125
  57.8 0.0 reduce-scatter.7.cloned.1.call-start
  57.9 37.1 %all-gather.2.cloned.1.call-done = bf16[512,3584]{1,0:T(8,128)(2,1)} async-done(((bf16[512,896]{1,0:T(8,128)(2,1)}), bf16[512,3584]{1,0:T(8,128)(2,1)}) %all-gather.2.cloned.1.call-update) | async-done | bytes 3670032 | tf_op jit(solution)/shard_map/all_gather | solution.py:124
  94.9 3.9 %fusion.19 = f32[512,256]{1,0:T(8,128)S(1)} fusion(bf16[512,3584]{1,0:T(8,128)(2,1)} %all-gather.2.cloned.1.call-done, bf16[1,3584,256]{2,1,0:T(8,128)(2,1)} %param.17), kind=kOutput, calls=%fused_computation.33 | convolution fusion | flops 939524096 | bytes 6029312 | tf_op jit(solution)/shard_map/dot_general | solution.py:57
  98.8 0.0 copy-done
  98.8 0.0 copy-done.13
  98.8 0.0 copy-start.1
  98.8 2.0 multiply_convert_fusion.3
  100.9 0.0 copy-done.1
  100.9 2.9 %fusion.1 = bf16[3584,512]{0,1:T(8,128)(2,1)} fusion(bf16[512,256]{1,0:T(8,128)(2,1)S(1)} %get-tuple-element.15, bf16[1,256,3584]{2,1,0:T(8,128)(2,1)S(1)} %copy-done.1), kind=kOutput, calls=%fused_computation.6 | convolution fusion | flops 941359104 | bytes 5767168 | tf_op jit(solution)/shard_map/dot_general | solution.py:66
  103.8 5.9 %copy.46 = bf16[3584,512]{1,0:T(8,128)(2,1)} copy(bf16[3584,512]{0,1:T(8,128)(2,1)} %fusion.1) | data formatting | bytes 7340032
  109.7 0.0 reduce-scatter.7.cloned.1.call-update
  109.8 0.0 reduce-scatter.9.cloned.1.call-start
  109.8 30.6 %all-to-all-done.2 = bf16[64,8,3584]{2,1,0:T(8,128)(2,1)} async-done(((bf16[64,8,3584]{2,1,0:T(8,128)(2,1)}), bf16[64,8,3584]{2,1,0:T(8,128)(2,1)}, u32[]{:S(2)}, u32[]{:S(2)}) %all-to-all-start.2) | async-done | bytes 3670048 | tf_op jit(solution)/shard_map/all_to_all | solution.py:125
  140.4 4.1 %multiply_convert_fusion.1 = (bf16[512,256]{1,0:T(8,128)(2,1)S(1)}, bf16[512,256]{1,0:T(8,128)(2,1)S(1)}) fusion(f32[512,256]{1,0:T(8,128)S(1)} %get-tuple-element.20, f32[512,256]{1,0:T(8,128)S(1)} %fusion.19, f32[512,256]{1,0:T(8,128)} %get-tuple-element.18, f32[512,256]{1,0:T(8,128)} %get-tuple-element.17, bf16[1,256,3584]{2,1,0:T(8,128)(2,1)} %param.19, ...), kind=kOutput, calls=%fused_computation.38 | convolution fusion | flops 940703744 | bytes 8126464 | tf_op jit(solution)/shard_map/dot_general | solution.py:69
  144.6 0.0 copy-start.4
  144.6 0.0 copy-start.6
  144.6 0.0 copy-done.3
  144.6 1.1 fusion.17
  145.7 0.0 copy-done.4
  145.8 3.0 %fusion = bf16[3584,512]{0,1:T(8,128)(2,1)} fusion(f32[512,3584]{1,0:T(8,128)S(1)} %fusion.17, bf16[512,256]{1,0:T(8,128)(2,1)S(1)} %get-tuple-element.39, bf16[1,3584,256]{2,1,0:T(8,128)(2,1)S(1)} %copy-done), kind=kOutput, calls=%fused_computation.5 | convolution fusion | flops 943194112 | bytes 13107200 | tf_op jit(solution)/shard_map/dot_general | solution.py:76
  148.7 5.9 %copy.48 = bf16[3584,512]{1,0:T(8,128)(2,1)} copy(bf16[3584,512]{0,1:T(8,128)(2,1)} %fusion) | data formatting | bytes 7340032
  154.7 0.0 reduce-scatter.9.cloned.1.call-update
  154.7 0.6 reduce-scatter.7.cloned.1.call-done
  155.3 2.2 copy.47
  157.5 10.7 %all-to-all-start.1 = ((bf16[64,8,896]{2,1,0:T(8,128)(2,1)}), bf16[64,8,896]{2,1,0:T(8,128)(2,1)S(1)}, u32[]{:S(2)}, u32[]{:S(2)}) async-start(bf16[64,8,896]{2,1,0:T(8,128)(2,1)} %bitcast.77), calls=%async_computation.1 | async-start | bytes 1835008 | tf_op jit(solution)/shard_map/all_to_all | solution.py:134
  168.2 0.1 copy.43
  168.4 0.1 reshape.64
  168.4 0.6 fusion.25
  169.0 33.7 %reduce-scatter.9.cloned.1.call-done = bf16[896,512]{1,0:T(8,128)(2,1)} async-done(((bf16[3584,512]{1,0:T(8,128)(2,1)}), bf16[896,512]{1,0:T(8,128)(2,1)}) %reduce-scatter.9.cloned.1.call-update) | async-done | bytes 917520
  202.8 2.3 copy.49
  205.0 0.0 all-to-all-done.1
  205.0 10.9 %all-to-all-start.3 = ((bf16[64,8,896]{2,1,0:T(8,128)(2,1)}), bf16[64,8,896]{2,1,0:T(8,128)(2,1)}, u32[]{:S(2)}, u32[]{:S(2)}) async-start(bf16[64,8,896]{2,1,0:T(8,128)(2,1)} %bitcast.75), calls=%async_computation.3 | async-start | bytes 1835008 | tf_op jit(solution)/shard_map/all_to_all | solution.py:139
  216.0 0.6 compare_and_fusion
  216.6 0.1 copy.44
  216.7 0.1 copy.42
  216.8 1.0 dynamic-slice_convert_fusion
  217.8 0.0 copy-start.7
  217.8 4.6 %fusion.4 = bf16[1,256,3584]{2,1,0:T(8,128)(2,1)} fusion(bf16[512,256]{1,0:T(8,128)(2,1)S(1)} %get-tuple-element.15, bf16[64,8,3584]{2,1,0:T(8,128)(2,1)} %all-to-all-done.2), kind=kOutput, calls=%fused_computation.12 | convolution fusion | flops 940441600 | bytes 5767168 | tf_op jit(solution)/shard_map/dot_general | solution.py:84
  222.3 0.0 copy-done.14
  222.4 2.4 fusion.3
  224.8 2.4 fusion.2
  227.2 5.3 %gather_fusion = bf16[1024,896]{1,0:T(8,128)(2,1)} fusion(bf16[512,896]{1,0:T(8,128)(2,1)S(1)} %bitcast.73, s32[1024]{0:T(1024)S(1)} %copy-done.8), kind=kCustom, calls=%fused_computation.clone | custom fusion | bytes 3674112 | tf_op jit(solution)/shard_map/jit(_take)/gather | solution.py:145
  232.4 2.3 fusion.7
  234.7 0.1 reduce_sum.66
  234.8 9.2 %psum.7 = f32[128,8]{0,1:T(8,128)} all-reduce(f32[128,8]{0,1:T(8,128)S(1)} %broadcast_select_fusion.1), channel_id=1, replica_groups=mesh['expert'=64,'tensor'=4] {'tensor'}, use_global_device_ids=true, to_apply=%region_8.10 | all-reduce | flops 1024 | bytes 8192 | tf_op jit(solution)/shard_map/psum | solution.py:161
  244.0 0.0 all-to-all-done.3
  244.0 7.1 %gather_fusion.1 = bf16[1024,896]{1,0:T(8,128)(2,1)} fusion(bf16[512,896]{1,0:T(8,128)(2,1)} %bitcast.16, s32[1024]{0:T(1024)S(1)} %copy-done.8), kind=kCustom, calls=%fused_computation.1.clone | custom fusion | bytes 3674112 | tf_op jit(solution)/shard_map/jit(_take)/gather | solution.py:150
  251.1 5.0 %fusion.8 = (bf16[128,896]{1,0:T(8,128)(2,1)}, bf16[128,896]{1,0:T(8,128)(2,1)}) fusion(bf16[1024,896]{1,0:T(8,128)(2,1)} %gather_fusion.1, pred[1024]{0:T(1024)(128)(4,1)S(1)} %copy-done.12, pred[128,8]{1,0:T(8,128)(4,1)S(1)} %copy.44, bf16[1024,896]{1,0:T(8,128)(2,1)} %gather_fusion, f32[128,8]{1,0:T(8,128)S(1)} %copy.42), kind=kLoop, calls=%fused_computation.19 | loop fusion | flops 7110656 | bytes 4134912 | tf_op jit(solution)/shard_map/reduce_sum | solution.py:156
  (18 shorter events, 0.1 us)
Async XLA Ops:
  7.2 91.6 %copy-start = (bf16[1,3584,256]{2,1,0:T(8,128)(2,1)S(1)}, bf16[1,3584,256]{2,1,0:T(8,128)(2,1)}, u32[]{:S(2)}) copy-start(bf16[1,3584,256]{2,1,0:T(8,128)(2,1)} %param.18) | copy-start | bytes 5505028
  7.2 17.6 %copy-start.9 = (f32[128,8]{0,1:T(8,128)S(1)}, f32[128,8]{0,1:T(8,128)}, u32[]{:S(2)}) copy-start(f32[128,8]{0,1:T(8,128)} %param.15) | copy-start | bytes 12292
  8.9 207.7 %copy-start.10 = (pred[128,8]{0,1:T(8,128)(4,1)}, pred[128,8]{0,1:T(8,128)(4,1)S(1)}, u32[]{:S(2)}) copy-start(pred[128,8]{0,1:T(8,128)(4,1)S(1)} %get-tuple-element.36) | copy-start | bytes 3076
  12.6 36.3 %all-to-all-start = ((bf16[64,8,896]{2,1,0:T(8,128)(2,1)}), bf16[64,8,896]{2,1,0:T(8,128)(2,1)S(1)}, u32[]{:S(2)}, u32[]{:S(2)}) async-start(bf16[64,8,896]{2,1,0:T(8,128)(2,1)} %fusion.21), calls=%async_computation | async-start | bytes 1835008 | tf_op jit(solution)/shard_map/all_to_all | solution.py:119
  24.7 70.2 %all-gather.2.cloned.1.call-start = ((), (), s32[]{:S(2)}) async-start(), calls=%async_computation.6 | async-start | bytes 4587520 | tf_op jit(solution)/shard_map/all_gather | solution.py:124
  48.9 0.9 copy-start.2
  49.9 90.5 %all-to-all-start.2 = ((bf16[64,8,3584]{2,1,0:T(8,128)(2,1)}), bf16[64,8,3584]{2,1,0:T(8,128)(2,1)}, u32[]{:S(2)}, u32[]{:S(2)}) async-start(bf16[64,8,3584]{2,1,0:T(8,128)(2,1)} %bitcast.74), calls=%async_computation.2 | async-start | bytes 7340032 | tf_op jit(solution)/shard_map/all_to_all | solution.py:125
  57.8 97.5 %reduce-scatter.7.cloned.1.call-start = ((), (), s32[]{:S(2)}) async-start(), calls=%async_computation.7 | async-start | bytes 4587520
  94.9 3.9 %copy-start.13 = (bf16[512,3584]{1,0:T(8,128)(2,1)S(1)}, bf16[512,3584]{1,0:T(8,128)(2,1)}, u32[]{:S(2)}) copy-start(bf16[512,3584]{1,0:T(8,128)(2,1)} %all-gather.2.cloned.1.call-done) | copy-start | bytes 11010052
  98.8 2.0 copy-start.1
  109.8 93.0 %reduce-scatter.9.cloned.1.call-start = ((), (), s32[]{:S(2)}) async-start(), calls=%async_computation.8 | async-start | bytes 4587520
  140.4 4.2 %copy-start.3 = (bf16[1,3584,256]{2,1,0:T(8,128)(2,1)S(1)}, bf16[1,3584,256]{2,1,0:T(8,128)(2,1)}, u32[]{:S(2)}) copy-start(bf16[1,3584,256]{2,1,0:T(8,128)(2,1)} %param.17) | copy-start | bytes 5505028
  144.6 1.2 copy-start.4
  144.6 1.2 copy-start.6
  157.5 47.5 %all-to-all-start.1 = ((bf16[64,8,896]{2,1,0:T(8,128)(2,1)}), bf16[64,8,896]{2,1,0:T(8,128)(2,1)S(1)}, u32[]{:S(2)}, u32[]{:S(2)}) async-start(bf16[64,8,896]{2,1,0:T(8,128)(2,1)} %bitcast.77), calls=%async_computation.1 | async-start | bytes 1835008 | tf_op jit(solution)/shard_map/all_to_all | solution.py:134
  205.0 39.0 %all-to-all-start.3 = ((bf16[64,8,896]{2,1,0:T(8,128)(2,1)}), bf16[64,8,896]{2,1,0:T(8,128)(2,1)}, u32[]{:S(2)}, u32[]{:S(2)}) async-start(bf16[64,8,896]{2,1,0:T(8,128)(2,1)} %bitcast.75), calls=%async_computation.3 | async-start | bytes 1835008 | tf_op jit(solution)/shard_map/all_to_all | solution.py:139
  217.8 4.6 %copy-start.7 = (bf16[512,256]{1,0:T(8,128)(2,1)S(1)}, bf16[512,256]{1,0:T(8,128)(2,1)}, u32[]{:S(2)}) copy-start(bf16[512,256]{1,0:T(8,128)(2,1)} %copy-done.6) | copy-start | bytes 786436
  217.8 4.6 %copy-start.14 = (bf16[512,3584]{1,0:T(8,128)(2,1)S(1)}, bf16[512,3584]{1,0:T(8,128)(2,1)}, u32[]{:S(2)}) copy-start(bf16[512,3584]{1,0:T(8,128)(2,1)} %all-gather.2.cloned.1.call-done) | copy-start | bytes 11010052
  222.4 2.4 copy-start.5
  224.8 2.4 copy-start.8
  227.2 5.3 %copy-start.12 = (pred[1024]{0:T(1024)(128)(4,1)S(1)}, pred[1024]{0:T(1024)(128)(4,1)}, u32[]{:S(2)}) copy-start(pred[1024]{0:T(1024)(128)(4,1)} %compare_and_fusion) | copy-start | bytes 3076
  232.4 2.4 copy-start.11
Sparse Core Ops, SparseCore 0:
  50.0 44.9 all-gather.1
  109.9 45.3 reduce-scatter.6
  157.9 44.8 reduce-scatter.8

commit v5 on v4

--- a/solution.py
+++ b/solution.py
@@ -146,15 +146,12 @@
         .reshape(tok_rows, per_token, feature_share)
         .astype(jnp.float32)
     )
-    returned_rows = (
-        jnp.take(came_back, positions, axis=0)
-        .reshape(tok_rows, per_token, feature_share)
-        .astype(jnp.float32)
-    )
     gate_scaling = jnp.where(slot_alive_mask, routing_gate_weight, 0.0)
     mixed = jnp.sum(gate_scaling[:, :, None] * out_rows, axis=1).astype(jnp.bfloat16)
-    token_gradient = jnp.sum(
-        jnp.where(slot_alive_mask[:, :, None], returned_rows, 0.0), axis=1
+    route_hits = destination_slot[None, :, :] == jnp.arange(send_rows, dtype=jnp.int32)[:, None, None]
+    slot_of_token = jnp.sum(route_hits.astype(jnp.int32), axis=2).astype(jnp.bfloat16)
+    token_gradient = lax.dot_general(
+        slot_of_token, came_back, (((0,), (0,)), ((), ())), preferred_element_type=jnp.float32
     ).astype(jnp.bfloat16)
     local_cotangent = local_cotangent_bf.astype(jnp.float32)
     hidden_totals = jnp.sum(local_cotangent[:, None, :] * out_rows, axis=2)

time: 264 us -> 256 us (0.970)
  local copies, waits for them, and re-layouts: 30.3 us -> 24 us
    gather x1 -> x0, local copies, waits for them, and re-layouts: 7.08 us -> none  [local(): jnp.take(came_back, positions, axis=0)]
    unnamed x34 -> x28, local copies, waits for them, and re-layouts: 17.4 us -> 18 us
  transfers between devices with their start and end apart: 7 -> 7, of which waited for: 5 -> 5; matrix products, arithmetic and copies ran while one was open for 22% -> 24% of each run, Pallas kernels for 0% -> 0%
where the time goes in v5:
time: 256 us; the launch traced here: 255 us
  waiting for transfers between devices  119 us (46%)
  starting transfers between devices  41.9 us (16%)
  matrix products  35.2 us (14%)
  local copies, waits for them, and re-layouts  24 us (9%)
  between operations  14 us (5%)
  other arithmetic  11 us (4%)
  blocking collectives  9.19 us (4%)
    all_gather x1, waiting for transfers between devices, local(): rows_all = lax.all_gather(rows_q, 'tensor', axis=1, tiled=True)  37.1 us
    unnamed x5, waiting for transfers between devices  34.3 us
    all_to_all x1, waiting for transfers between devices, local(): lax.all_to_all(cot_rows.reshape(expert_number, expert_capacity, feature_w...  29.9 us
    all_to_all x1, waiting for transfers between devices, local(): lax.all_to_all(token_sum.reshape(expert_number, expert_capacity, feature_...  18.2 us
    unnamed x28, local copies, waits for them, and re-layouts  18 us
    all_to_all x1, starting transfers between devices, local(): lax.all_to_all(token_sum.reshape(expert_number, expert_capacity, feature_...  12.2 us
    all_to_all x1, starting transfers between devices, local(): lax.all_to_all(total_back.T.reshape(sources, expert_capacity, feature_sha...  10.9 us
    all_to_all x1, starting transfers between devices, local(): lax.all_to_all(total_out.T.reshape(sources, expert_capacity, feature_shar...  10.7 us
  transfers between devices with their start and end apart: 7, of which 5 were waited for; matrix products, arithmetic and copies ran while one was open for 24% of the time, Pallas kernels for 0%

profile of v5, /device:TPU:6, one launch (start us, length us, event | category | flops | bytes accessed | tf_op | source)
XLA Modules:
  0.0 254.7 jit_solution(14209831472190948849)
XLA Ops:
  7.2 0.0 copy-start
  7.2 0.9 select_reduce_fusion.1
  8.1 0.7 broadcast_compare_fusion
  8.8 0.7 convert_reduce_fusion
  9.6 2.3 fusion.18
  11.8 12.2 %all-to-all-start = ((bf16[64,8,896]{2,1,0:T(8,128)(2,1)}), bf16[64,8,896]{2,1,0:T(8,128)(2,1)S(1)}, u32[]{:S(2)}, u32[]{:S(2)}) async-start(bf16[64,8,896]{2,1,0:T(8,128)(2,1)} %fusion.18), calls=%async_computation | async-start | bytes 1835008 | tf_op jit(solution)/shard_map/all_to_all | solution.py:119
  24.0 0.0 all-gather.2.cloned.1.call-start
  24.1 1.7 select_reduce_fusion
  25.8 4.2 %multiply_convert_fusion = bf16[512,3584]{1,0:T(8,128)(2,1)} fusion(bf16[128,3584]{1,0:T(8,128)(2,1)} %param.10, f32[512]{0:T(512)S(1)} %select_reduce_fusion, s32[512,128]{1,0:T(8,128)S(1)} %convert_reduce_fusion), kind=kOutput, calls=%fused_computation.2 | convolution fusion | flops 473497600 | bytes 4851712 | tf_op jit(solution)/shard_map/dot_general | solution.py:25
  30.0 18.2 %all-to-all-done = bf16[64,8,896]{2,1,0:T(8,128)(2,1)S(1)} async-done(((bf16[64,8,896]{2,1,0:T(8,128)(2,1)}), bf16[64,8,896]{2,1,0:T(8,128)(2,1)S(1)}, u32[]{:S(2)}, u32[]{:S(2)}) %all-to-all-start) | async-done | bytes 917536 | tf_op jit(solution)/shard_map/all_to_all | solution.py:119
  48.2 0.9 copy-done.2
  49.1 0.0 all-gather.2.cloned.1.call-update
  49.1 7.9 %all-to-all-start.2 = ((bf16[64,8,3584]{2,1,0:T(8,128)(2,1)}), bf16[64,8,3584]{2,1,0:T(8,128)(2,1)}, u32[]{:S(2)}, u32[]{:S(2)}) async-start(bf16[64,8,3584]{2,1,0:T(8,128)(2,1)} %bitcast.74), calls=%async_computation.2 | async-start | bytes 7340032 | tf_op jit(solution)/shard_map/all_to_all | solution.py:125
  57.1 0.0 reduce-scatter.7.cloned.1.call-start
  57.1 37.1 %all-gather.2.cloned.1.call-done = bf16[512,3584]{1,0:T(8,128)(2,1)} async-done(((bf16[512,896]{1,0:T(8,128)(2,1)}), bf16[512,3584]{1,0:T(8,128)(2,1)}) %all-gather.2.cloned.1.call-update) | async-done | bytes 3670032 | tf_op jit(solution)/shard_map/all_gather | solution.py:124
  94.2 3.9 %fusion.16 = f32[512,256]{1,0:T(8,128)S(1)} fusion(bf16[512,3584]{1,0:T(8,128)(2,1)} %all-gather.2.cloned.1.call-done, bf16[1,3584,256]{2,1,0:T(8,128)(2,1)} %param.15), kind=kOutput, calls=%fused_computation.29 | convolution fusion | flops 939524096 | bytes 6029312 | tf_op jit(solution)/shard_map/dot_general | solution.py:57
  98.1 0.0 copy-done
  98.1 0.0 copy-done.10
  98.1 0.0 copy-start.1
  98.1 2.0 multiply_convert_fusion.3
  100.1 0.7 copy-done.4
  100.8 0.0 copy-done.1
  100.8 2.9 %fusion.1 = bf16[3584,512]{0,1:T(8,128)(2,1)} fusion(bf16[512,256]{1,0:T(8,128)(2,1)S(1)} %get-tuple-element.14, bf16[1,256,3584]{2,1,0:T(8,128)(2,1)S(1)} %copy-done.1), kind=kOutput, calls=%fused_computation.5 | convolution fusion | flops 941359104 | bytes 5767168 | tf_op jit(solution)/shard_map/dot_general | solution.py:66
  103.8 5.9 %copy.47 = bf16[3584,512]{1,0:T(8,128)(2,1)} copy(bf16[3584,512]{0,1:T(8,128)(2,1)} %fusion.1) | data formatting | bytes 7340032
  109.7 0.0 reduce-scatter.7.cloned.1.call-update
  109.7 0.0 reduce-scatter.9.cloned.1.call-start
  109.8 29.9 %all-to-all-done.2 = bf16[64,8,3584]{2,1,0:T(8,128)(2,1)} async-done(((bf16[64,8,3584]{2,1,0:T(8,128)(2,1)}), bf16[64,8,3584]{2,1,0:T(8,128)(2,1)}, u32[]{:S(2)}, u32[]{:S(2)}) %all-to-all-start.2) | async-done | bytes 3670048 | tf_op jit(solution)/shard_map/all_to_all | solution.py:125
  139.7 4.2 %multiply_convert_fusion.1 = (bf16[512,256]{1,0:T(8,128)(2,1)S(1)}, bf16[512,256]{1,0:T(8,128)(2,1)S(1)}) fusion(f32[512,256]{1,0:T(8,128)S(1)} %get-tuple-element.19, f32[512,256]{1,0:T(8,128)S(1)} %fusion.16, f32[512,256]{1,0:T(8,128)} %get-tuple-element.17, f32[512,256]{1,0:T(8,128)} %get-tuple-element.16, bf16[1,256,3584]{2,1,0:T(8,128)(2,1)} %param.17, ...), kind=kOutput, calls=%fused_computation.35 | convolution fusion | flops 940703744 | bytes 8126464 | tf_op jit(solution)/shard_map/dot_general | solution.py:69
  143.9 0.0 copy-start.5
  143.9 0.0 copy-start.7
  143.9 0.0 copy-done.3
  143.9 1.1 fusion.14
  145.1 0.0 copy-done.5
  145.1 0.0 copy-done.7
  145.1 3.0 %fusion = bf16[3584,512]{0,1:T(8,128)(2,1)} fusion(f32[512,3584]{1,0:T(8,128)S(1)} %fusion.14, bf16[512,256]{1,0:T(8,128)(2,1)S(1)} %get-tuple-element.35, bf16[1,3584,256]{2,1,0:T(8,128)(2,1)S(1)} %copy-done), kind=kOutput, calls=%fused_computation.4 | convolution fusion | flops 943194112 | bytes 13107200 | tf_op jit(solution)/shard_map/dot_general | solution.py:76
  148.1 6.0 %copy.49 = bf16[3584,512]{1,0:T(8,128)(2,1)} copy(bf16[3584,512]{0,1:T(8,128)(2,1)} %fusion) | data formatting | bytes 7340032
  154.0 0.0 reduce-scatter.9.cloned.1.call-update
  154.0 1.3 reduce-scatter.7.cloned.1.call-done
  155.3 2.2 copy.48
  157.5 10.7 %all-to-all-start.1 = ((bf16[64,8,896]{2,1,0:T(8,128)(2,1)}), bf16[64,8,896]{2,1,0:T(8,128)(2,1)S(1)}, u32[]{:S(2)}, u32[]{:S(2)}) async-start(bf16[64,8,896]{2,1,0:T(8,128)(2,1)} %bitcast.77), calls=%async_computation.1 | async-start | bytes 1835008 | tf_op jit(solution)/shard_map/all_to_all | solution.py:134
  168.2 0.1 copy.43
  168.4 0.1 broadcast_in_dim.64
  168.5 0.1 copy.44
  168.6 0.1 reshape.104
  168.7 1.1 dynamic-slice_convert_fusion
  169.8 33.0 %reduce-scatter.9.cloned.1.call-done = bf16[896,512]{1,0:T(8,128)(2,1)} async-done(((bf16[3584,512]{1,0:T(8,128)(2,1)}), bf16[896,512]{1,0:T(8,128)(2,1)}) %reduce-scatter.9.cloned.1.call-update) | async-done | bytes 917520
  202.8 2.2 copy.50
  205.0 0.0 all-to-all-done.1
  205.0 10.9 %all-to-all-start.3 = ((bf16[64,8,896]{2,1,0:T(8,128)(2,1)}), bf16[64,8,896]{2,1,0:T(8,128)(2,1)}, u32[]{:S(2)}, u32[]{:S(2)}) async-start(bf16[64,8,896]{2,1,0:T(8,128)(2,1)} %bitcast.75), calls=%async_computation.3 | async-start | bytes 1835008 | tf_op jit(solution)/shard_map/all_to_all | solution.py:139
  216.0 0.0 copy-start.8
  216.0 0.0 copy-start.11
  216.0 4.6 %fusion.4 = bf16[1,256,3584]{2,1,0:T(8,128)(2,1)} fusion(bf16[512,256]{1,0:T(8,128)(2,1)} %copy-done.4, bf16[64,8,3584]{2,1,0:T(8,128)(2,1)} %all-to-all-done.2), kind=kOutput, calls=%fused_computation.11 | convolution fusion | flops 940441600 | bytes 5767168 | tf_op jit(solution)/shard_map/dot_general | solution.py:84
  220.6 0.0 copy-done.8
  220.6 0.0 copy-done.11
  220.6 2.4 fusion.3
  223.0 2.4 fusion.2
  225.4 5.3 %gather_fusion = bf16[1024,896]{1,0:T(8,128)(2,1)} fusion(bf16[512,896]{1,0:T(8,128)(2,1)S(1)} %bitcast.73, s32[1024]{0:T(1024)S(1)} %broadcast_clamp_fusion), kind=kCustom, calls=%fused_computation | custom fusion | bytes 3674112 | tf_op jit(solution)/shard_map/jit(_take)/gather | solution.py:145
  230.7 2.2 fusion.5
  232.9 0.1 reduce_sum.60
  233.1 0.1 copy.42
  233.2 9.2 %psum.7 = f32[128,8]{0,1:T(8,128)} all-reduce(f32[128,8]{0,1:T(8,128)S(1)} %get-tuple-element.40), channel_id=1, replica_groups=mesh['expert'=64,'tensor'=4] {'tensor'}, use_global_device_ids=true, to_apply=%region_7.8 | all-reduce | flops 1024 | bytes 8192 | tf_op jit(solution)/shard_map/psum | solution.py:158
  242.4 3.5 %multiply_reduce_fusion = bf16[128,896]{1,0:T(8,128)(2,1)} fusion(bf16[1024,896]{1,0:T(8,128)(2,1)} %gather_fusion, f32[128,8]{1,0:T(8,128)S(1)} %copy.42, pred[128,8]{1,0:T(8,128)(4,1)S(1)} %copy.43), kind=kLoop, calls=%fused_computation.17 | loop fusion | flops 3555328 | bytes 2069504 | tf_op jit(solution)/shard_map/reduce_sum | solution.py:150
  245.9 0.0 all-to-all-done.3
  245.9 2.2 convolution_convert_fusion.5
  (13 shorter events, 0.1 us)
Async XLA Ops:
  7.2 90.9 %copy-start = (bf16[1,3584,256]{2,1,0:T(8,128)(2,1)S(1)}, bf16[1,3584,256]{2,1,0:T(8,128)(2,1)}, u32[]{:S(2)}) copy-start(bf16[1,3584,256]{2,1,0:T(8,128)(2,1)} %param.16) | copy-start | bytes 5505028
  11.8 36.3 %all-to-all-start = ((bf16[64,8,896]{2,1,0:T(8,128)(2,1)}), bf16[64,8,896]{2,1,0:T(8,128)(2,1)S(1)}, u32[]{:S(2)}, u32[]{:S(2)}) async-start(bf16[64,8,896]{2,1,0:T(8,128)(2,1)} %fusion.18), calls=%async_computation | async-start | bytes 1835008 | tf_op jit(solution)/shard_map/all_to_all | solution.py:119
  24.0 70.2 %all-gather.2.cloned.1.call-start = ((), (), s32[]{:S(2)}) async-start(), calls=%async_computation.6 | async-start | bytes 4587520 | tf_op jit(solution)/shard_map/all_gather | solution.py:124
  48.2 0.9 copy-start.2
  49.1 90.5 %all-to-all-start.2 = ((bf16[64,8,3584]{2,1,0:T(8,128)(2,1)}), bf16[64,8,3584]{2,1,0:T(8,128)(2,1)}, u32[]{:S(2)}, u32[]{:S(2)}) async-start(bf16[64,8,3584]{2,1,0:T(8,128)(2,1)} %bitcast.74), calls=%async_computation.2 | async-start | bytes 7340032 | tf_op jit(solution)/shard_map/all_to_all | solution.py:125
  57.1 98.2 %reduce-scatter.7.cloned.1.call-start = ((), (), s32[]{:S(2)}) async-start(), calls=%async_computation.7 | async-start | bytes 4587520
  94.2 3.9 %copy-start.10 = (bf16[512,3584]{1,0:T(8,128)(2,1)S(1)}, bf16[512,3584]{1,0:T(8,128)(2,1)}, u32[]{:S(2)}) copy-start(bf16[512,3584]{1,0:T(8,128)(2,1)} %all-gather.2.cloned.1.call-done) | copy-start | bytes 11010052
  98.1 2.8 %copy-start.1 = (bf16[1,256,3584]{2,1,0:T(8,128)(2,1)S(1)}, bf16[1,256,3584]{2,1,0:T(8,128)(2,1)}, u32[]{:S(2)}) copy-start(bf16[1,256,3584]{2,1,0:T(8,128)(2,1)} %param.17) | copy-start | bytes 5505028
  100.1 0.7 copy-start.4
  109.7 93.0 %reduce-scatter.9.cloned.1.call-start = ((), (), s32[]{:S(2)}) async-start(), calls=%async_computation.8 | async-start | bytes 4587520
  139.7 4.2 %copy-start.3 = (bf16[1,3584,256]{2,1,0:T(8,128)(2,1)S(1)}, bf16[1,3584,256]{2,1,0:T(8,128)(2,1)}, u32[]{:S(2)}) copy-start(bf16[1,3584,256]{2,1,0:T(8,128)(2,1)} %param.15) | copy-start | bytes 5505028
  143.9 1.2 copy-start.5
  143.9 1.2 copy-start.7
  157.5 47.5 %all-to-all-start.1 = ((bf16[64,8,896]{2,1,0:T(8,128)(2,1)}), bf16[64,8,896]{2,1,0:T(8,128)(2,1)S(1)}, u32[]{:S(2)}, u32[]{:S(2)}) async-start(bf16[64,8,896]{2,1,0:T(8,128)(2,1)} %bitcast.77), calls=%async_computation.1 | async-start | bytes 1835008 | tf_op jit(solution)/shard_map/all_to_all | solution.py:134
  205.0 40.9 %all-to-all-start.3 = ((bf16[64,8,896]{2,1,0:T(8,128)(2,1)}), bf16[64,8,896]{2,1,0:T(8,128)(2,1)}, u32[]{:S(2)}, u32[]{:S(2)}) async-start(bf16[64,8,896]{2,1,0:T(8,128)(2,1)} %bitcast.75), calls=%async_computation.3 | async-start | bytes 1835008 | tf_op jit(solution)/shard_map/all_to_all | solution.py:139
  216.0 4.7 %copy-start.8 = (bf16[512,256]{1,0:T(8,128)(2,1)S(1)}, bf16[512,256]{1,0:T(8,128)(2,1)}, u32[]{:S(2)}) copy-start(bf16[512,256]{1,0:T(8,128)(2,1)} %copy-done.7) | copy-start | bytes 786436
  216.0 4.7 %copy-start.11 = (bf16[512,3584]{1,0:T(8,128)(2,1)S(1)}, bf16[512,3584]{1,0:T(8,128)(2,1)}, u32[]{:S(2)}) copy-start(bf16[512,3584]{1,0:T(8,128)(2,1)} %all-gather.2.cloned.1.call-done) | copy-start | bytes 11010052
  220.6 2.4 copy-start.6
  225.4 7.6 %copy-start.9 = (f32[128,8]{0,1:T(8,128)S(1)}, f32[128,8]{0,1:T(8,128)}, u32[]{:S(2)}) copy-start(f32[128,8]{0,1:T(8,128)} %param.13) | copy-start | bytes 12292
Sparse Core Ops, SparseCore 0:
  49.2 44.9 all-gather.1
  109.8 45.4 reduce-scatter.6
  157.9 44.8 reduce-scatter.8

commit v6 on v5

--- a/solution.py
+++ b/solution.py
@@ -62,18 +62,22 @@
     pre_gate, pre_up, logistic, active, hidden = lax.optimization_barrier(
         (pre_gate, pre_up, logistic, active, hidden)
     )
-    contract_h = (((1,), (1,)), ((), ()))
-    out_t = lax.dot_general(
-        down_weight.T, hidden, contract_h, preferred_element_type=jnp.float32
+    n_tensor = lax.axis_size("tensor")
+    share = gate_weight.shape[0] // n_tensor
+    down_parts = down_weight.reshape(down_weight.shape[0], n_tensor, share)
+    out_t = jnp.einsum(
+        "mh,hkd->kmd", hidden, down_parts, preferred_element_type=jnp.float32
     ).astype(jnp.bfloat16)
     grad_hidden = jnp.dot(expert_cots, down_weight.T, preferred_element_type=jnp.float32)
     grad_pre_gate = (grad_hidden * pre_up * logistic * (1.0 + pre_gate * (1.0 - logistic))).astype(
         jnp.bfloat16
     )
     grad_pre_up = (grad_hidden * active).astype(jnp.bfloat16)
+    gate_parts = gate_weight.reshape(n_tensor, share, gate_weight.shape[1])
+    up_parts = up_weight.reshape(n_tensor, share, up_weight.shape[1])
     back_t = (
-        lax.dot_general(gate_weight, grad_pre_gate, contract_h, preferred_element_type=jnp.float32)
-        + lax.dot_general(up_weight, grad_pre_up, contract_h, preferred_element_type=jnp.float32)
+        jnp.einsum("mh,kdh->kmd", grad_pre_gate, gate_parts, preferred_element_type=jnp.float32)
+        + jnp.einsum("mh,kdh->kmd", grad_pre_up, up_parts, preferred_element_type=jnp.float32)
     ).astype(jnp.bfloat16)
     grad_gate_w = jnp.dot(expert_rows.T, grad_pre_gate, preferred_element_type=jnp.float32).astype(
         jnp.bfloat16
@@ -132,12 +136,12 @@
     total_out = lax.psum_scatter(out_t, "tensor", scatter_dimension=0, tiled=True)
     sources = total_out.shape[1] // expert_capacity
     came_out = lax.all_to_all(
-        total_out.T.reshape(sources, expert_capacity, feature_share),
+        total_out.reshape(sources, expert_capacity, feature_share),
         "expert", split_axis=0, concat_axis=0, tiled=True,
     ).reshape(send_rows, feature_share)
     total_back = lax.psum_scatter(back_t, "tensor", scatter_dimension=0, tiled=True)
     came_back = lax.all_to_all(
-        total_back.T.reshape(sources, expert_capacity, feature_share),
+        total_back.reshape(sources, expert_capacity, feature_share),
         "expert", split_axis=0, concat_axis=0, tiled=True,
     ).reshape(send_rows, feature_share)
     positions = jnp.maximum(destination_slot, 0).reshape(-1)

time: 256 us -> 247 us (0.965)
  local copies, waits for them, and re-layouts: 24 us -> 11.9 us
  waiting for transfers between devices: 119 us -> 124 us
    reduce_scatter x0 -> x2, waiting for transfers between devices: none -> 36.6 us  [the longest x1 35.3 us: local(): lax.psum_scatter(back_t, 'tensor', scatter_dimension=0, tiled=True)]
    unnamed x5 -> x3, waiting for transfers between devices: 34.3 us -> 0.05 us
    unnamed x28 -> x24, local copies, waits for them, and re-layouts: 18 us -> 1.68 us
    all_to_all x1, waiting for transfers between devices: 29.9 us -> 35.7 us  [local(): lax.all_to_all(cot_rows.reshape(expert_number, expert_capacity, feature_w...]
    all_gather x1, waiting for transfers between devices: 37.1 us -> 32.8 us  [local(): rows_all = lax.all_gather(rows_q, 'tensor', axis=1, tiled=True)]
    another operation x0 -> x1, local copies, waits for them, and re-layouts: none -> 4.26 us  [expert_group_t(): down_parts = down_weight.reshape(down_weight.shape[0], n_tensor, share)]
  transfers between devices with their start and end apart: 7 -> 7, of which waited for: 5 -> 5; matrix products, arithmetic and copies ran while one was open for 24% -> 20% of each run, Pallas kernels for 0% -> 0%
where the time goes in v6:
time: 247 us
  waiting for transfers between devices  124 us (50%)
  starting transfers between devices  41.9 us (17%)
  matrix products  35.5 us (14%)
  between operations  14 us (6%)
  local copies, waits for them, and re-layouts  11.9 us (5%)
  other arithmetic  10.2 us (4%)
  blocking collectives  9.16 us (4%)
    all_to_all x1, waiting for transfers between devices, local(): lax.all_to_all(cot_rows.reshape(expert_number, expert_capacity, feature_w...  35.7 us
    reduce_scatter x1, waiting for transfers between devices, local(): lax.psum_scatter(back_t, 'tensor', scatter_dimension=0, tiled=True)  35.3 us
    all_gather x1, waiting for transfers between devices, local(): rows_all = lax.all_gather(rows_q, 'tensor', axis=1, tiled=True)  32.8 us
    all_to_all x1, waiting for transfers between devices, local(): lax.all_to_all(token_sum.reshape(expert_number, expert_capacity, feature_...  18.9 us
    all_to_all x1, starting transfers between devices, local(): lax.all_to_all(token_sum.reshape(expert_number, expert_capacity, feature_...  12.2 us
    all_to_all x1, starting transfers between devices, local(): lax.all_to_all(total_back.reshape(sources, expert_capacity, feature_share...  10.9 us
    all_to_all x1, starting transfers between devices, local(): lax.all_to_all(total_out.reshape(sources, expert_capacity, feature_share)...  10.7 us
    psum x1, blocking collectives, local(): lax.psum(jnp.where(slot_alive_mask, hidden_totals, 0.0), 'tensor')  9.16 us
  transfers between devices with their start and end apart: 7, of which 5 were waited for; matrix products, arithmetic and copies ran while one was open for 20% of the time, Pallas kernels for 0%

profile of v6, /device:TPU:6, one launch (start us, length us, event | category | flops | bytes accessed | tf_op | source)
XLA Modules:
  0.0 246.5 jit_solution(5502937178036064327)
XLA Ops:
  7.2 0.0 copy-start
  7.2 0.0 copy-start.9
  7.2 0.9 select_reduce_fusion.1
  8.1 0.7 broadcast_compare_fusion
  8.9 0.7 convert_reduce_fusion
  9.6 2.3 fusion.14
  11.8 12.2 %all-to-all-start = ((bf16[64,8,896]{2,1,0:T(8,128)(2,1)}), bf16[64,8,896]{2,1,0:T(8,128)(2,1)S(1)}, u32[]{:S(2)}, u32[]{:S(2)}) async-start(bf16[64,8,896]{2,1,0:T(8,128)(2,1)} %fusion.14), calls=%async_computation | async-start | bytes 1835008 | tf_op jit(solution)/shard_map/all_to_all | solution.py:123
  24.0 0.0 all-gather.2.cloned.1.call-start
  24.1 0.0 copy-done.9
  24.1 1.0 select_reduce_fusion
  25.1 4.2 %multiply_convert_fusion = bf16[512,3584]{1,0:T(8,128)(2,1)} fusion(bf16[128,3584]{1,0:T(8,128)(2,1)} %param.10, f32[512]{0:T(512)S(1)} %select_reduce_fusion, s32[512,128]{1,0:T(8,128)S(1)} %convert_reduce_fusion), kind=kOutput, calls=%fused_computation.2 | convolution fusion | flops 473497600 | bytes 4851712 | tf_op jit(solution)/shard_map/dot_general | solution.py:25
  29.3 18.9 %all-to-all-done = bf16[64,8,896]{2,1,0:T(8,128)(2,1)S(1)} async-done(((bf16[64,8,896]{2,1,0:T(8,128)(2,1)}), bf16[64,8,896]{2,1,0:T(8,128)(2,1)S(1)}, u32[]{:S(2)}, u32[]{:S(2)}) %all-to-all-start) | async-done | bytes 917536 | tf_op jit(solution)/shard_map/all_to_all | solution.py:123
  48.2 0.9 copy-done.2
  49.1 0.0 all-gather.2.cloned.1.call-update
  49.1 7.9 %all-to-all-start.2 = ((bf16[64,8,3584]{2,1,0:T(8,128)(2,1)}), bf16[64,8,3584]{2,1,0:T(8,128)(2,1)}, u32[]{:S(2)}, u32[]{:S(2)}) async-start(bf16[64,8,3584]{2,1,0:T(8,128)(2,1)} %bitcast.73), calls=%async_computation.3 | async-start | bytes 7340032 | tf_op jit(solution)/shard_map/all_to_all | solution.py:129
  57.1 0.0 reduce-scatter.3.cloned.1.call-start
  57.1 4.3 %reshape_squeeze.9 = bf16[256,4,896]{2,1,0:T(4,128)(2,1)} reshape(bf16[1,256,3584]{2,1,0:T(8,128)(2,1)} %param.17) | data formatting | bytes 3670016 | tf_op jit(solution)/shard_map/reshape;squeeze | solution.py:67
  61.4 32.8 %all-gather.2.cloned.1.call-done = bf16[512,3584]{1,0:T(8,128)(2,1)} async-done(((bf16[512,896]{1,0:T(8,128)(2,1)}), bf16[512,3584]{1,0:T(8,128)(2,1)}) %all-gather.2.cloned.1.call-update) | async-done | bytes 3670032 | tf_op jit(solution)/shard_map/all_gather | solution.py:128
  94.2 3.9 %fusion.11 = f32[512,256]{1,0:T(8,128)S(1)} fusion(bf16[512,3584]{1,0:T(8,128)(2,1)} %all-gather.2.cloned.1.call-done, bf16[1,3584,256]{2,1,0:T(8,128)(2,1)} %param.15), kind=kOutput, calls=%fused_computation.24 | convolution fusion | flops 939524096 | bytes 6029312 | tf_op jit(solution)/shard_map/dot_general | solution.py:57
  98.1 0.0 copy-done
  98.1 0.0 copy-done.10
  98.1 0.0 copy-start.1
  98.1 2.0 multiply_convert_fusion.3
  100.1 0.7 copy-done.4
  100.8 0.0 copy-done.1
  100.8 3.0 %convert_bitcast_fusion = bf16[4,512,896]{2,1,0:T(8,128)(2,1)} fusion(bf16[256,4,896]{2,1,0:T(4,128)(2,1)S(1)} %copy-done.1, bf16[512,256]{1,0:T(8,128)(2,1)S(1)} %get-tuple-element.14), kind=kOutput, calls=%fused_computation.16 | convolution fusion | flops 941359104 | bytes 5767168 | tf_op jit(solution)/shard_map/mh,hkd->kmd/dot_general | solution.py:68
  103.9 0.0 reduce-scatter.3.cloned.1.call-update
  103.9 0.0 reduce-scatter.5.cloned.1.call-start
  104.0 35.7 %all-to-all-done.2 = bf16[64,8,3584]{2,1,0:T(8,128)(2,1)} async-done(((bf16[64,8,3584]{2,1,0:T(8,128)(2,1)}), bf16[64,8,3584]{2,1,0:T(8,128)(2,1)}, u32[]{:S(2)}, u32[]{:S(2)}) %all-to-all-start.2) | async-done | bytes 3670048 | tf_op jit(solution)/shard_map/all_to_all | solution.py:129
  139.7 4.2 %multiply_convert_fusion.1 = (bf16[512,256]{1,0:T(8,128)(2,1)S(1)}, bf16[512,256]{1,0:T(8,128)(2,1)S(1)}) fusion(f32[512,256]{1,0:T(8,128)S(1)} %get-tuple-element.19, f32[512,256]{1,0:T(8,128)S(1)} %fusion.11, f32[512,256]{1,0:T(8,128)} %get-tuple-element.17, f32[512,256]{1,0:T(8,128)} %get-tuple-element.16, bf16[1,256,3584]{2,1,0:T(8,128)(2,1)} %param.17, ...), kind=kOutput, calls=%fused_computation.31 | convolution fusion | flops 940703744 | bytes 8126464 | tf_op jit(solution)/shard_map/dot_general | solution.py:71
  143.8 0.0 copy-start.5
  143.8 0.0 copy-start.7
  143.9 0.0 copy-done.3
  143.9 1.1 fusion.17
  145.0 0.0 copy-done.5
  145.0 0.0 copy-done.7
  145.0 3.1 %fusion.3 = bf16[4,512,896]{2,1,0:T(8,128)(2,1)} fusion(f32[512,4,896]{2,0,1:T(8,128)S(1)} %fusion.17, bf16[4,896,256]{2,1,0:T(8,128)(2,1)S(1)} %bitcast.71, bf16[512,256]{1,0:T(8,128)(2,1)S(1)} %get-tuple-element.29), kind=kOutput, calls=%fused_computation.9 | convolution fusion | flops 943194112 | bytes 13107200 | tf_op jit(solution)/shard_map/mh,kdh->kmd/dot_general | solution.py:80
  148.2 0.0 reduce-scatter.5.cloned.1.call-update
  148.2 1.3 reduce-scatter.3.cloned.1.call-done
  149.5 10.7 %all-to-all-start.1 = ((bf16[64,8,896]{2,1,0:T(8,128)(2,1)}), bf16[64,8,896]{2,1,0:T(8,128)(2,1)S(1)}, u32[]{:S(2)}, u32[]{:S(2)}) async-start(bf16[64,8,896]{2,1,0:T(8,128)(2,1)} %bitcast.77), calls=%async_computation.2 | async-start | bytes 1835008 | tf_op jit(solution)/shard_map/all_to_all | solution.py:138
  160.2 0.1 copy.34
  160.3 0.1 broadcast_in_dim.64
  160.5 0.1 copy.36
  160.6 0.1 reshape.104
  160.7 1.0 dynamic-slice_convert_fusion
  161.7 35.3 %reduce-scatter.5.cloned.1.call-done = bf16[1,512,896]{2,1,0:T(8,128)(2,1)} async-done(((bf16[4,512,896]{2,1,0:T(8,128)(2,1)}), bf16[1,512,896]{2,1,0:T(8,128)(2,1)}) %reduce-scatter.5.cloned.1.call-update) | async-done | bytes 917520 | tf_op jit(solution)/shard_map/reduce_scatter | solution.py:142
  197.0 0.0 all-to-all-done.1
  197.0 10.9 %all-to-all-start.3 = ((bf16[64,8,896]{2,1,0:T(8,128)(2,1)}), bf16[64,8,896]{2,1,0:T(8,128)(2,1)}, u32[]{:S(2)}, u32[]{:S(2)}) async-start(bf16[64,8,896]{2,1,0:T(8,128)(2,1)} %bitcast.76), calls=%async_computation.5 | async-start | bytes 1835008 | tf_op jit(solution)/shard_map/all_to_all | solution.py:143
  207.9 0.0 copy-start.8
  207.9 0.0 copy-start.11
  207.9 4.6 %fusion.2 = bf16[1,256,3584]{2,1,0:T(8,128)(2,1)} fusion(bf16[512,256]{1,0:T(8,128)(2,1)} %copy-done.4, bf16[64,8,3584]{2,1,0:T(8,128)(2,1)} %all-to-all-done.2), kind=kOutput, calls=%fused_computation.8 | convolution fusion | flops 940441600 | bytes 5767168 | tf_op jit(solution)/shard_map/dot_general | solution.py:88
  212.5 0.0 copy-done.8
  212.5 0.0 copy-done.11
  212.5 2.4 fusion.1
  214.9 0.0 copy-done.6
  214.9 2.4 fusion
  217.3 5.3 %gather_fusion = bf16[1024,896]{1,0:T(8,128)(2,1)} fusion(bf16[512,896]{1,0:T(8,128)(2,1)S(1)} %bitcast.72, s32[1024]{0:T(1024)S(1)} %broadcast_clamp_fusion), kind=kCustom, calls=%fused_computation | custom fusion | bytes 3674112 | tf_op jit(solution)/shard_map/jit(_take)/gather | solution.py:149
  222.6 2.2 fusion.4
  224.8 0.1 reduce_sum.60
  225.0 0.1 copy.33
  225.1 9.2 %psum.7 = f32[128,8]{0,1:T(8,128)} all-reduce(f32[128,8]{0,1:T(8,128)S(1)} %get-tuple-element.34), channel_id=1, replica_groups=mesh['expert'=64,'tensor'=4] {'tensor'}, use_global_device_ids=true, to_apply=%region_7.8 | all-reduce | flops 1024 | bytes 8192 | tf_op jit(solution)/shard_map/psum | solution.py:162
  234.3 3.5 %multiply_reduce_fusion = bf16[128,896]{1,0:T(8,128)(2,1)} fusion(bf16[1024,896]{1,0:T(8,128)(2,1)} %gather_fusion, f32[128,8]{1,0:T(8,128)S(1)} %copy.33, pred[128,8]{1,0:T(8,128)(4,1)S(1)} %copy.34), kind=kLoop, calls=%fused_computation.15 | loop fusion | flops 3555328 | bytes 2069504 | tf_op jit(solution)/shard_map/reduce_sum | solution.py:154
  237.8 0.0 all-to-all-done.3
  237.8 2.2 convolution_convert_fusion.4
  (10 shorter events, 0.1 us)
Async XLA Ops:
  7.2 90.9 %copy-start = (bf16[1,3584,256]{2,1,0:T(8,128)(2,1)S(1)}, bf16[1,3584,256]{2,1,0:T(8,128)(2,1)}, u32[]{:S(2)}) copy-start(bf16[1,3584,256]{2,1,0:T(8,128)(2,1)} %param.16) | copy-start | bytes 5505028
  7.2 16.9 %copy-start.9 = (f32[128,8]{0,1:T(8,128)S(1)}, f32[128,8]{0,1:T(8,128)}, u32[]{:S(2)}) copy-start(f32[128,8]{0,1:T(8,128)} %param.13) | copy-start | bytes 12292
  11.8 36.3 %all-to-all-start = ((bf16[64,8,896]{2,1,0:T(8,128)(2,1)}), bf16[64,8,896]{2,1,0:T(8,128)(2,1)S(1)}, u32[]{:S(2)}, u32[]{:S(2)}) async-start(bf16[64,8,896]{2,1,0:T(8,128)(2,1)} %fusion.14), calls=%async_computation | async-start | bytes 1835008 | tf_op jit(solution)/shard_map/all_to_all | solution.py:123
  24.0 70.2 %all-gather.2.cloned.1.call-start = ((), (), s32[]{:S(2)}) async-start(), calls=%async_computation.6 | async-start | bytes 4587520 | tf_op jit(solution)/shard_map/all_gather | solution.py:128
  48.2 0.9 copy-start.2
  49.1 90.5 %all-to-all-start.2 = ((bf16[64,8,3584]{2,1,0:T(8,128)(2,1)}), bf16[64,8,3584]{2,1,0:T(8,128)(2,1)}, u32[]{:S(2)}, u32[]{:S(2)}) async-start(bf16[64,8,3584]{2,1,0:T(8,128)(2,1)} %bitcast.73), calls=%async_computation.3 | async-start | bytes 7340032 | tf_op jit(solution)/shard_map/all_to_all | solution.py:129
  57.1 92.4 %reduce-scatter.3.cloned.1.call-start = ((), (), s32[]{:S(2)}) async-start(), calls=%async_computation.7 | async-start | bytes 4587520 | tf_op jit(solution)/shard_map/reduce_scatter | solution.py:136
  94.2 3.9 %copy-start.10 = (bf16[512,3584]{1,0:T(8,128)(2,1)S(1)}, bf16[512,3584]{1,0:T(8,128)(2,1)}, u32[]{:S(2)}) copy-start(bf16[512,3584]{1,0:T(8,128)(2,1)} %all-gather.2.cloned.1.call-done) | copy-start | bytes 11010052
  98.1 2.7 %copy-start.1 = (bf16[256,4,896]{2,1,0:T(4,128)(2,1)S(1)}, bf16[256,4,896]{2,1,0:T(4,128)(2,1)}, u32[]{:S(2)}) copy-start(bf16[256,4,896]{2,1,0:T(4,128)(2,1)} %reshape_squeeze.9) | copy-start | bytes 5505028
  100.1 0.7 copy-start.4
  103.9 93.0 %reduce-scatter.5.cloned.1.call-start = ((), (), s32[]{:S(2)}) async-start(), calls=%async_computation.8 | async-start | bytes 4587520 | tf_op jit(solution)/shard_map/reduce_scatter | solution.py:142
  139.7 4.2 %copy-start.3 = (bf16[1,3584,256]{2,1,0:T(8,128)(2,1)S(1)}, bf16[1,3584,256]{2,1,0:T(8,128)(2,1)}, u32[]{:S(2)}) copy-start(bf16[1,3584,256]{2,1,0:T(8,128)(2,1)} %param.15) | copy-start | bytes 5505028
  143.8 1.2 copy-start.5
  143.8 1.2 copy-start.7
  149.5 47.5 %all-to-all-start.1 = ((bf16[64,8,896]{2,1,0:T(8,128)(2,1)}), bf16[64,8,896]{2,1,0:T(8,128)(2,1)S(1)}, u32[]{:S(2)}, u32[]{:S(2)}) async-start(bf16[64,8,896]{2,1,0:T(8,128)(2,1)} %bitcast.77), calls=%async_computation.2 | async-start | bytes 1835008 | tf_op jit(solution)/shard_map/all_to_all | solution.py:138
  197.0 40.8 %all-to-all-start.3 = ((bf16[64,8,896]{2,1,0:T(8,128)(2,1)}), bf16[64,8,896]{2,1,0:T(8,128)(2,1)}, u32[]{:S(2)}, u32[]{:S(2)}) async-start(bf16[64,8,896]{2,1,0:T(8,128)(2,1)} %bitcast.76), calls=%async_computation.5 | async-start | bytes 1835008 | tf_op jit(solution)/shard_map/all_to_all | solution.py:143
  207.9 4.7 %copy-start.8 = (bf16[512,256]{1,0:T(8,128)(2,1)S(1)}, bf16[512,256]{1,0:T(8,128)(2,1)}, u32[]{:S(2)}) copy-start(bf16[512,256]{1,0:T(8,128)(2,1)} %copy-done.7) | copy-start | bytes 786436
  207.9 4.7 %copy-start.11 = (bf16[512,3584]{1,0:T(8,128)(2,1)S(1)}, bf16[512,3584]{1,0:T(8,128)(2,1)}, u32[]{:S(2)}) copy-start(bf16[512,3584]{1,0:T(8,128)(2,1)} %all-gather.2.cloned.1.call-done) | copy-start | bytes 11010052
  212.5 2.4 copy-start.6
Sparse Core Ops, SparseCore 0:
  49.3 44.9 all-gather.1
  104.0 45.4 reduce-scatter.2
  152.0 44.8 reduce-scatter.4

commit v7 on v6

--- a/solution.py
+++ b/solution.py
@@ -73,12 +73,6 @@
         jnp.bfloat16
     )
     grad_pre_up = (grad_hidden * active).astype(jnp.bfloat16)
-    gate_parts = gate_weight.reshape(n_tensor, share, gate_weight.shape[1])
-    up_parts = up_weight.reshape(n_tensor, share, up_weight.shape[1])
-    back_t = (
-        jnp.einsum("mh,kdh->kmd", grad_pre_gate, gate_parts, preferred_element_type=jnp.float32)
-        + jnp.einsum("mh,kdh->kmd", grad_pre_up, up_parts, preferred_element_type=jnp.float32)
-    ).astype(jnp.bfloat16)
     grad_gate_w = jnp.dot(expert_rows.T, grad_pre_gate, preferred_element_type=jnp.float32).astype(
         jnp.bfloat16
     )
@@ -88,7 +82,7 @@
     grad_down_w = jnp.dot(hidden.T, expert_cots, preferred_element_type=jnp.float32).astype(
         jnp.bfloat16
     )
-    return (out_t, back_t, (grad_gate_w, grad_up_w, grad_down_w))
+    return (out_t, (grad_pre_gate, grad_pre_up), (grad_gate_w, grad_up_w, grad_down_w))
 
 
 def local(
@@ -112,6 +106,22 @@
     slot_alive_mask, destination_slot = routing_layout(
         chosen_experts, chosen_slots, padded_slot_count[0], expert_capacity
     )
+    n_tensor = lax.axis_size("tensor")
+    me = lax.axis_index("tensor")
+    weight_parts = jnp.stack(
+        [
+            w_gate[0].reshape(n_tensor, feature_share, w_gate.shape[2]),
+            w_up[0].reshape(n_tensor, feature_share, w_up.shape[2]),
+        ],
+        axis=1,
+    )
+    by_shift = [lax.dynamic_index_in_dim(weight_parts, me, 0, keepdims=False)]
+    for shift in range(1, n_tensor):
+        outgoing = lax.dynamic_index_in_dim(weight_parts, (me + shift) % n_tensor, 0, keepdims=False)
+        by_shift.append(
+            lax.ppermute(outgoing, "tensor", [(i, (i + shift) % n_tensor) for i in range(n_tensor)])
+        )
+    source_of_shift = (me - jnp.arange(n_tensor)) % n_tensor
     local_tokens = lax.dynamic_slice_in_dim(tokens, first_col, feature_share, 1)
     local_cotangent_bf = lax.dynamic_slice_in_dim(cotangent, first_col, feature_share, 1)
     token_sum, _ = pack_slots(
@@ -124,22 +134,32 @@
         token_sum.reshape(expert_number, expert_capacity, feature_share),
         "expert", split_axis=0, concat_axis=0, tiled=True,
     ).reshape(send_rows, feature_share)
-    rows_q, cot_rows = lax.optimization_barrier((rows_q, cot_rows))
+    rows_q, cot_rows, by_shift = lax.optimization_barrier((rows_q, cot_rows, by_shift))
+    swapped = jnp.stack(by_shift)
     rows_all = lax.all_gather(rows_q, "tensor", axis=1, tiled=True)
     cots_all = lax.all_to_all(
         cot_rows.reshape(expert_number, expert_capacity, feature_width),
         "expert", split_axis=0, concat_axis=0, tiled=True,
     ).reshape(send_rows, feature_width)
-    out_t, back_t, grads = expert_group_t(
+    out_t, grads_pre, grads = expert_group_t(
         rows_all, cots_all, w_gate[0], w_up[0], w_down[0]
     )
     total_out = lax.psum_scatter(out_t, "tensor", scatter_dimension=0, tiled=True)
+    total_out, grads_pre = lax.optimization_barrier((total_out, grads_pre))
     sources = total_out.shape[1] // expert_capacity
     came_out = lax.all_to_all(
         total_out.reshape(sources, expert_capacity, feature_share),
         "expert", split_axis=0, concat_axis=0, tiled=True,
     ).reshape(send_rows, feature_share)
-    total_back = lax.psum_scatter(back_t, "tensor", scatter_dimension=0, tiled=True)
+    grad_all = jnp.take(
+        lax.all_gather(jnp.stack(grads_pre), "tensor", axis=1, tiled=False),
+        source_of_shift,
+        axis=1,
+    )
+    total_back = (
+        jnp.einsum("kmh,kdh->md", grad_all[0], swapped[:, 0], preferred_element_type=jnp.float32)
+        + jnp.einsum("kmh,kdh->md", grad_all[1], swapped[:, 1], preferred_element_type=jnp.float32)
+    ).astype(jnp.bfloat16)
     came_back = lax.all_to_all(
         total_back.reshape(sources, expert_capacity, feature_share),
         "expert", split_axis=0, concat_axis=0, tiled=True,

time: 247 us -> 271 us (1.097)
  other arithmetic: 10.2 us -> 21.3 us
  starting transfers between devices: 41.9 us -> 49.8 us
  local copies, waits for them, and re-layouts: 11.9 us -> 17.9 us
  matrix products: 35.5 us -> 32.3 us
    ppermute x0 -> x3, waiting for transfers between devices: none -> 36.7 us  [local(): lax.ppermute(outgoing, 'tensor', [(i, (i + shift) % n_tensor) for i in ra...]
    reduce_scatter x1 -> x0, waiting for transfers between devices: 35.3 us -> none  [local(): lax.psum_scatter(back_t, 'tensor', scatter_dimension=0, tiled=True)]
    all_to_all x1, waiting for transfers between devices: 18.9 us -> 0.01 us  [local(): lax.all_to_all(token_sum.reshape(expert_number, expert_capacity, feature_...]
    all_gather x0 -> x1, waiting for transfers between devices: none -> 15.2 us  [local(): lax.all_gather(jnp.stack(grads_pre), 'tensor', axis=1, tiled=False)]
    ppermute x0 -> x3, starting transfers between devices: none -> 5.22 us  [local(): lax.ppermute(outgoing, 'tensor', [(i, (i + shift) % n_tensor) for i in ra...]
    all_to_all x1, waiting for transfers between devices: 35.7 us -> 40.5 us  [local(): lax.all_to_all(cot_rows.reshape(expert_number, expert_capacity, feature_w...]
    another operation x0 -> x2, other arithmetic: none -> 4.3 us  [the longest x1 3.46 us: local(): swapped = jnp.stack(by_shift)]
    gather x0 -> x1, local copies, waits for them, and re-layouts: none -> 3.69 us  [local(): jnp.take(lax.all_gather(jnp.stack(grads_pre), 'tensor', axis=1, tiled=Fal...]
  transfers between devices with their start and end apart: 7 -> 10, of which waited for: 5 -> 6; matrix products, arithmetic and copies ran while one was open for 20% -> 22% of each run, Pallas kernels for 0% -> 0%
where the time goes in v7:
time: 271 us; the launch traced here: 270 us
  waiting for transfers between devices  125 us (46%)
  starting transfers between devices  49.8 us (18%)
  matrix products  32.3 us (12%)
  other arithmetic  21.3 us (8%)
  local copies, waits for them, and re-layouts  17.9 us (7%)
  between operations  14 us (5%)
  blocking collectives  9.16 us (3%)
    all_to_all x1, waiting for transfers between devices, local(): lax.all_to_all(cot_rows.reshape(expert_number, expert_capacity, feature_w...  40.5 us
    ppermute x3, waiting for transfers between devices, local(): lax.ppermute(outgoing, 'tensor', [(i, (i + shift) % n_tensor) for i in ra...  36.7 us
    all_gather x1, waiting for transfers between devices, local(): rows_all = lax.all_gather(rows_q, 'tensor', axis=1, tiled=True)  31.8 us
    all_gather x1, waiting for transfers between devices, local(): lax.all_gather(jnp.stack(grads_pre), 'tensor', axis=1, tiled=False)  15.2 us
    all_to_all x1, starting transfers between devices, local(): lax.all_to_all(token_sum.reshape(expert_number, expert_capacity, feature_...  12.2 us
    all_to_all x1, starting transfers between devices, local(): lax.all_to_all(total_out.reshape(sources, expert_capacity, feature_share)...  10.9 us
    all_to_all x1, starting transfers between devices, local(): lax.all_to_all(total_back.reshape(sources, expert_capacity, feature_share...  10.9 us
    all_to_all x1, starting transfers between devices, local(): lax.all_to_all(cot_rows.reshape(expert_number, expert_capacity, feature_w...  10.5 us
  transfers between devices with their start and end apart: 10, of which 6 were waited for; matrix products, arithmetic and copies ran while one was open for 22% of the time, Pallas kernels for 0%

profile of v7, /device:TPU:6, one launch (start us, length us, event | category | flops | bytes accessed | tf_op | source)
XLA Modules:
  0.0 269.9 jit_solution(17209134542311615274)
XLA Ops:
  7.2 0.0 copy-start
  7.2 0.9 select_reduce_fusion.1
  8.1 1.3 broadcast_compare_fusion
  9.4 0.7 convert_reduce_fusion
  10.1 1.3 fusion.17
  11.4 12.2 %all-to-all-start = ((bf16[64,8,896]{2,1,0:T(8,128)(2,1)}), bf16[64,8,896]{2,1,0:T(8,128)(2,1)S(1)}, u32[]{:S(2)}, u32[]{:S(2)}) async-start(bf16[64,8,896]{2,1,0:T(8,128)(2,1)} %fusion.17), calls=%async_computation | async-start | bytes 1835008 | tf_op jit(solution)/shard_map/all_to_all | solution.py:133
  23.6 0.0 all-gather.4.cloned.1.call-start
  23.7 0.0 copy-start.17
  23.7 0.0 copy-start.7
  23.7 3.3 %fusion.20 = (bf16[2,896,256]{2,1,0:T(8,128)(2,1)S(1)}, bf16[2,896,256]{2,1,0:T(8,128)(2,1)}, bf16[2,896,256]{2,1,0:T(8,128)(2,1)S(1)}, bf16[2,896,256]{2,1,0:T(8,128)(2,1)S(1)}) fusion(s32[]{:T(128)S(6)} %select_n.119, bf16[4,1,896,256]{3,2,1,0:T(8,128)(2,1)} %bitcast.116, bf16[4,1,896,256]{3,2,1,0:T(8,128)(2,1)} %bitcast.117, s32[]{:T(128)S(6)} %select_n.113, ...), kind=kLoop, calls=%fused_computation.50 | loop fusion | flops 1835008 | bytes 7340048 | tf_op jit(solution)/shard_map/jit(dynamic_index_in_dim)/squeeze | solution.py:120
  27.0 3.0 %collective-permute-start.2 = (bf16[2,896,256]{2,1,0:T(8,128)(2,1)S(1)}, bf16[2,896,256]{2,1,0:T(8,128)(2,1)S(1)}, u32[]{:S(2)}, u32[]{:S(2)}) collective-permute-start(bf16[2,896,256]{2,1,0:T(8,128)(2,1)S(1)} %get-tuple-element.43), channel_id=1, source_target_pairs={{0,3},{1,0},{2,1},{3,2},{4,7},{5,4},{6,5},{7,6},{8,11},{9,8},{10,9... | collective-permute-start | bytes 2752520 | tf_op jit(solution)/shard_map/ppermute | solution.py:122
  30.0 0.0 collective-permute-start
  30.0 2.2 collective-permute-start.1
  32.2 1.0 select_reduce_fusion
  33.3 3.0 %multiply_convert_fusion = bf16[512,3584]{1,0:T(8,128)(2,1)} fusion(bf16[128,3584]{1,0:T(8,128)(2,1)S(1)} %copy-done.7, f32[512]{0:T(512)S(1)} %select_reduce_fusion, s32[512,128]{1,0:T(8,128)S(1)} %convert_reduce_fusion), kind=kOutput, calls=%fused_computation.2 | convolution fusion | flops 473497600 | bytes 4851712 | tf_op jit(solution)/shard_map/dot_general | solution.py:25
  36.3 33.3 %collective-permute-done.2 = bf16[2,896,256]{2,1,0:T(8,128)(2,1)S(1)} collective-permute-done((bf16[2,896,256]{2,1,0:T(8,128)(2,1)S(1)}, bf16[2,896,256]{2,1,0:T(8,128)(2,1)S(1)}, u32[]{:S(2)}, u32[]{:S(2)}) %collective-permute-start.2) | collective-permute-done | bytes 917536 | tf_op jit(solution)/shard_map/ppermute | solution.py:122
  69.6 3.4 %collective-permute-done = bf16[2,896,256]{2,1,0:T(8,128)(2,1)S(1)} collective-permute-done((bf16[2,896,256]{2,1,0:T(8,128)(2,1)S(1)}, bf16[2,896,256]{2,1,0:T(8,128)(2,1)S(1)}, u32[]{:S(2)}, u32[]{:S(2)}) %collective-permute-start) | collective-permute-done | bytes 917536 | tf_op jit(solution)/shard_map/ppermute | solution.py:122
  73.0 0.9 copy-done.15
  74.0 0.9 copy-done.4
  74.9 0.0 all-gather.4.cloned.1.call-update
  74.9 3.3 %reshape_squeeze.3 = bf16[256,4,896]{2,1,0:T(4,128)(2,1)S(1)} reshape(bf16[1,256,3584]{2,1,0:T(8,128)(2,1)} %param.17) | data formatting | bytes 3670016 | tf_op jit(solution)/shard_map/reshape;squeeze | solution.py:67
  78.2 10.5 %all-to-all-start.1 = ((bf16[64,8,3584]{2,1,0:T(8,128)(2,1)}), bf16[64,8,3584]{2,1,0:T(8,128)(2,1)}, u32[]{:S(2)}, u32[]{:S(2)}) async-start(bf16[64,8,3584]{2,1,0:T(8,128)(2,1)} %bitcast.112), calls=%async_computation.2 | async-start | bytes 7340032 | tf_op jit(solution)/shard_map/all_to_all | solution.py:140
  88.7 0.0 reduce-scatter.2.cloned.1.call-start
  88.8 31.8 %all-gather.4.cloned.1.call-done = bf16[512,3584]{1,0:T(8,128)(2,1)} async-done(((bf16[512,896]{1,0:T(8,128)(2,1)}), bf16[512,3584]{1,0:T(8,128)(2,1)}) %all-gather.4.cloned.1.call-update) | async-done | bytes 3670032 | tf_op jit(solution)/shard_map/all_gather | solution.py:139
  120.5 3.9 %fusion.14 = f32[512,256]{1,0:T(8,128)S(1)} fusion(bf16[512,3584]{1,0:T(8,128)(2,1)} %all-gather.4.cloned.1.call-done, bf16[1,3584,256]{2,1,0:T(8,128)(2,1)} %param.15), kind=kOutput, calls=%fused_computation.40 | convolution fusion | flops 939524096 | bytes 6029312 | tf_op jit(solution)/shard_map/dot_general | solution.py:57
  124.4 0.4 copy-done.22
  124.8 2.2 multiply_convert_fusion.3
  127.0 0.7 copy-done.8
  127.7 3.0 %convert_bitcast_fusion = bf16[4,512,896]{2,1,0:T(8,128)(2,1)} fusion(bf16[256,4,896]{2,1,0:T(4,128)(2,1)S(1)} %reshape_squeeze.3, bf16[512,256]{1,0:T(8,128)(2,1)S(1)} %get-tuple-element.21), kind=kOutput, calls=%fused_computation.24 | convolution fusion | flops 941359104 | bytes 5767168 | tf_op jit(solution)/shard_map/mh,hkd->kmd/dot_general | solution.py:68
  130.7 0.0 reduce-scatter.2.cloned.1.call-update
  130.7 0.0 all-gather.6.cloned.1.call-start
  130.8 40.5 %all-to-all-done.1 = bf16[64,8,3584]{2,1,0:T(8,128)(2,1)} async-done(((bf16[64,8,3584]{2,1,0:T(8,128)(2,1)}), bf16[64,8,3584]{2,1,0:T(8,128)(2,1)}, u32[]{:S(2)}, u32[]{:S(2)}) %all-to-all-start.1) | async-done | bytes 3670048 | tf_op jit(solution)/shard_map/all_to_all | solution.py:140
  171.3 3.8 %multiply_convert_fusion.1 = (bf16[512,256]{1,0:T(8,128)(2,1)S(1)}, bf16[512,256]{1,0:T(8,128)(2,1)S(1)}) fusion(f32[512,256]{1,0:T(8,128)} %get-tuple-element.26, f32[512,256]{1,0:T(8,128)} %copy-done.16, f32[512,256]{1,0:T(8,128)} %get-tuple-element.24, f32[512,256]{1,0:T(8,128)} %get-tuple-element.23, bf16[1,256,3584]{2,1,0:T(8,128)(2,1)S(1)} %copy-done.2, ...), kind=kOutput, calls=%fused_computation.59 | convolution fusion | flops 940703744 | bytes 8126464 | tf_op jit(solution)/shard_map/dot_general | solution.py:71
  175.1 1.2 reduce-scatter.2.cloned.1.call-done
  176.3 0.8 pad_maximum_fusion.1
  177.1 0.0 all-gather.6.cloned.1.call-update
  177.2 0.1 copy.43
  177.3 0.1 reshape.160
  177.4 0.6 pad_clamp_fusion
  178.0 0.6 compare_select_fusion
  178.6 10.9 %all-to-all-start.2 = ((bf16[64,8,896]{2,1,0:T(8,128)(2,1)}), bf16[64,8,896]{2,1,0:T(8,128)(2,1)S(1)}, u32[]{:S(2)}, u32[]{:S(2)}) async-start(bf16[64,8,896]{2,1,0:T(8,128)(2,1)} %bitcast.122), calls=%async_computation.3 | async-start | bytes 1835008 | tf_op jit(solution)/shard_map/all_to_all | solution.py:150
  189.5 0.5 compare_and_fusion.1
  190.0 0.8 copy.39
  190.8 0.7 broadcast_in_dim.76
  191.5 1.0 dynamic-slice_convert_fusion
  192.5 0.7 broadcast_clamp_fusion
  193.2 3.5 %pad_maximum_fusion = bf16[4,2,896,256]{3,2,0,1:T(8,128)(2,1)} fusion(bf16[1,2,896,256]{3,2,0,1:T(8,128)(2,1)} %bitcast.120, bf16[1,2,896,256]{3,2,0,1:T(8,128)(2,1)} %bitcast.30, bf16[1,2,896,256]{3,2,0,1:T(8,128)(2,1)} %bitcast.121, bf16[1,2,896,256]{3,2,0,1:T(8,128)(2,1)S(1)} %bitcast.114), kind=kLoop, calls=%fused_computation.17 | loop fusion | flops 5505024 | bytes 7340032 | tf_op jit(solution)/shard_map/stack | solution.py:138
  196.6 15.2 %all-gather.6.cloned.1.call-done = bf16[2,2048,256]{2,1,0:T(8,128)(2,1)} async-done(((bf16[2,512,256]{2,1,0:T(8,128)(2,1)}), bf16[2,2048,256]{2,1,0:T(8,128)(2,1)}) %all-gather.6.cloned.1.call-update) | async-done | bytes 2097168 | tf_op jit(solution)/shard_map/all_gather | solution.py:155
  211.8 3.7 %gather_fusion.1 = bf16[4,2,512,256]{3,2,1,0:T(8,128)(2,1)} fusion(bf16[2,4,512,256]{3,2,1,0:T(8,128)(2,1)} %bitcast.115, s32[1024]{0:T(1024)} %pad_clamp_fusion), kind=kCustom, calls=%fused_computation.1 | custom fusion | bytes 4194320 | tf_op jit(solution)/shard_map/jit(_take)/gather | solution.py:154
  215.5 2.0 fusion.7
  217.5 0.7 copy-done.3
  218.2 1.3 fusion.8
  219.5 2.3 fusion.18
  221.7 10.9 %all-to-all-start.3 = ((bf16[64,8,896]{2,1,0:T(8,128)(2,1)}), bf16[64,8,896]{2,1,0:T(8,128)(2,1)}, u32[]{:S(2)}, u32[]{:S(2)}) async-start(bf16[64,8,896]{2,1,0:T(8,128)(2,1)} %fusion.18), calls=%async_computation.4 | async-start | bytes 1835008 | tf_op jit(solution)/shard_map/all_to_all | solution.py:163
  232.7 4.6 %fusion.2 = bf16[1,256,3584]{2,1,0:T(8,128)(2,1)} fusion(bf16[512,256]{1,0:T(8,128)(2,1)S(1)} %copy-done.9, bf16[64,8,3584]{2,1,0:T(8,128)(2,1)} %all-to-all-done.1), kind=kOutput, calls=%fused_computation.16 | convolution fusion | flops 940441600 | bytes 5767168 | tf_op jit(solution)/shard_map/dot_general | solution.py:82
  237.2 2.4 fusion.1
  239.6 2.4 fusion
  242.1 5.3 %gather_fusion = bf16[1024,896]{1,0:T(8,128)(2,1)} fusion(bf16[512,896]{1,0:T(8,128)(2,1)S(1)} %bitcast.111, s32[1024]{0:T(1024)S(1)} %broadcast_clamp_fusion), kind=kCustom, calls=%fused_computation | custom fusion | bytes 3674112 | tf_op jit(solution)/shard_map/jit(_take)/gather | solution.py:169
  247.4 2.4 fusion.3
  249.8 0.1 reduce_sum.60
  249.9 0.1 copy.38
  250.0 9.2 %psum.7 = f32[128,8]{0,1:T(8,128)} all-reduce(f32[128,8]{0,1:T(8,128)S(1)} %get-tuple-element.52), channel_id=1, replica_groups=mesh['expert'=64,'tensor'=4] {'tensor'}, use_global_device_ids=true, to_apply=%region_6.7 | all-reduce | flops 1024 | bytes 8192 | tf_op jit(solution)/shard_map/psum | solution.py:182
  259.2 2.0 multiply_reduce_fusion
  261.2 2.2 convolution_convert_fusion.4
  (48 shorter events, 0.2 us)
Async XLA Ops:
  7.2 2.9 %copy-start = (bf16[128,3584]{1,0:T(8,128)(2,1)S(1)}, bf16[128,3584]{1,0:T(8,128)(2,1)}, u32[]{:S(2)}) copy-start(bf16[128,3584]{1,0:T(8,128)(2,1)} %param.9) | copy-start | bytes 2752516
  11.4 62.5 %all-to-all-start = ((bf16[64,8,896]{2,1,0:T(8,128)(2,1)}), bf16[64,8,896]{2,1,0:T(8,128)(2,1)S(1)}, u32[]{:S(2)}, u32[]{:S(2)}) async-start(bf16[64,8,896]{2,1,0:T(8,128)(2,1)} %fusion.17), calls=%async_computation | async-start | bytes 1835008 | tf_op jit(solution)/shard_map/all_to_all | solution.py:133
  23.6 97.0 %all-gather.4.cloned.1.call-start = ((), (), s32[]{:S(2)}) async-start(), calls=%async_computation.5 | async-start | bytes 4587520 | tf_op jit(solution)/shard_map/all_gather | solution.py:139
  23.7 8.6 %copy-start.17 = (f32[128,8]{0,1:T(8,128)S(1)}, f32[128,8]{0,1:T(8,128)}, u32[]{:S(2)}) copy-start(f32[128,8]{0,1:T(8,128)} %param.13) | copy-start | bytes 12292
  23.7 9.6 %copy-start.7 = (bf16[128,3584]{1,0:T(8,128)(2,1)S(1)}, bf16[128,3584]{1,0:T(8,128)(2,1)}, u32[]{:S(2)}) copy-start(bf16[128,3584]{1,0:T(8,128)(2,1)} %param.10) | copy-start | bytes 2752516
  27.0 42.6 %collective-permute-start.2 = (bf16[2,896,256]{2,1,0:T(8,128)(2,1)S(1)}, bf16[2,896,256]{2,1,0:T(8,128)(2,1)S(1)}, u32[]{:S(2)}, u32[]{:S(2)}) collective-permute-start(bf16[2,896,256]{2,1,0:T(8,128)(2,1)S(1)} %get-tuple-element.43), channel_id=1, source_target_pairs={{0,3},{1,0},{2,1},{3,2},{4,7},{5,4},{6,5},{7,6},{8,11},{9,8},{10,9... | collective-permute-start | bytes 2752520 | tf_op jit(solution)/shard_map/ppermute | solution.py:122
  30.0 43.0 %collective-permute-start = (bf16[2,896,256]{2,1,0:T(8,128)(2,1)S(1)}, bf16[2,896,256]{2,1,0:T(8,128)(2,1)S(1)}, u32[]{:S(2)}, u32[]{:S(2)}) collective-permute-start(bf16[2,896,256]{2,1,0:T(8,128)(2,1)S(1)} %get-tuple-element.45), channel_id=1, source_target_pairs={{0,1},{1,2},{2,3},{3,0},{4,5},{5,6},{6,7},{7,4},{8,9},{9,10},{10,1... | collective-permute-start | bytes 2752520 | tf_op jit(solution)/shard_map/ppermute | solution.py:122
  30.0 43.9 %collective-permute-start.1 = (bf16[2,896,256]{2,1,0:T(8,128)(2,1)S(1)}, bf16[2,896,256]{2,1,0:T(8,128)(2,1)}, u32[]{:S(2)}, u32[]{:S(2)}) collective-permute-start(bf16[2,896,256]{2,1,0:T(8,128)(2,1)S(1)} %get-tuple-element.46), channel_id=1, source_target_pairs={{0,2},{1,3},{2,0},{3,1},{4,6},{5,7},{6,4},{7,5},{8,10},{9,11},{10,... | collective-permute-start | bytes 2752520 | tf_op jit(solution)/shard_map/ppermute | solution.py:122
  69.6 3.4 %copy-start.14 = (bf16[2,896,256]{2,1,0:T(8,128)(2,1)}, bf16[2,896,256]{2,1,0:T(8,128)(2,1)S(1)}, u32[]{:S(2)}) copy-start(bf16[2,896,256]{2,1,0:T(8,128)(2,1)S(1)} %collective-permute-done.2) | copy-start | bytes 2752516
  73.0 0.9 copy-start.15
  74.0 0.9 copy-start.4
  78.2 93.1 %all-to-all-start.1 = ((bf16[64,8,3584]{2,1,0:T(8,128)(2,1)}), bf16[64,8,3584]{2,1,0:T(8,128)(2,1)}, u32[]{:S(2)}, u32[]{:S(2)}) async-start(bf16[64,8,3584]{2,1,0:T(8,128)(2,1)} %bitcast.112), calls=%async_computation.2 | async-start | bytes 7340032 | tf_op jit(solution)/shard_map/all_to_all | solution.py:140
  88.7 87.6 %reduce-scatter.2.cloned.1.call-start = ((), (), s32[]{:S(2)}) async-start(), calls=%async_computation.6 | async-start | bytes 4587520 | tf_op jit(solution)/shard_map/reduce_scatter | solution.py:147
  120.5 3.9 %copy-start.6 = (bf16[1,3584,256]{2,1,0:T(8,128)(2,1)S(1)}, bf16[1,3584,256]{2,1,0:T(8,128)(2,1)}, u32[]{:S(2)}) copy-start(bf16[1,3584,256]{2,1,0:T(8,128)(2,1)} %param.16) | copy-start | bytes 5505028
  120.5 4.2 %copy-start.22 = (bf16[512,3584]{1,0:T(8,128)(2,1)S(1)}, bf16[512,3584]{1,0:T(8,128)(2,1)}, u32[]{:S(2)}) copy-start(bf16[512,3584]{1,0:T(8,128)(2,1)} %all-gather.4.cloned.1.call-done) | copy-start | bytes 11010052
  124.8 2.2 copy-start.16
  127.0 0.7 copy-start.8
  130.7 40.6 %copy-start.2 = (bf16[1,256,3584]{2,1,0:T(8,128)(2,1)S(1)}, bf16[1,256,3584]{2,1,0:T(8,128)(2,1)}, u32[]{:S(2)}) copy-start(bf16[1,256,3584]{2,1,0:T(8,128)(2,1)} %param.17) | copy-start | bytes 5505028
  130.7 81.1 %all-gather.6.cloned.1.call-start = ((), (), s32[]{:S(2)}) async-start(), calls=%async_computation.7 | async-start | bytes 2621440 | tf_op jit(solution)/shard_map/all_gather | solution.py:155
  175.1 15.7 %copy-start.10 = (bf16[512,256]{1,0:T(8,128)(2,1)}, bf16[512,256]{1,0:T(8,128)(2,1)S(1)}, u32[]{:S(2)}) copy-start(bf16[512,256]{1,0:T(8,128)(2,1)S(1)} %get-tuple-element.28) | copy-start | bytes 786436
  175.1 15.7 %copy-start.12 = (bf16[512,256]{1,0:T(8,128)(2,1)}, bf16[512,256]{1,0:T(8,128)(2,1)S(1)}, u32[]{:S(2)}) copy-start(bf16[512,256]{1,0:T(8,128)(2,1)S(1)} %get-tuple-element.29) | copy-start | bytes 786436
  176.3 16.9 %copy-start.5 = (bf16[2,896,256]{2,1,0:T(8,128)(2,1)S(1)}, bf16[2,896,256]{2,1,0:T(8,128)(2,1)}, u32[]{:S(2)}) copy-start(bf16[2,896,256]{2,1,0:T(8,128)(2,1)} %get-tuple-element.30) | copy-start | bytes 2752516
  178.6 43.2 %all-to-all-start.2 = ((bf16[64,8,896]{2,1,0:T(8,128)(2,1)}), bf16[64,8,896]{2,1,0:T(8,128)(2,1)S(1)}, u32[]{:S(2)}, u32[]{:S(2)}) async-start(bf16[64,8,896]{2,1,0:T(8,128)(2,1)} %bitcast.122), calls=%async_computation.3 | async-start | bytes 1835008 | tf_op jit(solution)/shard_map/all_to_all | solution.py:150
  211.8 3.7 %copy-start.21 = (pred[4]{0:T(512)(128)(4,1)S(1)}, pred[4]{0:T(512)(128)(4,1)}, u32[]{:S(2)}) copy-start(pred[4]{0:T(512)(128)(4,1)} %compare_and_fusion.1) | copy-start | bytes 16
  215.5 2.7 copy-start.3
  219.4 13.2 %copy-start.9 = (bf16[512,256]{1,0:T(8,128)(2,1)S(1)}, bf16[512,256]{1,0:T(8,128)(2,1)}, u32[]{:S(2)}) copy-start(bf16[512,256]{1,0:T(8,128)(2,1)} %copy-done.8) | copy-start | bytes 786436
  221.7 39.5 %all-to-all-start.3 = ((bf16[64,8,896]{2,1,0:T(8,128)(2,1)}), bf16[64,8,896]{2,1,0:T(8,128)(2,1)}, u32[]{:S(2)}, u32[]{:S(2)}) async-start(bf16[64,8,896]{2,1,0:T(8,128)(2,1)} %fusion.18), calls=%async_computation.4 | async-start | bytes 1835008 | tf_op jit(solution)/shard_map/all_to_all | solution.py:163
  232.7 4.6 %copy-start.13 = (bf16[512,256]{1,0:T(8,128)(2,1)S(1)}, bf16[512,256]{1,0:T(8,128)(2,1)}, u32[]{:S(2)}) copy-start(bf16[512,256]{1,0:T(8,128)(2,1)} %copy-done.12) | copy-start | bytes 786436
  232.7 4.6 %copy-start.23 = (bf16[512,3584]{1,0:T(8,128)(2,1)S(1)}, bf16[512,3584]{1,0:T(8,128)(2,1)}, u32[]{:S(2)}) copy-start(bf16[512,3584]{1,0:T(8,128)(2,1)} %all-gather.4.cloned.1.call-done) | copy-start | bytes 11010052
  237.2 2.4 copy-start.11
  242.0 5.3 %copy-start.19 = (pred[1024]{0:T(1024)(128)(4,1)S(1)}, pred[1024]{0:T(1024)(128)(4,1)}, u32[]{:S(2)}) copy-start(pred[1024]{0:T(1024)(128)(4,1)} %broadcast_in_dim.76) | copy-start | bytes 3076
  247.4 2.5 copy-start.18
  247.4 2.5 copy-start.20
  247.4 11.8 %copy-start.1 = (bf16[1024,896]{1,0:T(8,128)(2,1)S(1)}, bf16[1024,896]{1,0:T(8,128)(2,1)}, u32[]{:S(2)}) copy-start(bf16[1024,896]{1,0:T(8,128)(2,1)} %gather_fusion) | copy-start | bytes 5505028
Sparse Core Ops, SparseCore 0:
  75.0 45.4 all-gather.3
  130.8 45.4 reduce-scatter.1
  178.7 33.0 all-gather.5

commit v8 on v6

--- a/solution.py
+++ b/solution.py
@@ -54,16 +54,18 @@
 
 
 def expert_group_t(expert_rows, expert_cots, gate_weight, up_weight, down_weight):
-    pre_gate = jnp.dot(expert_rows, gate_weight, preferred_element_type=jnp.float32)
-    pre_up = jnp.dot(expert_rows, up_weight, preferred_element_type=jnp.float32)
+    n_tensor = expert_rows.shape[0]
+    share = expert_rows.shape[2]
+    gate_parts = gate_weight.reshape(n_tensor, share, gate_weight.shape[1])
+    up_parts = up_weight.reshape(n_tensor, share, up_weight.shape[1])
+    pre_gate = jnp.einsum("kmd,kdh->mh", expert_rows, gate_parts, preferred_element_type=jnp.float32)
+    pre_up = jnp.einsum("kmd,kdh->mh", expert_rows, up_parts, preferred_element_type=jnp.float32)
     logistic = jax.nn.sigmoid(pre_gate)
     active = pre_gate * logistic
     hidden = (active * pre_up).astype(jnp.bfloat16)
     pre_gate, pre_up, logistic, active, hidden = lax.optimization_barrier(
         (pre_gate, pre_up, logistic, active, hidden)
     )
-    n_tensor = lax.axis_size("tensor")
-    share = gate_weight.shape[0] // n_tensor
     down_parts = down_weight.reshape(down_weight.shape[0], n_tensor, share)
     out_t = jnp.einsum(
         "mh,hkd->kmd", hidden, down_parts, preferred_element_type=jnp.float32
@@ -73,17 +75,19 @@
         jnp.bfloat16
     )
     grad_pre_up = (grad_hidden * active).astype(jnp.bfloat16)
-    gate_parts = gate_weight.reshape(n_tensor, share, gate_weight.shape[1])
-    up_parts = up_weight.reshape(n_tensor, share, up_weight.shape[1])
     back_t = (
         jnp.einsum("mh,kdh->kmd", grad_pre_gate, gate_parts, preferred_element_type=jnp.float32)
         + jnp.einsum("mh,kdh->kmd", grad_pre_up, up_parts, preferred_element_type=jnp.float32)
     ).astype(jnp.bfloat16)
-    grad_gate_w = jnp.dot(expert_rows.T, grad_pre_gate, preferred_element_type=jnp.float32).astype(
-        jnp.bfloat16
+    grad_gate_w = (
+        jnp.einsum("kmd,mh->kdh", expert_rows, grad_pre_gate, preferred_element_type=jnp.float32)
+        .astype(jnp.bfloat16)
+        .reshape(gate_weight.shape)
     )
-    grad_up_w = jnp.dot(expert_rows.T, grad_pre_up, preferred_element_type=jnp.float32).astype(
-        jnp.bfloat16
+    grad_up_w = (
+        jnp.einsum("kmd,mh->kdh", expert_rows, grad_pre_up, preferred_element_type=jnp.float32)
+        .astype(jnp.bfloat16)
+        .reshape(up_weight.shape)
     )
     grad_down_w = jnp.dot(hidden.T, expert_cots, preferred_element_type=jnp.float32).astype(
         jnp.bfloat16
@@ -125,7 +129,7 @@
         "expert", split_axis=0, concat_axis=0, tiled=True,
     ).reshape(send_rows, feature_share)
     rows_q, cot_rows = lax.optimization_barrier((rows_q, cot_rows))
-    rows_all = lax.all_gather(rows_q, "tensor", axis=1, tiled=True)
+    rows_all = lax.all_gather(rows_q, "tensor", axis=0, tiled=False)
     cots_all = lax.all_to_all(
         cot_rows.reshape(expert_number, expert_capacity, feature_width),
         "expert", split_axis=0, concat_axis=0, tiled=True,

time: 247 us -> 247 us (level)
  no operation moved by 1% of the time
where the time goes in v8:
time: 247 us
  waiting for transfers between devices  124 us (50%)
  starting transfers between devices  41.9 us (17%)
  matrix products  35.5 us (14%)
  between operations  14 us (6%)
  local copies, waits for them, and re-layouts  11.9 us (5%)
  other arithmetic  10.2 us (4%)
  blocking collectives  9.14 us (4%)
    all_to_all x1, waiting for transfers between devices, local(): lax.all_to_all(cot_rows.reshape(expert_number, expert_capacity, feature_w...  35.7 us
    reduce_scatter x1, waiting for transfers between devices, local(): lax.psum_scatter(back_t, 'tensor', scatter_dimension=0, tiled=True)  35.3 us
    all_gather x1, waiting for transfers between devices, local(): rows_all = lax.all_gather(rows_q, 'tensor', axis=0, tiled=False)  32.8 us
    all_to_all x1, waiting for transfers between devices, local(): lax.all_to_all(token_sum.reshape(expert_number, expert_capacity, feature_...  18.9 us
    all_to_all x1, starting transfers between devices, local(): lax.all_to_all(token_sum.reshape(expert_number, expert_capacity, feature_...  12.2 us
    all_to_all x1, starting transfers between devices, local(): lax.all_to_all(total_back.reshape(sources, expert_capacity, feature_share...  10.9 us
    all_to_all x1, starting transfers between devices, local(): lax.all_to_all(total_out.reshape(sources, expert_capacity, feature_share)...  10.7 us
    psum x1, blocking collectives, local(): lax.psum(jnp.where(slot_alive_mask, hidden_totals, 0.0), 'tensor')  9.14 us
  transfers between devices with their start and end apart: 7, of which 5 were waited for; matrix products, arithmetic and copies ran while one was open for 20% of the time, Pallas kernels for 0%

profile of v8, /device:TPU:6, one launch (start us, length us, event | category | flops | bytes accessed | tf_op | source)
XLA Modules:
  0.0 246.5 jit_solution(17991150893615313137)
XLA Ops:
  7.2 0.0 copy-start
  7.2 0.0 copy-start.9
  7.2 0.9 select_reduce_fusion.1
  8.1 0.7 broadcast_compare_fusion
  8.9 0.7 convert_reduce_fusion
  9.6 2.3 fusion.8
  11.8 12.2 %all-to-all-start = ((bf16[64,8,896]{2,1,0:T(8,128)(2,1)}), bf16[64,8,896]{2,1,0:T(8,128)(2,1)S(1)}, u32[]{:S(2)}, u32[]{:S(2)}) async-start(bf16[64,8,896]{2,1,0:T(8,128)(2,1)} %fusion.8), calls=%async_computation | async-start | bytes 1835008 | tf_op jit(solution)/shard_map/all_to_all | solution.py:127
  24.0 0.0 all-gather.3.cloned.1.call-start
  24.1 0.0 copy-done.9
  24.1 1.0 select_reduce_fusion
  25.1 4.2 %multiply_convert_fusion = bf16[512,3584]{1,0:T(8,128)(2,1)} fusion(bf16[128,3584]{1,0:T(8,128)(2,1)} %param.10, f32[512]{0:T(512)S(1)} %select_reduce_fusion, s32[512,128]{1,0:T(8,128)S(1)} %convert_reduce_fusion), kind=kOutput, calls=%fused_computation.2 | convolution fusion | flops 473497600 | bytes 4851712 | tf_op jit(solution)/shard_map/dot_general | solution.py:25
  29.3 18.9 %all-to-all-done = bf16[64,8,896]{2,1,0:T(8,128)(2,1)S(1)} async-done(((bf16[64,8,896]{2,1,0:T(8,128)(2,1)}), bf16[64,8,896]{2,1,0:T(8,128)(2,1)S(1)}, u32[]{:S(2)}, u32[]{:S(2)}) %all-to-all-start) | async-done | bytes 917536 | tf_op jit(solution)/shard_map/all_to_all | solution.py:127
  48.2 0.9 copy-done.2
  49.1 0.0 all-gather.3.cloned.1.call-update
  49.1 7.9 %all-to-all-start.2 = ((bf16[64,8,3584]{2,1,0:T(8,128)(2,1)}), bf16[64,8,3584]{2,1,0:T(8,128)(2,1)}, u32[]{:S(2)}, u32[]{:S(2)}) async-start(bf16[64,8,3584]{2,1,0:T(8,128)(2,1)} %bitcast.71), calls=%async_computation.3 | async-start | bytes 7340032 | tf_op jit(solution)/shard_map/all_to_all | solution.py:133
  57.1 0.0 reduce-scatter.3.cloned.1.call-start
  57.1 4.3 %reshape_squeeze.11 = bf16[256,4,896]{2,1,0:T(4,128)(2,1)} reshape(bf16[1,256,3584]{2,1,0:T(8,128)(2,1)} %param.17) | data formatting | bytes 3670016 | tf_op jit(solution)/shard_map/reshape;squeeze | solution.py:69
  61.4 32.8 %all-gather.3.cloned.1.call-done = bf16[2048,896]{1,0:T(8,128)(2,1)} async-done(((bf16[512,896]{1,0:T(8,128)(2,1)}), bf16[2048,896]{1,0:T(8,128)(2,1)}) %all-gather.3.cloned.1.call-update) | async-done | bytes 3670032 | tf_op jit(solution)/shard_map/all_gather | solution.py:132
  94.2 3.9 %convolution_bitcast_fusion.1 = f32[512,256]{1,0:T(8,128)S(1)} fusion(bf16[4,512,896]{2,1,0:T(8,128)(2,1)} %bitcast.79, bf16[4,896,256]{2,1,0:T(8,128)(2,1)} %bitcast.73), kind=kOutput, calls=%fused_computation.24 | convolution fusion | flops 939524096 | bytes 6029312 | tf_op jit(solution)/shard_map/kmd,kdh->mh/dot_general | solution.py:61
  98.1 0.0 copy-done
  98.1 0.0 copy-done.10
  98.1 0.0 copy-start.1
  98.1 2.0 multiply_convert_fusion.3
  100.2 0.7 copy-done.4
  100.9 0.0 copy-done.1
  100.9 3.0 %convert_bitcast_fusion = bf16[4,512,896]{2,1,0:T(8,128)(2,1)} fusion(bf16[256,4,896]{2,1,0:T(4,128)(2,1)S(1)} %copy-done.1, bf16[512,256]{1,0:T(8,128)(2,1)S(1)} %get-tuple-element.14), kind=kOutput, calls=%fused_computation.12 | convolution fusion | flops 941359104 | bytes 5767168 | tf_op jit(solution)/shard_map/mh,hkd->kmd/dot_general | solution.py:70
  103.9 0.0 reduce-scatter.3.cloned.1.call-update
  103.9 0.0 reduce-scatter.5.cloned.1.call-start
  104.0 35.7 %all-to-all-done.2 = bf16[64,8,3584]{2,1,0:T(8,128)(2,1)} async-done(((bf16[64,8,3584]{2,1,0:T(8,128)(2,1)}), bf16[64,8,3584]{2,1,0:T(8,128)(2,1)}, u32[]{:S(2)}, u32[]{:S(2)}) %all-to-all-start.2) | async-done | bytes 3670048 | tf_op jit(solution)/shard_map/all_to_all | solution.py:133
  139.7 4.1 %fusion.11 = (bf16[512,256,1]{1,0,2:T(8,128)(2,1)S(1)}, bf16[512,256,1]{1,0,2:T(8,128)(2,1)S(1)}) fusion(f32[512,256]{1,0:T(8,128)S(1)} %get-tuple-element.19, f32[512,256]{1,0:T(8,128)S(1)} %convolution_bitcast_fusion.1, f32[512,256]{1,0:T(8,128)} %get-tuple-element.17, f32[512,256]{1,0:T(8,128)} %get-tuple-element.16, bf16[1,256,3584]{2,1,0:T(8,128)(2,1)} %param.17, ...), kind=kOutput, calls=%fused_computation.32 | convolution fusion | flops 940703744 | bytes 8126464 | tf_op jit(solution)/shard_map/dot_general | solution.py:73
  143.8 0.0 copy-start.5
  143.8 0.0 copy-start.7
  143.9 0.0 copy-done.3
  143.9 1.1 fusion.23
  145.0 0.0 copy-done.5
  145.0 0.0 copy-done.7
  145.0 3.1 %fusion.1 = bf16[4,512,896]{2,1,0:T(8,128)(2,1)} fusion(f32[512,4,896]{2,0,1:T(8,128)S(1)} %fusion.23, bf16[512,256,1]{1,0,2:T(8,128)(2,1)S(1)} %get-tuple-element.29, bf16[4,896,256]{2,1,0:T(8,128)(2,1)S(1)} %bitcast.69), kind=kOutput, calls=%fused_computation.5 | convolution fusion | flops 943194112 | bytes 13107200 | tf_op jit(solution)/shard_map/mh,kdh->kmd/dot_general | solution.py:80
  148.2 0.0 reduce-scatter.5.cloned.1.call-update
  148.2 1.3 reduce-scatter.3.cloned.1.call-done
  149.5 10.7 %all-to-all-start.1 = ((bf16[64,8,896]{2,1,0:T(8,128)(2,1)}), bf16[64,8,896]{2,1,0:T(8,128)(2,1)S(1)}, u32[]{:S(2)}, u32[]{:S(2)}) async-start(bf16[64,8,896]{2,1,0:T(8,128)(2,1)} %bitcast.76), calls=%async_computation.2 | async-start | bytes 1835008 | tf_op jit(solution)/shard_map/all_to_all | solution.py:142
  160.2 0.1 copy.38
  160.4 0.1 broadcast_in_dim.58
  160.5 0.1 copy.40
  160.6 0.1 reshape.104
  160.7 1.0 dynamic-slice_convert_fusion
  161.7 35.3 %reduce-scatter.5.cloned.1.call-done = bf16[1,512,896]{2,1,0:T(8,128)(2,1)} async-done(((bf16[4,512,896]{2,1,0:T(8,128)(2,1)}), bf16[1,512,896]{2,1,0:T(8,128)(2,1)}) %reduce-scatter.5.cloned.1.call-update) | async-done | bytes 917520 | tf_op jit(solution)/shard_map/reduce_scatter | solution.py:146
  197.0 0.0 all-to-all-done.1
  197.0 10.9 %all-to-all-start.3 = ((bf16[64,8,896]{2,1,0:T(8,128)(2,1)}), bf16[64,8,896]{2,1,0:T(8,128)(2,1)}, u32[]{:S(2)}, u32[]{:S(2)}) async-start(bf16[64,8,896]{2,1,0:T(8,128)(2,1)} %bitcast.75), calls=%async_computation.5 | async-start | bytes 1835008 | tf_op jit(solution)/shard_map/all_to_all | solution.py:147
  207.9 0.0 copy-start.8
  207.9 0.0 copy-start.11
  207.9 4.6 %fusion = bf16[1,256,3584]{2,1,0:T(8,128)(2,1)} fusion(bf16[512,256]{1,0:T(8,128)(2,1)} %copy-done.4, bf16[64,8,3584]{2,1,0:T(8,128)(2,1)} %all-to-all-done.2), kind=kOutput, calls=%fused_computation.4 | convolution fusion | flops 940441600 | bytes 5767168 | tf_op jit(solution)/shard_map/dot_general | solution.py:92
  212.5 0.0 copy-done.8
  212.5 0.0 copy-done.11
  212.6 2.4 convolution_convert_fusion.1
  215.0 0.0 copy-done.6
  215.0 2.4 convolution_convert_fusion.2
  217.4 5.3 %gather_fusion = bf16[1024,896]{1,0:T(8,128)(2,1)} fusion(bf16[512,896]{1,0:T(8,128)(2,1)S(1)} %bitcast.70, s32[1024]{0:T(1024)S(1)} %broadcast_clamp_fusion), kind=kCustom, calls=%fused_computation | custom fusion | bytes 3674112 | tf_op jit(solution)/shard_map/jit(_take)/gather | solution.py:153
  222.6 2.2 fusion.2
  224.9 0.1 reduce_sum.60
  225.0 0.1 copy.37
  225.1 9.1 %psum.7 = f32[128,8]{0,1:T(8,128)} all-reduce(f32[128,8]{0,1:T(8,128)S(1)} %get-tuple-element.34), channel_id=1, replica_groups=mesh['expert'=64,'tensor'=4] {'tensor'}, use_global_device_ids=true, to_apply=%region_7.8 | all-reduce | flops 1024 | bytes 8192 | tf_op jit(solution)/shard_map/psum | solution.py:166
  234.3 3.5 %multiply_reduce_fusion = bf16[128,896]{1,0:T(8,128)(2,1)} fusion(bf16[1024,896]{1,0:T(8,128)(2,1)} %gather_fusion, f32[128,8]{1,0:T(8,128)S(1)} %copy.37, pred[128,8]{1,0:T(8,128)(4,1)S(1)} %copy.38), kind=kLoop, calls=%fused_computation.11 | loop fusion | flops 3555328 | bytes 2069504 | tf_op jit(solution)/shard_map/reduce_sum | solution.py:158
  237.8 0.0 all-to-all-done.3
  237.8 2.2 convolution_convert_fusion.4
  (10 shorter events, 0.1 us)
Async XLA Ops:
  7.2 90.9 %copy-start = (bf16[1,3584,256]{2,1,0:T(8,128)(2,1)S(1)}, bf16[1,3584,256]{2,1,0:T(8,128)(2,1)}, u32[]{:S(2)}) copy-start(bf16[1,3584,256]{2,1,0:T(8,128)(2,1)} %param.16) | copy-start | bytes 5505028
  7.2 16.9 %copy-start.9 = (f32[128,8]{0,1:T(8,128)S(1)}, f32[128,8]{0,1:T(8,128)}, u32[]{:S(2)}) copy-start(f32[128,8]{0,1:T(8,128)} %param.13) | copy-start | bytes 12292
  11.8 36.3 %all-to-all-start = ((bf16[64,8,896]{2,1,0:T(8,128)(2,1)}), bf16[64,8,896]{2,1,0:T(8,128)(2,1)S(1)}, u32[]{:S(2)}, u32[]{:S(2)}) async-start(bf16[64,8,896]{2,1,0:T(8,128)(2,1)} %fusion.8), calls=%async_computation | async-start | bytes 1835008 | tf_op jit(solution)/shard_map/all_to_all | solution.py:127
  24.0 70.2 %all-gather.3.cloned.1.call-start = ((), (), s32[]{:S(2)}) async-start(), calls=%async_computation.8 | async-start | bytes 4587520 | tf_op jit(solution)/shard_map/all_gather | solution.py:132
  48.2 0.9 copy-start.2
  49.1 90.5 %all-to-all-start.2 = ((bf16[64,8,3584]{2,1,0:T(8,128)(2,1)}), bf16[64,8,3584]{2,1,0:T(8,128)(2,1)}, u32[]{:S(2)}, u32[]{:S(2)}) async-start(bf16[64,8,3584]{2,1,0:T(8,128)(2,1)} %bitcast.71), calls=%async_computation.3 | async-start | bytes 7340032 | tf_op jit(solution)/shard_map/all_to_all | solution.py:133
  57.1 92.4 %reduce-scatter.3.cloned.1.call-start = ((), (), s32[]{:S(2)}) async-start(), calls=%async_computation.6 | async-start | bytes 4587520 | tf_op jit(solution)/shard_map/reduce_scatter | solution.py:140
  94.2 3.9 %copy-start.10 = (bf16[2048,896]{1,0:T(8,128)(2,1)S(1)}, bf16[2048,896]{1,0:T(8,128)(2,1)}, u32[]{:S(2)}) copy-start(bf16[2048,896]{1,0:T(8,128)(2,1)} %all-gather.3.cloned.1.call-done) | copy-start | bytes 11010052
  98.1 2.8 %copy-start.1 = (bf16[256,4,896]{2,1,0:T(4,128)(2,1)S(1)}, bf16[256,4,896]{2,1,0:T(4,128)(2,1)}, u32[]{:S(2)}) copy-start(bf16[256,4,896]{2,1,0:T(4,128)(2,1)} %reshape_squeeze.11) | copy-start | bytes 5505028
  100.1 0.7 copy-start.4
  103.9 93.0 %reduce-scatter.5.cloned.1.call-start = ((), (), s32[]{:S(2)}) async-start(), calls=%async_computation.7 | async-start | bytes 4587520 | tf_op jit(solution)/shard_map/reduce_scatter | solution.py:146
  139.7 4.2 %copy-start.3 = (bf16[1,3584,256]{2,1,0:T(8,128)(2,1)S(1)}, bf16[1,3584,256]{2,1,0:T(8,128)(2,1)}, u32[]{:S(2)}) copy-start(bf16[1,3584,256]{2,1,0:T(8,128)(2,1)} %param.15) | copy-start | bytes 5505028
  143.8 1.2 copy-start.5
  143.8 1.2 copy-start.7
  149.5 47.5 %all-to-all-start.1 = ((bf16[64,8,896]{2,1,0:T(8,128)(2,1)}), bf16[64,8,896]{2,1,0:T(8,128)(2,1)S(1)}, u32[]{:S(2)}, u32[]{:S(2)}) async-start(bf16[64,8,896]{2,1,0:T(8,128)(2,1)} %bitcast.76), calls=%async_computation.2 | async-start | bytes 1835008 | tf_op jit(solution)/shard_map/all_to_all | solution.py:142
  197.0 40.8 %all-to-all-start.3 = ((bf16[64,8,896]{2,1,0:T(8,128)(2,1)}), bf16[64,8,896]{2,1,0:T(8,128)(2,1)}, u32[]{:S(2)}, u32[]{:S(2)}) async-start(bf16[64,8,896]{2,1,0:T(8,128)(2,1)} %bitcast.75), calls=%async_computation.5 | async-start | bytes 1835008 | tf_op jit(solution)/shard_map/all_to_all | solution.py:147
  207.9 4.7 %copy-start.8 = (bf16[512,256,1]{1,0,2:T(8,128)(2,1)S(1)}, bf16[512,256,1]{1,0,2:T(8,128)(2,1)}, u32[]{:S(2)}) copy-start(bf16[512,256,1]{1,0,2:T(8,128)(2,1)} %copy-done.7) | copy-start | bytes 786436
  207.9 4.7 %copy-start.11 = (bf16[2048,896]{1,0:T(8,128)(2,1)S(1)}, bf16[2048,896]{1,0:T(8,128)(2,1)}, u32[]{:S(2)}) copy-start(bf16[2048,896]{1,0:T(8,128)(2,1)} %all-gather.3.cloned.1.call-done) | copy-start | bytes 11010052
  212.5 2.4 copy-start.6
Sparse Core Ops, SparseCore 0:
  49.3 44.9 all-gather.2
  104.0 45.4 reduce-scatter.2
  152.1 44.8 reduce-scatter.4

commit v9 on v6

--- a/solution.py
+++ b/solution.py
@@ -134,12 +134,24 @@
         rows_all, cots_all, w_gate[0], w_up[0], w_down[0]
     )
     total_out = lax.psum_scatter(out_t, "tensor", scatter_dimension=0, tiled=True)
+    total_out, back_t = lax.optimization_barrier((total_out, back_t))
     sources = total_out.shape[1] // expert_capacity
     came_out = lax.all_to_all(
         total_out.reshape(sources, expert_capacity, feature_share),
         "expert", split_axis=0, concat_axis=0, tiled=True,
     ).reshape(send_rows, feature_share)
-    total_back = lax.psum_scatter(back_t, "tensor", scatter_dimension=0, tiled=True)
+    ring_cols = 4 * 128
+    sc_part = lax.psum_scatter(back_t[:, :, ring_cols:], "tensor", scatter_dimension=0, tiled=True)
+    ring_in = back_t[:, :, :ring_cols]
+    n_tensor = ring_in.shape[0]
+    me = lax.axis_index("tensor")
+    reverse = [(i, (i - 1) % n_tensor) for i in range(n_tensor)]
+    acc = lax.dynamic_index_in_dim(ring_in, (me + 1) % n_tensor, 0, keepdims=False)
+    for step in range(1, n_tensor):
+        moved = lax.ppermute(acc, "tensor", reverse)
+        mine = lax.dynamic_index_in_dim(ring_in, (me + 1 + step) % n_tensor, 0, keepdims=False)
+        acc = (moved.astype(jnp.float32) + mine.astype(jnp.float32)).astype(jnp.bfloat16)
+    total_back = jnp.concatenate([acc, sc_part[0]], axis=1)
     came_back = lax.all_to_all(
         total_back.reshape(sources, expert_capacity, feature_share),
         "expert", split_axis=0, concat_axis=0, tiled=True,

time: 247 us -> 264 us (1.069)
  local copies, waits for them, and re-layouts: 11.9 us -> 21.7 us
  other arithmetic: 10.2 us -> 19.3 us
  waiting for transfers between devices: 124 us -> 116 us
  starting transfers between devices: 41.9 us -> 44.9 us
    reduce_scatter x1, waiting for transfers between devices: 35.3 us -> 0.02 us  [local(): lax.psum_scatter(back_t[:, :, ring_cols:], 'tensor', scatter_dimension=0,...]
    ppermute x0 -> x3, waiting for transfers between devices: none -> 27.3 us  [local(): moved = lax.ppermute(acc, 'tensor', reverse)]
    ppermute x0 -> x3, starting transfers between devices: none -> 6.66 us  [local(): moved = lax.ppermute(acc, 'tensor', reverse)]
    slice x0 -> x2, local copies, waits for them, and re-layouts: none -> 4.43 us  [the longest x1 2.71 us: local(): back_t[:, :, ring_cols:]]
    concatenate x0 -> x2, other arithmetic: none -> 3.22 us  [local(): total_back = jnp.concatenate([acc, sc_part[0]], axis=1)]
    all_to_all x1, starting transfers between devices: 10.9 us -> 8.12 us  [local(): lax.all_to_all(total_back.reshape(sources, expert_capacity, feature_share...]
    convert_element_type x0 -> x2, other arithmetic: none -> 2.67 us  [local(): (moved.astype(jnp.float32) + mine.astype(jnp.float32)).astype(jnp.bfloat16)]
  transfers between devices with their start and end apart: 7 -> 10, of which waited for: 5 -> 7; matrix products, arithmetic and copies ran while one was open for 20% -> 24% of each run, Pallas kernels for 0% -> 0%
where the time goes in v9:
time: 264 us; the launch traced here: 263 us
  waiting for transfers between devices  116 us (44%)
  starting transfers between devices  44.9 us (17%)
  matrix products  35.4 us (13%)
  local copies, waits for them, and re-layouts  21.7 us (8%)
  other arithmetic  19.3 us (7%)
  between operations  14 us (5%)
  blocking collectives  11.6 us (4%)
    all_to_all x1, waiting for transfers between devices, local(): lax.all_to_all(cot_rows.reshape(expert_number, expert_capacity, feature_w...  35.7 us
    all_gather x1, waiting for transfers between devices, local(): rows_all = lax.all_gather(rows_q, 'tensor', axis=1, tiled=True)  32.8 us
    ppermute x3, waiting for transfers between devices, local(): moved = lax.ppermute(acc, 'tensor', reverse)  27.3 us
    all_to_all x1, waiting for transfers between devices, local(): lax.all_to_all(token_sum.reshape(expert_number, expert_capacity, feature_...  18.9 us
    all_to_all x1, starting transfers between devices, local(): lax.all_to_all(token_sum.reshape(expert_number, expert_capacity, feature_...  12.2 us
    psum x1, blocking collectives, local(): lax.psum(jnp.where(slot_alive_mask, hidden_totals, 0.0), 'tensor')  11.6 us
    all_to_all x1, starting transfers between devices, local(): lax.all_to_all(total_out.reshape(sources, expert_capacity, feature_share)...  9.89 us
    all_to_all x1, starting transfers between devices, local(): lax.all_to_all(total_back.reshape(sources, expert_capacity, feature_share...  8.12 us
  transfers between devices with their start and end apart: 10, of which 7 were waited for; matrix products, arithmetic and copies ran while one was open for 24% of the time, Pallas kernels for 0%

profile of v9, /device:TPU:6, one launch (start us, length us, event | category | flops | bytes accessed | tf_op | source)
XLA Modules:
  0.0 263.0 jit_solution(2098012738741600959)
XLA Ops:
  7.2 0.0 copy-start
  7.2 0.0 copy-start.13
  7.2 0.9 select_reduce_fusion.1
  8.1 1.3 broadcast_compare_fusion
  9.4 0.7 convert_reduce_fusion
  10.1 2.3 fusion.14
  12.4 12.2 %all-to-all-start = ((bf16[64,8,896]{2,1,0:T(8,128)(2,1)}), bf16[64,8,896]{2,1,0:T(8,128)(2,1)S(1)}, u32[]{:S(2)}, u32[]{:S(2)}) async-start(bf16[64,8,896]{2,1,0:T(8,128)(2,1)} %fusion.14), calls=%async_computation | async-start | bytes 1835008 | tf_op jit(solution)/shard_map/all_to_all | solution.py:123
  24.6 0.0 all-gather.2.cloned.1.call-start
  24.6 1.0 select_reduce_fusion
  25.7 4.2 %multiply_convert_fusion = bf16[512,3584]{1,0:T(8,128)(2,1)} fusion(bf16[128,3584]{1,0:T(8,128)(2,1)} %param.10, f32[512]{0:T(512)S(1)} %select_reduce_fusion, s32[512,128]{1,0:T(8,128)S(1)} %convert_reduce_fusion), kind=kOutput, calls=%fused_computation.2 | convolution fusion | flops 473497600 | bytes 4851712 | tf_op jit(solution)/shard_map/dot_general | solution.py:25
  29.9 18.9 %all-to-all-done = bf16[64,8,896]{2,1,0:T(8,128)(2,1)S(1)} async-done(((bf16[64,8,896]{2,1,0:T(8,128)(2,1)}), bf16[64,8,896]{2,1,0:T(8,128)(2,1)S(1)}, u32[]{:S(2)}, u32[]{:S(2)}) %all-to-all-start) | async-done | bytes 917536 | tf_op jit(solution)/shard_map/all_to_all | solution.py:123
  48.8 0.9 copy-done.3
  49.7 0.0 all-gather.2.cloned.1.call-update
  49.7 7.9 %all-to-all-start.1 = ((bf16[64,8,3584]{2,1,0:T(8,128)(2,1)}), bf16[64,8,3584]{2,1,0:T(8,128)(2,1)}, u32[]{:S(2)}, u32[]{:S(2)}) async-start(bf16[64,8,3584]{2,1,0:T(8,128)(2,1)} %bitcast.86), calls=%async_computation.2 | async-start | bytes 7340032 | tf_op jit(solution)/shard_map/all_to_all | solution.py:129
  57.7 0.0 reduce-scatter.3.cloned.1.call-start
  57.7 4.3 %reshape_squeeze.9 = bf16[256,4,896]{2,1,0:T(4,128)(2,1)} reshape(bf16[1,256,3584]{2,1,0:T(8,128)(2,1)} %param.17) | data formatting | bytes 3670016 | tf_op jit(solution)/shard_map/reshape;squeeze | solution.py:67
  62.0 32.8 %all-gather.2.cloned.1.call-done = bf16[512,3584]{1,0:T(8,128)(2,1)} async-done(((bf16[512,896]{1,0:T(8,128)(2,1)}), bf16[512,3584]{1,0:T(8,128)(2,1)}) %all-gather.2.cloned.1.call-update) | async-done | bytes 3670032 | tf_op jit(solution)/shard_map/all_gather | solution.py:128
  94.8 3.9 %fusion.11 = f32[512,256]{1,0:T(8,128)S(1)} fusion(bf16[512,3584]{1,0:T(8,128)(2,1)} %all-gather.2.cloned.1.call-done, bf16[1,3584,256]{2,1,0:T(8,128)(2,1)} %param.15), kind=kOutput, calls=%fused_computation.24 | convolution fusion | flops 939524096 | bytes 6029312 | tf_op jit(solution)/shard_map/dot_general | solution.py:57
  98.7 2.0 multiply_convert_fusion.3
  100.7 0.7 copy-done.6
  101.4 3.0 %convert_bitcast_fusion = bf16[4,512,896]{2,1,0:T(8,128)(2,1)} fusion(bf16[256,4,896]{2,1,0:T(4,128)(2,1)S(1)} %copy-done.2, bf16[512,256]{1,0:T(8,128)(2,1)S(1)} %get-tuple-element.16), kind=kOutput, calls=%fused_computation.16 | convolution fusion | flops 941359104 | bytes 5767168 | tf_op jit(solution)/shard_map/mh,hkd->kmd/dot_general | solution.py:68
  104.5 0.0 reduce-scatter.3.cloned.1.call-update
  104.5 0.0 reduce-scatter.5.cloned.1.call-start
  104.5 35.7 %all-to-all-done.1 = bf16[64,8,3584]{2,1,0:T(8,128)(2,1)} async-done(((bf16[64,8,3584]{2,1,0:T(8,128)(2,1)}), bf16[64,8,3584]{2,1,0:T(8,128)(2,1)}, u32[]{:S(2)}, u32[]{:S(2)}) %all-to-all-start.1) | async-done | bytes 3670048 | tf_op jit(solution)/shard_map/all_to_all | solution.py:129
  140.2 4.1 %multiply_convert_fusion.1 = (bf16[512,256]{1,0:T(8,128)(2,1)S(1)}, bf16[512,256]{1,0:T(8,128)(2,1)S(1)}) fusion(f32[512,256]{1,0:T(8,128)S(1)} %get-tuple-element.21, f32[512,256]{1,0:T(8,128)S(1)} %fusion.11, f32[512,256]{1,0:T(8,128)} %get-tuple-element.19, f32[512,256]{1,0:T(8,128)} %get-tuple-element.18, bf16[1,256,3584]{2,1,0:T(8,128)(2,1)} %param.17, ...), kind=kOutput, calls=%fused_computation.40 | convolution fusion | flops 940703744 | bytes 8126464 | tf_op jit(solution)/shard_map/dot_general | solution.py:71
  144.4 1.1 fusion.21
  145.6 3.1 %fusion.3 = bf16[4,512,896]{2,1,0:T(8,128)(2,1)} fusion(f32[512,4,896]{2,0,1:T(8,128)S(1)} %fusion.21, bf16[4,896,256]{2,1,0:T(8,128)(2,1)S(1)} %bitcast.84, bf16[512,256]{1,0:T(8,128)(2,1)S(1)} %get-tuple-element.33), kind=kOutput, calls=%fused_computation.9 | convolution fusion | flops 943194112 | bytes 13107200 | tf_op jit(solution)/shard_map/mh,kdh->kmd/dot_general | solution.py:80
  148.7 1.3 reduce-scatter.3.cloned.1.call-done
  150.1 2.7 %slice.7 = bf16[4,512,384]{2,1,0:T(8,128)(2,1)} slice(bf16[4,512,896]{2,1,0:T(8,128)(2,1)} %fusion.3), slice={[0:4], [0:512], [512:896]} | slice | bytes 3145728 | tf_op jit(solution)/shard_map/slice | solution.py:144
  152.8 0.0 reduce-scatter.5.cloned.1.call-update
  152.8 1.7 slice.6
  154.5 1.4 copy-done.1
  156.0 1.9 collective-permute-start
  157.9 9.9 %all-to-all-start.2 = ((bf16[64,8,896]{2,1,0:T(8,128)(2,1)}), bf16[64,8,896]{2,1,0:T(8,128)(2,1)S(1)}, u32[]{:S(2)}, u32[]{:S(2)}) async-start(bf16[64,8,896]{2,1,0:T(8,128)(2,1)} %bitcast.89), calls=%async_computation.3 | async-start | bytes 1835008 | tf_op jit(solution)/shard_map/all_to_all | solution.py:139
  167.8 8.1 %collective-permute-done = bf16[512,512]{1,0:T(8,128)(2,1)} collective-permute-done((bf16[512,512]{1,0:T(8,128)(2,1)S(1)}, bf16[512,512]{1,0:T(8,128)(2,1)}, u32[]{:S(2)}, u32[]{:S(2)}) %collective-permute-start) | collective-permute-done | bytes 524320 | tf_op jit(solution)/shard_map/ppermute | solution.py:151
  175.9 1.3 fusion.17
  177.3 2.1 collective-permute-start.1
  179.4 0.8 copy.34
  180.2 0.6 broadcast_in_dim.64
  180.8 1.3 broadcast_maximum_fusion
  182.1 1.4 copy.36
  183.5 1.5 reshape.113
  185.0 9.6 %collective-permute-done.1 = bf16[512,512]{1,0:T(8,128)(2,1)} collective-permute-done((bf16[512,512]{1,0:T(8,128)(2,1)S(1)}, bf16[512,512]{1,0:T(8,128)(2,1)}, u32[]{:S(2)}, u32[]{:S(2)}) %collective-permute-start.1) | collective-permute-done | bytes 524320 | tf_op jit(solution)/shard_map/ppermute | solution.py:151
  194.6 1.3 fusion.16
  196.0 2.6 collective-permute-start.2
  198.6 1.8 dynamic-slice_convert_fusion
  200.3 0.6 broadcast_clamp_fusion
  200.9 9.6 %collective-permute-done.2 = bf16[512,512]{1,0:T(8,128)(2,1)S(1)} collective-permute-done((bf16[512,512]{1,0:T(8,128)(2,1)S(1)}, bf16[512,512]{1,0:T(8,128)(2,1)S(1)}, u32[]{:S(2)}, u32[]{:S(2)}) %collective-permute-start.2) | collective-permute-done | bytes 524320 | tf_op jit(solution)/shard_map/ppermute | solution.py:151
  210.5 1.2 fusion.19
  211.7 0.0 reduce-scatter.5.cloned.1.call-done
  211.7 2.0 pad_maximum_fusion
  213.7 8.1 %all-to-all-start.3 = ((bf16[64,8,896]{2,1,0:T(8,128)(2,1)}), bf16[64,8,896]{2,1,0:T(8,128)(2,1)}, u32[]{:S(2)}, u32[]{:S(2)}) async-start(bf16[64,8,896]{2,1,0:T(8,128)(2,1)} %pad_maximum_fusion), calls=%async_computation.5 | async-start | bytes 1835008 | tf_op jit(solution)/shard_map/all_to_all | solution.py:155
  221.9 0.0 copy-start.10
  221.9 4.6 %fusion.2 = bf16[1,256,3584]{2,1,0:T(8,128)(2,1)} fusion(bf16[512,256]{1,0:T(8,128)(2,1)} %copy-done.6, bf16[64,8,3584]{2,1,0:T(8,128)(2,1)} %all-to-all-done.1), kind=kOutput, calls=%fused_computation.8 | convolution fusion | flops 940441600 | bytes 5767168 | tf_op jit(solution)/shard_map/dot_general | solution.py:88
  226.6 2.4 fusion.1
  229.0 2.4 fusion
  231.4 5.3 %gather_fusion = bf16[1024,896]{1,0:T(8,128)(2,1)} fusion(bf16[512,896]{1,0:T(8,128)(2,1)S(1)} %bitcast.85, s32[1024]{0:T(1024)S(1)} %copy-done.12), kind=kCustom, calls=%fused_computation | custom fusion | bytes 3674112 | tf_op jit(solution)/shard_map/jit(_take)/gather | solution.py:161
  236.6 0.0 copy-start.17
  236.7 2.3 fusion.4
  238.9 0.1 reduce_sum.60
  239.1 0.1 copy.33
  239.2 11.6 %psum.7 = f32[128,8]{0,1:T(8,128)} all-reduce(f32[128,8]{0,1:T(8,128)S(1)} %get-tuple-element.38), channel_id=1, replica_groups=mesh['expert'=64,'tensor'=4] {'tensor'}, use_global_device_ids=true, to_apply=%region_7.8 | all-reduce | flops 1024 | bytes 8192 | tf_op jit(solution)/shard_map/psum | solution.py:174
  250.8 3.5 %multiply_reduce_fusion = bf16[128,896]{1,0:T(8,128)(2,1)} fusion(bf16[1024,896]{1,0:T(8,128)(2,1)} %gather_fusion, f32[128,8]{1,0:T(8,128)S(1)} %copy.33, pred[128,8]{1,0:T(8,128)(4,1)S(1)} %copy.34), kind=kLoop, calls=%fused_computation.15 | loop fusion | flops 3555328 | bytes 2069504 | tf_op jit(solution)/shard_map/reduce_sum | solution.py:166
  254.3 2.2 convolution_convert_fusion.4
  (39 shorter events, 0.2 us)
Async XLA Ops:
  7.2 91.5 %copy-start = (bf16[1,3584,256]{2,1,0:T(8,128)(2,1)S(1)}, bf16[1,3584,256]{2,1,0:T(8,128)(2,1)}, u32[]{:S(2)}) copy-start(bf16[1,3584,256]{2,1,0:T(8,128)(2,1)} %param.16) | copy-start | bytes 5505028
  7.2 17.5 %copy-start.13 = (f32[128,8]{0,1:T(8,128)S(1)}, f32[128,8]{0,1:T(8,128)}, u32[]{:S(2)}) copy-start(f32[128,8]{0,1:T(8,128)} %param.13) | copy-start | bytes 12292
  9.4 20.5 %copy-start.11 = (s32[128,8]{0,1:T(8,128)}, s32[128,8]{0,1:T(8,128)S(1)}, u32[]{:S(2)}) copy-start(s32[128,8]{0,1:T(8,128)S(1)} %get-tuple-element.31) | copy-start | bytes 12292
  12.4 36.3 %all-to-all-start = ((bf16[64,8,896]{2,1,0:T(8,128)(2,1)}), bf16[64,8,896]{2,1,0:T(8,128)(2,1)S(1)}, u32[]{:S(2)}, u32[]{:S(2)}) async-start(bf16[64,8,896]{2,1,0:T(8,128)(2,1)} %fusion.14), calls=%async_computation | async-start | bytes 1835008 | tf_op jit(solution)/shard_map/all_to_all | solution.py:123
  24.6 70.2 %all-gather.2.cloned.1.call-start = ((), (), s32[]{:S(2)}) async-start(), calls=%async_computation.6 | async-start | bytes 4587520 | tf_op jit(solution)/shard_map/all_gather | solution.py:128
  48.7 0.9 copy-start.3
  49.7 90.5 %all-to-all-start.1 = ((bf16[64,8,3584]{2,1,0:T(8,128)(2,1)}), bf16[64,8,3584]{2,1,0:T(8,128)(2,1)}, u32[]{:S(2)}, u32[]{:S(2)}) async-start(bf16[64,8,3584]{2,1,0:T(8,128)(2,1)} %bitcast.86), calls=%async_computation.2 | async-start | bytes 7340032 | tf_op jit(solution)/shard_map/all_to_all | solution.py:129
  57.7 92.4 %reduce-scatter.3.cloned.1.call-start = ((), (), s32[]{:S(2)}) async-start(), calls=%async_computation.7 | async-start | bytes 4587520 | tf_op jit(solution)/shard_map/reduce_scatter | solution.py:136
  94.8 3.9 %copy-start.18 = (bf16[512,3584]{1,0:T(8,128)(2,1)S(1)}, bf16[512,3584]{1,0:T(8,128)(2,1)}, u32[]{:S(2)}) copy-start(bf16[512,3584]{1,0:T(8,128)(2,1)} %all-gather.2.cloned.1.call-done) | copy-start | bytes 11010052
  98.7 2.7 %copy-start.2 = (bf16[256,4,896]{2,1,0:T(4,128)(2,1)S(1)}, bf16[256,4,896]{2,1,0:T(4,128)(2,1)}, u32[]{:S(2)}) copy-start(bf16[256,4,896]{2,1,0:T(4,128)(2,1)} %reshape_squeeze.9) | copy-start | bytes 5505028
  100.7 0.7 copy-start.6
  104.5 107.2 %reduce-scatter.5.cloned.1.call-start = ((), (), s32[]{:S(2)}) async-start(), calls=%async_computation.8 | async-start | bytes 1966080 | tf_op jit(solution)/shard_map/reduce_scatter | solution.py:144
  140.2 4.2 %copy-start.4 = (bf16[1,3584,256]{2,1,0:T(8,128)(2,1)S(1)}, bf16[1,3584,256]{2,1,0:T(8,128)(2,1)}, u32[]{:S(2)}) copy-start(bf16[1,3584,256]{2,1,0:T(8,128)(2,1)} %param.15) | copy-start | bytes 5505028
  144.4 1.2 copy-start.7
  144.4 1.2 copy-start.9
  154.5 1.4 copy-start.1
  156.0 20.0 %collective-permute-start = (bf16[512,512]{1,0:T(8,128)(2,1)S(1)}, bf16[512,512]{1,0:T(8,128)(2,1)}, u32[]{:S(2)}, u32[]{:S(2)}) collective-permute-start(bf16[512,512]{1,0:T(8,128)(2,1)S(1)} %dynamic-slice_bitcast_fusion), channel_id=1, source_target_pairs={{0,3},{1,0},{2,1},{3,2},{4,7},{5,4},{6,5},{7,6},{8,11},{9,8},{10,9... | collective-permute-start | bytes 1572872 | tf_op jit(solution)/shard_map/ppermute | solution.py:151
  157.9 55.8 %all-to-all-start.2 = ((bf16[64,8,896]{2,1,0:T(8,128)(2,1)}), bf16[64,8,896]{2,1,0:T(8,128)(2,1)S(1)}, u32[]{:S(2)}, u32[]{:S(2)}) async-start(bf16[64,8,896]{2,1,0:T(8,128)(2,1)} %bitcast.89), calls=%async_computation.3 | async-start | bytes 1835008 | tf_op jit(solution)/shard_map/all_to_all | solution.py:139
  177.3 17.3 %collective-permute-start.1 = (bf16[512,512]{1,0:T(8,128)(2,1)S(1)}, bf16[512,512]{1,0:T(8,128)(2,1)}, u32[]{:S(2)}, u32[]{:S(2)}) collective-permute-start(bf16[512,512]{1,0:T(8,128)(2,1)S(1)} %fusion.17), channel_id=1, source_target_pairs={{0,3},{1,0},{2,1},{3,2},{4,7},{5,4},{6,5},{7,6},{8,11},{9,8},{10,9... | collective-permute-start | bytes 1572872 | tf_op jit(solution)/shard_map/ppermute | solution.py:151
  185.0 15.3 %copy-start.15 = (s32[1024,1]{0,1:T(1,128)S(1)}, s32[1024,1]{0,1:T(1,128)}, u32[]{:S(2)}) copy-start(s32[1024,1]{0,1:T(1,128)} %reshape.113) | copy-start | bytes 12292
  196.0 14.5 %collective-permute-start.2 = (bf16[512,512]{1,0:T(8,128)(2,1)S(1)}, bf16[512,512]{1,0:T(8,128)(2,1)S(1)}, u32[]{:S(2)}, u32[]{:S(2)}) collective-permute-start(bf16[512,512]{1,0:T(8,128)(2,1)S(1)} %fusion.16), channel_id=1, source_target_pairs={{0,3},{1,0},{2,1},{3,2},{4,7},{5,4},{6,5},{7,6},{8,11},{9,8},{10,9... | collective-permute-start | bytes 1572872 | tf_op jit(solution)/shard_map/ppermute | solution.py:151
  213.7 40.6 %all-to-all-start.3 = ((bf16[64,8,896]{2,1,0:T(8,128)(2,1)}), bf16[64,8,896]{2,1,0:T(8,128)(2,1)}, u32[]{:S(2)}, u32[]{:S(2)}) async-start(bf16[64,8,896]{2,1,0:T(8,128)(2,1)} %pad_maximum_fusion), calls=%async_computation.5 | async-start | bytes 1835008 | tf_op jit(solution)/shard_map/all_to_all | solution.py:155
  221.9 4.7 %copy-start.10 = (bf16[512,256]{1,0:T(8,128)(2,1)S(1)}, bf16[512,256]{1,0:T(8,128)(2,1)}, u32[]{:S(2)}) copy-start(bf16[512,256]{1,0:T(8,128)(2,1)} %copy-done.9) | copy-start | bytes 786436
  221.9 4.7 %copy-start.19 = (bf16[512,3584]{1,0:T(8,128)(2,1)S(1)}, bf16[512,3584]{1,0:T(8,128)(2,1)}, u32[]{:S(2)}) copy-start(bf16[512,3584]{1,0:T(8,128)(2,1)} %all-gather.2.cloned.1.call-done) | copy-start | bytes 11010052
  226.5 2.4 copy-start.8
  229.0 2.4 copy-start.12
  231.4 5.3 %copy-start.5 = (f32[128,896]{1,0:T(8,128)S(1)}, f32[128,896]{1,0:T(8,128)}, u32[]{:S(2)}) copy-start(f32[128,896]{1,0:T(8,128)} %dynamic-slice_convert_fusion) | copy-start | bytes 1376260
  231.4 5.3 %copy-start.16 = (pred[1024]{0:T(1024)(128)(4,1)S(1)}, pred[1024]{0:T(1024)(128)(4,1)}, u32[]{:S(2)}) copy-start(pred[1024]{0:T(1024)(128)(4,1)} %broadcast_in_dim.64) | copy-start | bytes 3076
  236.6 2.4 copy-start.14
  236.6 2.4 copy-start.17
Sparse Core Ops, SparseCore 0:
  49.8 44.9 all-gather.1
  104.6 45.4 reduce-scatter.2
  153.2 33.5 reduce-scatter.4
